TPU v7x, 32 devices: a whole 2x2x4 slice. The times are simulated.
32 devices in a mesh: blk: 8 (over z, y), dp: 4 (over x, core).
Axes of the slice: x: 2, y: 2, z: 4, core: 2. Of those that a mesh axis runs over, the one named last changes fastest.
Arguments:
- feature_map: bfloat16 [20480, 320], P(('blk', 'dp')), may hold values from -8 to 8, as said below
- head_weight: bfloat16 [320, 1280], replicated, may hold values from -0.3125 to 0.3125
- head_shift: float32 [1280], replicated, may hold values from -0.5 to 0.5
- proj_weight: bfloat16 [1280, 256], replicated, may hold values from -0.15625 to 0.15625
Outputs:
- loss: float32 [], replicated
- grad_head: float32 [320, 1280], replicated
- grad_shift: float32 [1280], replicated
- grad_proj: float32 [1280, 256], replicated
Inputs may be any that keep to these rules, and one draw needn't show every extreme that they name: `feature_map`: features of order one.
All inputs are finite; a program needn't handle non-finite values.
Results may differ from a plain program's by a relative error of at most 0.00067.
Values may be sent and summed in bfloat16 or wider, within the bound.
No kernel may reach another device: no remote copies, remote signals or barrier semaphores. Data moves between devices by JAX's collectives and lax.ppermute only.
A program may use at most 64 MiB of HBM per device.

v0:
```python
import jax
import jax.numpy as jnp
from jax import lax
from jax.sharding import PartitionSpec as P

POS = 16


def pair_terms(rows_z, row_ids, piece, col_ids):
    sim = lax.dot_general(
        rows_z, piece, (((1,), (1,)), ((), ())), preferred_element_type=jnp.float32
    )
    kern = jnp.exp(4.0 * (sim - 1.0))
    kern = jnp.where(row_ids[:, None] == col_ids[None, :], jnp.float32(0.0), kern)
    srow = jnp.sum(kern, axis=1)
    numer = jnp.dot(kern.astype(jnp.bfloat16), piece, preferred_element_type=jnp.float32)
    return (srow, numer)


def body(feature_map, head_weight, head_shift, proj_weight):
    images = feature_map.shape[0] // POS
    channels = head_weight.shape[1]
    pre = jnp.dot(feature_map, head_weight, preferred_element_type=jnp.float32) + head_shift
    act = jax.nn.silu(pre)
    pooled = jnp.mean(act.reshape(images, POS, channels), axis=1).astype(jnp.bfloat16)
    proj = jnp.dot(pooled, proj_weight, preferred_element_type=jnp.float32)
    rnorm = jnp.sqrt(jnp.sum(proj * proj, axis=1, keepdims=True) + 1e-06)
    unit = proj / rnorm
    zed = unit.astype(jnp.bfloat16)
    batch = images * lax.axis_size("blk") * lax.axis_size("dp")
    my_ids = lax.axis_index(("blk", "dp")) * images + jnp.arange(images, dtype=jnp.int32)
    piece = lax.all_gather(zed, ("blk", "dp"), axis=0, tiled=True)
    col_ids = jnp.arange(piece.shape[0], dtype=jnp.int32)
    srow, numer = pair_terms(zed, my_ids, piece, col_ids)
    total = lax.psum(jnp.sum(srow), ("blk", "dp"))
    loss = jnp.log(total / (batch * (batch - 1.0)))
    grad_unit = batch * 8.0 / total * numer
    grad_rows = (
        (grad_unit - unit * jnp.sum(unit * grad_unit, axis=1, keepdims=True)) / rnorm
    ).astype(jnp.bfloat16)
    grad_proj = lax.dot_general(
        pooled, grad_rows, (((0,), (0,)), ((), ())), preferred_element_type=jnp.float32
    )
    grad_pooled = lax.dot_general(
        grad_rows, proj_weight, (((1,), (1,)), ((), ())), preferred_element_type=jnp.float32
    )
    grad_act = jnp.broadcast_to((grad_pooled / POS)[:, None, :], (images, POS, channels)).reshape(
        images * POS, channels
    )
    sig = jax.nn.sigmoid(pre)
    grad_pre = (grad_act * sig * (1.0 + pre * (1.0 - sig))).astype(jnp.bfloat16)
    grad_shift = jnp.sum(grad_pre.astype(jnp.float32), axis=0)
    grad_head = lax.dot_general(
        feature_map, grad_pre, (((0,), (0,)), ((), ())), preferred_element_type=jnp.float32
    )
    grad_head, grad_shift, grad_proj = lax.psum((grad_head, grad_shift, grad_proj), ("blk", "dp"))
    return (loss, grad_head, grad_shift, grad_proj)


def solution(mesh):
    return jax.shard_map(
        body,
        mesh=mesh,
        in_specs=(P(("blk", "dp"), None), P(), P(), P()),
        out_specs=(P(), P(), P(), P()),
        check_vma=False,
    )
```

profile of v0, /device:TPU:0, one launch (start us, length us, event | category | flops | bytes accessed | tf_op | source)
XLA Modules:
  0.0 256.1 jit_solution(15273268031777491178)
XLA Ops:
  7.2 0.0 copy-start
  7.2 0.0 all-reduce.3.cloned.1.call-start
  7.2 1.1 copy-done
  8.3 5.0 %fusion.2 = (f32[640,1280]{1,0:T(8,128)}, f32[640,1280]{1,0:T(8,128)}) fusion(f32[1280]{0:T(1024)} %param.6, bf16[640,320]{0,1:T(8,128)(2,1)} %param.4, bf16[320,1280]{1,0:T(8,128)(2,1)S(1)} %copy-done), kind=kOutput, calls=%fused_computation.6 | convolution fusion | flops 528384000 | bytes 7787520 | tf_op jit(solution)/shard_map/dot_general | solution.py:23
  13.3 0.0 copy-start.2
  13.3 2.5 reduce_sum.49
  15.8 0.0 copy-done.2
  15.8 0.3 multiply_reduce_fusion.1
  16.2 0.1 fusion.11
  16.3 45.0 %all_gather.3 = bf16[1280,256]{1,0:T(8,128)(2,1)S(1)} all-gather(bf16[40,256]{1,0:T(8,128)(2,1)S(1)} %fusion.11), channel_id=1, replica_groups=mesh['blk'=8,'dp'=4] {'blk','dp'}, dimensions={0}, use_global_device_ids=true | all-gather | bytes 675840 | tf_op jit(solution)/shard_map/all_gather | solution.py:32
  61.3 1.0 fusion.13
  62.3 37.0 %psum.28 = f32[]{:T(128)} all-reduce(f32[]{:T(128)} %get-tuple-element.12), channel_id=1, replica_groups=mesh['blk'=8,'dp'=4] {'blk','dp'}, use_global_device_ids=true, to_apply=%region_3.4 | all-reduce | flops 1 | bytes 8 | tf_op jit(solution)/shard_map/psum | solution.py:35
  100.0 0.0 copy-start.1
  100.0 0.3 multiply_reduce_fusion
  100.4 1.5 fusion.7
  101.8 0.0 copy-start.4
  101.8 0.4 convolution_multiply_fusion
  102.2 0.2 copy-done.1
  102.4 1.4 convert_reduce_fusion
  103.7 0.0 copy-done.4
  103.8 2.0 convolution_bitcast_fusion
  105.7 0.0 all-reduce.3.cloned.1.call-update
  106.4 41.6 %psum.30 = f32[1280]{0:T(1024)} all-reduce(f32[1280]{0:T(1024)S(1)} %get-tuple-element.6), channel_id=1, replica_groups=mesh['blk'=8,'dp'=4] {'blk','dp'}, use_global_device_ids=true, to_apply=%region_7.8 | all-reduce | flops 1280 | bytes 10240 | tf_op jit(solution)/shard_map/psum | solution.py:56
  148.0 96.3 %all-reduce.3.cloned.1.call-done = (f32[320,1280]{1,0:T(8,128)}, f32[1280,256]{1,0:T(8,128)}) async-done(((f32[320,1280]{1,0:T(8,128)}, f32[1280,256]{1,0:T(8,128)}), (f32[320,1280]{1,0:T(8,128)}, f32[1280,256]{1,0:T(8,128)})) %all-reduce.3.cloned.1.call-update) | async-done | bytes 2949136 | tf_op jit(solution)/shard_map/psum | solution.py:56
  244.3 0.0 copy-start.3
  244.3 2.8 %copy.10 = f32[320,1280]{1,0:T(8,128)} copy(f32[320,1280]{1,0:T(8,128)} %get-tuple-element.19) | data formatting | bytes 3276800
  247.1 0.0 copy-done.3
  247.1 1.1 copy.11
  (2 shorter events, 0.0 us)
Async XLA Ops:
  7.2 1.2 copy-start
  7.2 237.1 %all-reduce.3.cloned.1.call-start = ((), (), s32[]{:S(2)}) async-start(), calls=%async_computation | async-start | bytes 5898240 | tf_op jit(solution)/shard_map/psum | solution.py:56
  13.3 2.5 copy-start.2
  100.0 2.4 copy-start.1
  101.8 1.9 copy-start.4
  244.3 2.8 %copy-start.3 = (f32[1280,256]{1,0:T(8,128)S(1)}, f32[1280,256]{1,0:T(8,128)}, u32[]{:S(2)}) copy-start(f32[1280,256]{1,0:T(8,128)} %get-tuple-element.21) | copy-start | bytes 3932164
Sparse Core Ops, SparseCore 0:
  105.9 138.3 all-reduce.2
where the time goes:
time: 257 us; the launch traced here: 256 us
  blocking collectives  124 us (48%)
  waiting for transfers between devices  96.3 us (37%)
  between operations  16.6 us (6%)
  matrix products  10.4 us (4%)
  local copies, waits for them, and re-layouts  5.18 us (2%)
  other arithmetic  3.97 us (2%)
    psum x1, waiting for transfers between devices, body(): lax.psum((grad_head, grad_shift, grad_proj), ('blk', 'dp'))  96.3 us
    all_gather x1, blocking collectives, body(): piece = lax.all_gather(zed, ('blk', 'dp'), axis=0, tiled=True)  45 us
    psum x1, blocking collectives, body(): lax.psum((grad_head, grad_shift, grad_proj), ('blk', 'dp'))  41.6 us
    psum x1, blocking collectives, body(): total = lax.psum(jnp.sum(srow), ('blk', 'dp'))  37 us
    unnamed x12, local copies, waits for them, and re-layouts  5.18 us
  transfers between devices with their start and end apart: 1, of which 1 were waited for; matrix products, arithmetic and copies ran while one was open for 0% of the time, Pallas kernels for 0%

commit v1 on v0

v1 whole, which is shorter than its diff:
```python
import jax
import jax.numpy as jnp
from jax import lax
from jax.sharding import PartitionSpec as P

POS = 16
FULL_KERNEL_MAX_BATCH = 2048


def exchange_steps(mesh):
    steps = []
    for ax in ("dp", "blk"):
        size = mesh.shape[ax]
        if size & (size - 1):
            return []
        mask = 1
        while mask < size:
            steps.append((ax, mask))
            mask *= 2
    return steps


def swap(x, mesh, ax, mask):
    return lax.ppermute(x, ax, [(i, i ^ mask) for i in range(mesh.shape[ax])])


def my_bit(ax, mask):
    return (lax.axis_index(ax) & mask) != 0


def gather_blocks(zed, mesh, steps):
    order = list(reversed(steps))
    buf = zed[None]
    for ax, mask in order:
        got = swap(buf, mesh, ax, mask)
        buf = jnp.where(my_bit(ax, mask), jnp.stack([got, buf]), jnp.stack([buf, got]))
    block = sum(my_bit(ax, mask).astype(jnp.int32) << k for k, (ax, mask) in enumerate(order))
    return buf.reshape(-1, zed.shape[-1]), block


def halving_plan(shape, steps):
    plan, dims = [], list(shape)
    for _ in steps:
        if len(dims) == 2 and dims[0] % 16 == 0:
            plan.append(0)
            dims[0] //= 2
        elif len(dims) == 2 and dims[1] % 256 == 0:
            plan.append(1)
            dims[1] //= 2
        else:
            plan.append(None)
    return plan


def all_reduce(arrays, mesh, steps):
    plans = [halving_plan(a.shape, steps) for a in arrays]
    cur = list(arrays)
    for k, (ax, mask) in enumerate(steps):
        bit = my_bit(ax, mask).astype(jnp.int32)
        keeps, sends = [], []
        for a, plan in zip(cur, plans):
            d = plan[k]
            if d is None:
                keeps.append(a)
                sends.append(a)
            else:
                h = a.shape[d] // 2
                keeps.append(lax.dynamic_slice_in_dim(a, bit * h, h, axis=d))
                sends.append(lax.dynamic_slice_in_dim(a, (1 - bit) * h, h, axis=d))
        got = swap(sends, mesh, ax, mask)
        cur = [kk + g for kk, g in zip(keeps, got)]
    for k in reversed(range(len(steps))):
        ax, mask = steps[k]
        idx = [j for j, plan in enumerate(plans) if plans[j][k] is not None]
        if not idx:
            continue
        got = swap([cur[j] for j in idx], mesh, ax, mask)
        bit = my_bit(ax, mask)
        for j, g in zip(idx, got):
            d = plans[j][k]
            c = cur[j]
            cur[j] = jnp.where(bit, jnp.concatenate([g, c], axis=d), jnp.concatenate([c, g], axis=d))
    return cur


def pair_terms(rows_z, row_ids, piece, col_ids):
    sim = lax.dot_general(
        rows_z, piece, (((1,), (1,)), ((), ())), preferred_element_type=jnp.float32
    )
    kern = jnp.exp(4.0 * (sim - 1.0))
    kern = jnp.where(row_ids[:, None] == col_ids[None, :], jnp.float32(0.0), kern)
    return kern


def make_body(mesh):
    steps = exchange_steps(mesh)

    def body(feature_map, head_weight, head_shift, proj_weight):
        images = feature_map.shape[0] // POS
        channels = head_weight.shape[1]
        pre = jnp.dot(feature_map, head_weight, preferred_element_type=jnp.float32) + head_shift
        act = jax.nn.silu(pre)
        pooled = jnp.mean(act.reshape(images, POS, channels), axis=1).astype(jnp.bfloat16)
        proj = jnp.dot(pooled, proj_weight, preferred_element_type=jnp.float32)
        rnorm = jnp.sqrt(jnp.sum(proj * proj, axis=1, keepdims=True) + 1e-06)
        unit = proj / rnorm
        zed = unit.astype(jnp.bfloat16)
        batch = images * mesh.shape["blk"] * mesh.shape["dp"]
        if steps:
            piece, block = gather_blocks(zed, mesh, steps)
        else:
            piece = lax.all_gather(zed, ("blk", "dp"), axis=0, tiled=True)
            block = lax.axis_index(("blk", "dp"))
        my_ids = block * images + jnp.arange(images, dtype=jnp.int32)
        col_ids = jnp.arange(piece.shape[0], dtype=jnp.int32)
        kern = pair_terms(zed, my_ids, piece, col_ids)
        numer = jnp.dot(kern.astype(jnp.bfloat16), piece, preferred_element_type=jnp.float32)
        if batch <= FULL_KERNEL_MAX_BATCH:
            total = jnp.sum(pair_terms(piece, col_ids, piece, col_ids))
        else:
            total = lax.psum(jnp.sum(kern), ("blk", "dp"))
        loss = jnp.log(total / (batch * (batch - 1.0)))
        grad_unit = batch * 8.0 / total * numer
        grad_rows = (
            (grad_unit - unit * jnp.sum(unit * grad_unit, axis=1, keepdims=True)) / rnorm
        ).astype(jnp.bfloat16)
        grad_proj = lax.dot_general(
            pooled, grad_rows, (((0,), (0,)), ((), ())), preferred_element_type=jnp.float32
        )
        grad_pooled = lax.dot_general(
            grad_rows, proj_weight, (((1,), (1,)), ((), ())), preferred_element_type=jnp.float32
        )
        grad_act = jnp.broadcast_to(
            (grad_pooled / POS)[:, None, :], (images, POS, channels)
        ).reshape(images * POS, channels)
        sig = jax.nn.sigmoid(pre)
        grad_pre = (grad_act * sig * (1.0 + pre * (1.0 - sig))).astype(jnp.bfloat16)
        grad_shift = jnp.sum(grad_pre.astype(jnp.float32), axis=0)
        grad_head = lax.dot_general(
            feature_map, grad_pre, (((0,), (0,)), ((), ())), preferred_element_type=jnp.float32
        )
        if steps:
            grad_head, grad_proj, grad_shift = all_reduce([grad_head, grad_proj, grad_shift], mesh, steps)
        else:
            grad_head, grad_shift, grad_proj = lax.psum((grad_head, grad_shift, grad_proj), ("blk", "dp"))
        return (loss, grad_head, grad_shift, grad_proj)

    return body


def solution(mesh):
    return jax.shard_map(
        make_body(mesh),
        mesh=mesh,
        in_specs=(P(("blk", "dp"), None), P(), P(), P()),
        out_specs=(P(), P(), P(), P()),
        check_vma=False,
    )
```

time: 257 us -> 129 us (0.50)
  blocking collectives: 124 us -> 0 us
  starting transfers between devices: 0.04 us -> 42.6 us
  waiting for transfers between devices: 96.3 us -> 55.9 us
  between operations: 16.6 us -> 3.48 us
  other arithmetic: 3.97 us -> 12.8 us
    psum x1 -> x0, waiting for transfers between devices: 96.3 us -> none  [body(): lax.psum((grad_head, grad_shift, grad_proj), ('blk', 'dp'))]
    psum x2 -> x0, blocking collectives: 78.6 us -> none  [the longest x1 41.6 us: body(): lax.psum((grad_head, grad_shift, grad_proj), ('blk', 'dp'))]
    ppermute x0 -> x29, waiting for transfers between devices: none -> 55.9 us  [swap(): return lax.ppermute(x, ax, [(i, i ^ mask) for i in range(mesh.shape[ax])])]
    all_gather x1 -> x0, blocking collectives: 45 us -> none  [body(): piece = lax.all_gather(zed, ('blk', 'dp'), axis=0, tiled=True)]
    ppermute x0 -> x29, starting transfers between devices: none -> 42.6 us  [swap(): return lax.ppermute(x, ax, [(i, i ^ mask) for i in range(mesh.shape[ax])])]
    select_n x0 -> x15, other arithmetic: none -> 5.14 us  [the longest x9 4.04 us: all_reduce(): jnp.where(bit, jnp.concatenate([g, c], axis=d), jnp.concatenate([c, g], a...]
    add x1 -> x16, other arithmetic: 0.01 us -> 3.45 us  [the longest x15 3.45 us: all_reduce(): cur = [kk + g for kk, g in zip(keeps, got)]]
  transfers between devices with their start and end apart: 1 -> 29, of which waited for: 1 -> 21; matrix products, arithmetic and copies ran while one was open for 0% -> 7% of each run, Pallas kernels for 0% -> 0%
where the time goes in v1:
time: 129 us
  waiting for transfers between devices  55.9 us (43%)
  starting transfers between devices  42.6 us (33%)
  other arithmetic  12.8 us (10%)
  matrix products  10.1 us (8%)
  local copies, waits for them, and re-layouts  3.79 us (3%)
  between operations  3.48 us (3%)
    ppermute x29, waiting for transfers between devices, swap(): return lax.ppermute(x, ax, [(i, i ^ mask) for i in range(mesh.shape[ax])])  55.9 us
    ppermute x29, starting transfers between devices, swap(): return lax.ppermute(x, ax, [(i, i ^ mask) for i in range(mesh.shape[ax])])  42.6 us
    dot_general x1, matrix products, body(): jnp.dot(feature_map, head_weight, preferred_element_type=jnp.float32)  5.08 us
    select_n x9, other arithmetic, all_reduce(): jnp.where(bit, jnp.concatenate([g, c], axis=d), jnp.concatenate([c, g], a...  4.04 us
    add x15, other arithmetic, all_reduce(): cur = [kk + g for kk, g in zip(keeps, got)]  3.45 us
    unnamed x12, local copies, waits for them, and re-layouts  2.69 us
  transfers between devices with their start and end apart: 29, of which 21 were waited for; matrix products, arithmetic and copies ran while one was open for 7% of the time, Pallas kernels for 0%

profile of v1, /device:TPU:0, one launch (start us, length us, event | category | flops | bytes accessed | tf_op | source)
XLA Modules:
  0.0 128.7 jit_solution(15334717436704450784)
XLA Ops:
  1.8 5.1 %fusion.5 = (f32[640,1280]{1,0:T(8,128)}, f32[640,1280]{1,0:T(8,128)}) fusion(f32[1280]{0:T(1024)} %param.6, bf16[640,320]{0,1:T(8,128)(2,1)} %param.4, bf16[320,1280]{1,0:T(8,128)(2,1)S(1)} %copy-done), kind=kOutput, calls=%fused_computation.11 | convolution fusion | flops 528384000 | bytes 7787520 | tf_op jit(solution)/shard_map/dot_general | solution.py:101
  6.9 2.5 %reduce_sum.45 = f32[40,1280]{1,0:T(8,128)S(1)} reduce(f32[40,16,1280]{2,1,0:T(8,128)} %bitcast.69, f32[]{:T(128)} %constant.52.clone.1), dimensions={1}, to_apply=%region_0.1 | reduce | flops 768000 | bytes 3481604 | tf_op jit(solution)/shard_map/reduce_sum | solution.py:103
  9.8 4.1 %collective-permute-start = (bf16[1,40,256]{2,1,0:T(8,128)(2,1)S(1)}, bf16[1,40,256]{2,1,0:T(8,128)(2,1)S(1)}, u32[]{:S(2)}, u32[]{:S(2)}) collective-permute-start(bf16[1,40,256]{2,1,0:T(8,128)(2,1)S(1)} %fusion.51), channel_id=1, source_target_pairs={{0,16},{4,20},{8,24},{12,28},{16,0},{20,4},{24,8},{28,12},{1,17},{... | collective-permute-start | bytes 61448 | tf_op jit(solution)/shard_map/ppermute | solution.py:24
  15.8 2.0 %collective-permute-start.1 = (bf16[2,1,40,256]{3,2,0,1:T(8,128)(2,1)S(1)}, bf16[2,1,40,256]{3,2,0,1:T(8,128)(2,1)S(1)}, u32[]{:S(2)}, u32[]{:S(2)}) collective-permute-start(bf16[2,1,40,256]{3,2,0,1:T(8,128)(2,1)S(1)} %maximum_select_fusion.16), channel_id=1, source_target_pairs={{0,8},{4,12},{8,0},{12,4},{16,24},{20,28},{24,16},{28,20},{1,9},{5... | collective-permute-start | bytes 122888 | tf_op jit(solution)/shard_map/ppermute | solution.py:24
  17.7 2.1 %collective-permute-done.1 = bf16[2,1,40,256]{3,2,0,1:T(8,128)(2,1)S(1)} collective-permute-done((bf16[2,1,40,256]{3,2,0,1:T(8,128)(2,1)S(1)}, bf16[2,1,40,256]{3,2,0,1:T(8,128)(2,1)S(1)}, u32[]{:S(2)}, u32[]{:S(2)}) %collective-permute-start.1) | collective-permute-done | bytes 40992 | tf_op jit(solution)/shard_map/ppermute | solution.py:24
  19.8 2.0 %collective-permute-start.2 = (bf16[2,2,1,40,256]{4,3,1,0,2:T(8,128)(2,1)S(1)}, bf16[2,2,1,40,256]{4,3,1,0,2:T(8,128)(2,1)S(1)}, u32[]{:S(2)}, u32[]{:S(2)}) collective-permute-start(bf16[2,2,1,40,256]{4,3,1,0,2:T(8,128)(2,1)S(1)} %maximum_select_fusion.13), channel_id=1, source_target_pairs={{0,4},{4,0},{8,12},{12,8},{16,20},{20,16},{24,28},{28,24},{1,5},{5... | collective-permute-start | bytes 245768 | tf_op jit(solution)/shard_map/ppermute | solution.py:24
  21.9 2.5 %collective-permute-done.2 = bf16[2,2,1,40,256]{4,3,1,0,2:T(8,128)(2,1)S(1)} collective-permute-done((bf16[2,2,1,40,256]{4,3,1,0,2:T(8,128)(2,1)S(1)}, bf16[2,2,1,40,256]{4,3,1,0,2:T(8,128)(2,1)S(1)}, u32[]{:S(2)}, u32[]{:S(2)}) %collective-permute-start.2) | collective-permute-done | bytes 81952 | tf_op jit(solution)/shard_map/ppermute | solution.py:24
  24.4 2.0 %collective-permute-start.3 = (bf16[2,2,2,1,40,256]{5,4,2,1,0,3:T(8,128)(2,1)S(1)}, bf16[2,2,2,1,40,256]{5,4,2,1,0,3:T(8,128)(2,1)S(1)}, u32[]{:S(2)}, u32[]{:S(2)}) collective-permute-start(bf16[2,2,2,1,40,256]{5,4,2,1,0,3:T(8,128)(2,1)S(1)} %maximum_select_fusion.10), channel_id=1, source_target_pairs={{0,2},{1,3},{2,0},{3,1},{4,6},{5,7},{6,4},{7,5},{8,10},{9,11},{10,... | collective-permute-start | bytes 491528 | tf_op jit(solution)/shard_map/ppermute | solution.py:24
  26.4 3.4 %collective-permute-done.3 = bf16[2,2,2,1,40,256]{5,4,2,1,0,3:T(8,128)(2,1)S(1)} collective-permute-done((bf16[2,2,2,1,40,256]{5,4,2,1,0,3:T(8,128)(2,1)S(1)}, bf16[2,2,2,1,40,256]{5,4,2,1,0,3:T(8,128)(2,1)S(1)}, u32[]{:S(2)}, u32[]{:S(2)}) %collective-permute-start.3) | collective-permute-done | bytes 163872 | tf_op jit(solution)/shard_map/ppermute | solution.py:24
  32.5 2.5 %fusion.10 = f32[]{:T(128)} fusion(bf16[1280,256]{1,0:T(8,128)(2,1)S(1)} %bitcast.74), kind=kOutput, calls=%fused_computation.19 | convolution fusion | flops 847052800 | bytes 655364 | tf_op jit(solution)/shard_map/dot_general | solution.py:87
  43.3 2.0 %collective-permute-start.20 = (f32[320,256]{1,0:T(8,128)S(1)}, f32[320,256]{1,0:T(8,128)S(1)}, u32[]{:S(2)}, u32[]{:S(2)}) collective-permute-start(f32[320,256]{1,0:T(8,128)S(1)} %constant_dynamic-slice_fusion.3), channel_id=1, source_target_pairs={{0,2},{1,3},{2,0},{3,1},{4,6},{5,7},{6,4},{7,5},{8,10},{9,11},{10,... | collective-permute-start | bytes 983048 | tf_op jit(solution)/shard_map/ppermute | solution.py:24
  46.8 6.8 %collective-permute-done.20 = f32[320,256]{1,0:T(8,128)S(1)} collective-permute-done((f32[320,256]{1,0:T(8,128)S(1)}, f32[320,256]{1,0:T(8,128)S(1)}, u32[]{:S(2)}, u32[]{:S(2)}) %collective-permute-start.20) | collective-permute-done | bytes 327712 | tf_op jit(solution)/shard_map/ppermute | solution.py:24
  53.6 1.8 %collective-permute-start.21 = (f32[160,256]{1,0:T(8,128)S(1)}, f32[160,256]{1,0:T(8,128)S(1)}, u32[]{:S(2)}, u32[]{:S(2)}) collective-permute-start(f32[160,256]{1,0:T(8,128)S(1)} %constant_dynamic-slice_fusion.2), channel_id=1, source_target_pairs={{0,4},{4,0},{8,12},{12,8},{16,20},{20,16},{24,28},{28,24},{1,5},{5... | collective-permute-start | bytes 491528 | tf_op jit(solution)/shard_map/ppermute | solution.py:24
  57.1 2.4 %collective-permute-done.21 = f32[160,256]{1,0:T(8,128)S(1)} collective-permute-done((f32[160,256]{1,0:T(8,128)S(1)}, f32[160,256]{1,0:T(8,128)S(1)}, u32[]{:S(2)}, u32[]{:S(2)}) %collective-permute-start.21) | collective-permute-done | bytes 163872 | tf_op jit(solution)/shard_map/ppermute | solution.py:24
  61.2 5.0 %collective-permute-done.6 = f32[80,1280]{1,0:T(8,128)S(1)} collective-permute-done((f32[80,1280]{1,0:T(8,128)S(1)}, f32[80,1280]{1,0:T(8,128)S(1)}, u32[]{:S(2)}, u32[]{:S(2)}) %collective-permute-start.6) | collective-permute-done | bytes 409632 | tf_op jit(solution)/shard_map/ppermute | solution.py:24
  66.8 2.6 %collective-permute-start.23 = (f32[40,256]{1,0:T(8,128)S(1)}, f32[40,256]{1,0:T(8,128)S(1)}, u32[]{:S(2)}, u32[]{:S(2)}) collective-permute-start(f32[40,256]{1,0:T(8,128)S(1)} %constant_dynamic-slice_fusion), channel_id=1, source_target_pairs={{0,16},{4,20},{8,24},{12,28},{16,0},{20,4},{24,8},{28,12},{1,17},{... | collective-permute-start | bytes 122888 | tf_op jit(solution)/shard_map/ppermute | solution.py:24
  69.4 2.6 %collective-permute-done.7 = f32[40,1280]{1,0:T(8,128)S(1)} collective-permute-done((f32[40,1280]{1,0:T(8,128)S(1)}, f32[40,1280]{1,0:T(8,128)S(1)}, u32[]{:S(2)}, u32[]{:S(2)}) %collective-permute-start.7) | collective-permute-done | bytes 204832 | tf_op jit(solution)/shard_map/ppermute | solution.py:24
  73.7 2.8 %collective-permute-start.24 = (f32[40,256]{1,0:T(8,128)S(1)}, f32[40,256]{1,0:T(8,128)S(1)}, u32[]{:S(2)}, u32[]{:S(2)}) collective-permute-start(f32[40,256]{1,0:T(8,128)S(1)} %dynamic-slice_add_fusion.7), channel_id=1, source_target_pairs={{0,16},{4,20},{8,24},{12,28},{16,0},{20,4},{24,8},{28,12},{1,17},{... | collective-permute-start | bytes 122888 | tf_op jit(solution)/shard_map/ppermute | solution.py:24
  77.8 2.7 %collective-permute-start.9 = (f32[40,640]{1,0:T(8,128)S(1)}, f32[40,640]{1,0:T(8,128)S(1)}, u32[]{:S(2)}, u32[]{:S(2)}) collective-permute-start(f32[40,640]{1,0:T(8,128)S(1)} %dynamic-slice_add_fusion.5), channel_id=1, source_target_pairs={{0,16},{4,20},{8,24},{12,28},{16,0},{20,4},{24,8},{28,12},{1,17},{... | collective-permute-start | bytes 307208 | tf_op jit(solution)/shard_map/ppermute | solution.py:24
  82.2 2.5 %collective-permute-done.9 = f32[40,640]{1,0:T(8,128)S(1)} collective-permute-done((f32[40,640]{1,0:T(8,128)S(1)}, f32[40,640]{1,0:T(8,128)S(1)}, u32[]{:S(2)}, u32[]{:S(2)}) %collective-permute-start.9) | collective-permute-done | bytes 102432 | tf_op jit(solution)/shard_map/ppermute | solution.py:24
  85.5 3.9 %collective-permute-done.10 = f32[40,640]{1,0:T(8,128)S(1)} collective-permute-done((f32[40,640]{1,0:T(8,128)S(1)}, f32[40,640]{1,0:T(8,128)S(1)}, u32[]{:S(2)}, u32[]{:S(2)}) %collective-permute-start.10) | collective-permute-done | bytes 102432 | tf_op jit(solution)/shard_map/ppermute | solution.py:24
  90.8 2.4 %collective-permute-start.27 = (f32[320,256]{1,0:T(8,128)S(1)}, f32[320,256]{1,0:T(8,128)S(1)}, u32[]{:S(2)}, u32[]{:S(2)}) collective-permute-start(f32[320,256]{1,0:T(8,128)S(1)} %maximum_select_fusion.8), channel_id=1, source_target_pairs={{0,2},{1,3},{2,0},{3,1},{4,6},{5,7},{6,4},{7,5},{8,10},{9,11},{10,... | collective-permute-start | bytes 983048 | tf_op jit(solution)/shard_map/ppermute | solution.py:24
  93.3 2.0 %collective-permute-done.11 = f32[40,1280]{1,0:T(8,128)S(1)} collective-permute-done((f32[40,1280]{1,0:T(8,128)S(1)}, f32[40,1280]{1,0:T(8,128)S(1)}, u32[]{:S(2)}, u32[]{:S(2)}) %collective-permute-start.11) | collective-permute-done | bytes 204832 | tf_op jit(solution)/shard_map/ppermute | solution.py:24
  96.4 2.6 %collective-permute-done.27 = f32[320,256]{1,0:T(8,128)S(1)} collective-permute-done((f32[320,256]{1,0:T(8,128)S(1)}, f32[320,256]{1,0:T(8,128)S(1)}, u32[]{:S(2)}, u32[]{:S(2)}) %collective-permute-start.27) | collective-permute-done | bytes 327712 | tf_op jit(solution)/shard_map/ppermute | solution.py:24
  99.1 4.2 %collective-permute-done.12 = f32[80,1280]{1,0:T(8,128)S(1)} collective-permute-done((f32[80,1280]{1,0:T(8,128)S(1)}, f32[80,1280]{1,0:T(8,128)S(1)}, u32[]{:S(2)}, u32[]{:S(2)}) %collective-permute-start.12) | collective-permute-done | bytes 409632 | tf_op jit(solution)/shard_map/ppermute | solution.py:24
  104.0 1.8 %collective-permute-done.14 = f32[1280]{0:T(1024)S(1)} collective-permute-done((f32[1280]{0:T(1024)S(1)}, f32[1280]{0:T(1024)S(1)}, u32[]{:S(2)}, u32[]{:S(2)}) %collective-permute-start.14) | collective-permute-done | bytes 5152 | tf_op jit(solution)/shard_map/ppermute | solution.py:24
  105.8 1.7 %collective-permute-start.15 = (f32[1280]{0:T(1024)S(1)}, f32[1280]{0:T(1024)S(1)}, u32[]{:S(2)}, u32[]{:S(2)}) collective-permute-start(f32[1280]{0:T(1024)S(1)} %add.153), channel_id=1, source_target_pairs={{0,2},{1,3},{2,0},{3,1},{4,6},{5,7},{6,4},{7,5},{8,10},{9,11},{10,... | collective-permute-start | bytes 15368 | tf_op jit(solution)/shard_map/ppermute | solution.py:24
  107.5 1.9 %collective-permute-done.15 = f32[1280]{0:T(1024)S(1)} collective-permute-done((f32[1280]{0:T(1024)S(1)}, f32[1280]{0:T(1024)S(1)}, u32[]{:S(2)}, u32[]{:S(2)}) %collective-permute-start.15) | collective-permute-done | bytes 5152 | tf_op jit(solution)/shard_map/ppermute | solution.py:24
  110.2 2.9 %collective-permute-done.16 = f32[1280]{0:T(1024)S(1)} collective-permute-done((f32[1280]{0:T(1024)S(1)}, f32[1280]{0:T(1024)S(1)}, u32[]{:S(2)}, u32[]{:S(2)}) %collective-permute-start.16) | collective-permute-done | bytes 5152 | tf_op jit(solution)/shard_map/ppermute | solution.py:24
  114.2 2.6 %collective-permute-done.17 = f32[1280]{0:T(1024)S(1)} collective-permute-done((f32[1280]{0:T(1024)S(1)}, f32[1280]{0:T(1024)S(1)}, u32[]{:S(2)}, u32[]{:S(2)}) %collective-permute-start.17) | collective-permute-done | bytes 5152 | tf_op jit(solution)/shard_map/ppermute | solution.py:24
  116.8 4.7 %collective-permute-start.18 = (f32[1280]{0:T(1024)S(1)}, f32[1280]{0:T(1024)S(1)}, u32[]{:S(2)}, u32[]{:S(2)}) collective-permute-start(f32[1280]{0:T(1024)S(1)} %add.156), channel_id=1, source_target_pairs={{0,16},{4,20},{8,24},{12,28},{16,0},{20,4},{24,8},{28,12},{1,17},{... | collective-permute-start | bytes 15368 | tf_op jit(solution)/shard_map/ppermute | solution.py:24
  123.7 2.5 %maximum_select_fusion.1 = f32[1280,256]{1,0:T(8,128)} fusion(f32[640,256]{1,0:T(8,128)S(1)} %maximum_select_fusion.3, f32[640,256]{1,0:T(8,128)} %collective-permute-done.28, pred[]{:T(512)S(6)} %ne.10), kind=kLoop, calls=%fused_computation.20 | loop fusion | flops 983040 | bytes 2621441 | tf_op jit(solution)/shard_map/jit(_where)/select_n | solution.py:82
  (95 shorter events, 32.5 us)
Async XLA Ops:
  6.9 2.5 %copy-start.2 = (bf16[1280,256]{1,0:T(8,128)(2,1)S(1)}, bf16[1280,256]{1,0:T(8,128)(2,1)}, u32[]{:S(2)}) copy-start(bf16[1280,256]{1,0:T(8,128)(2,1)} %param.7) | copy-start | bytes 1966084
  9.8 5.9 %collective-permute-start = (bf16[1,40,256]{2,1,0:T(8,128)(2,1)S(1)}, bf16[1,40,256]{2,1,0:T(8,128)(2,1)S(1)}, u32[]{:S(2)}, u32[]{:S(2)}) collective-permute-start(bf16[1,40,256]{2,1,0:T(8,128)(2,1)S(1)} %fusion.51), channel_id=1, source_target_pairs={{0,16},{4,20},{8,24},{12,28},{16,0},{20,4},{24,8},{28,12},{1,17},{... | collective-permute-start | bytes 61448 | tf_op jit(solution)/shard_map/ppermute | solution.py:24
  15.8 4.1 %collective-permute-start.1 = (bf16[2,1,40,256]{3,2,0,1:T(8,128)(2,1)S(1)}, bf16[2,1,40,256]{3,2,0,1:T(8,128)(2,1)S(1)}, u32[]{:S(2)}, u32[]{:S(2)}) collective-permute-start(bf16[2,1,40,256]{3,2,0,1:T(8,128)(2,1)S(1)} %maximum_select_fusion.16), channel_id=1, source_target_pairs={{0,8},{4,12},{8,0},{12,4},{16,24},{20,28},{24,16},{28,20},{1,9},{5... | collective-permute-start | bytes 122888 | tf_op jit(solution)/shard_map/ppermute | solution.py:24
  19.8 4.5 %collective-permute-start.2 = (bf16[2,2,1,40,256]{4,3,1,0,2:T(8,128)(2,1)S(1)}, bf16[2,2,1,40,256]{4,3,1,0,2:T(8,128)(2,1)S(1)}, u32[]{:S(2)}, u32[]{:S(2)}) collective-permute-start(bf16[2,2,1,40,256]{4,3,1,0,2:T(8,128)(2,1)S(1)} %maximum_select_fusion.13), channel_id=1, source_target_pairs={{0,4},{4,0},{8,12},{12,8},{16,20},{20,16},{24,28},{28,24},{1,5},{5... | collective-permute-start | bytes 245768 | tf_op jit(solution)/shard_map/ppermute | solution.py:24
  24.4 5.4 %collective-permute-start.3 = (bf16[2,2,2,1,40,256]{5,4,2,1,0,3:T(8,128)(2,1)S(1)}, bf16[2,2,2,1,40,256]{5,4,2,1,0,3:T(8,128)(2,1)S(1)}, u32[]{:S(2)}, u32[]{:S(2)}) collective-permute-start(bf16[2,2,2,1,40,256]{5,4,2,1,0,3:T(8,128)(2,1)S(1)} %maximum_select_fusion.10), channel_id=1, source_target_pairs={{0,2},{1,3},{2,0},{3,1},{4,6},{5,7},{6,4},{7,5},{8,10},{9,11},{10,... | collective-permute-start | bytes 491528 | tf_op jit(solution)/shard_map/ppermute | solution.py:24
  29.8 1.7 %collective-permute-start.4 = (bf16[2,2,2,2,1,40,256]{6,5,3,2,1,4,0:T(8,128)(2,1)S(1)}, bf16[2,2,2,2,1,40,256]{6,5,3,2,1,4,0:T(8,128)(2,1)S(1)}, u32[]{:S(2)}, u32[]{:S(2)}) collective-permute-start(bf16[2,2,2,2,1,40,256]{6,5,3,2,1,4,0:T(8,128)(2,1)S(1)} %maximum_select_fusion.5), channel_id=1, source_target_pairs={{0,1},{1,0},{2,3},{3,2},{4,5},{5,4},{6,7},{7,6},{8,9},{9,8},{10,11... | collective-permute-start | bytes 983048 | tf_op jit(solution)/shard_map/ppermute | solution.py:24
  32.5 3.2 %copy-start.4 = (bf16[2,2,2,2,2,1,40,256]{7,6,4,3,2,5,1,0:T(8,128)(2,1)S(1)}, bf16[2,2,2,2,2,1,40,256]{7,6,4,3,2,5,1,0:T(8,128)(2,1)}, u32[]{:S(2)}) copy-start(bf16[2,2,2,2,2,1,40,256]{7,6,4,3,2,5,1,0:T(8,128)(2,1)} %get-tuple-element.6) | copy-start | bytes 1966084
  37.1 2.8 %copy-start.5 = (bf16[640,320]{0,1:T(8,128)(2,1)S(1)}, bf16[640,320]{0,1:T(8,128)(2,1)}, u32[]{:S(2)}) copy-start(bf16[640,320]{0,1:T(8,128)(2,1)} %param.4) | copy-start | bytes 1228804
  38.0 4.1 %collective-permute-start.19 = (f32[640,256]{1,0:T(8,128)}, f32[640,256]{1,0:T(8,128)}, u32[]{:S(2)}, u32[]{:S(2)}) collective-permute-start(f32[640,256]{1,0:T(8,128)} %constant_dynamic-slice_fusion.4), channel_id=1, source_target_pairs={{0,1},{1,0},{2,3},{3,2},{4,5},{5,4},{6,7},{7,6},{8,9},{9,8},{10,11... | collective-permute-start | bytes 1966088 | tf_op jit(solution)/shard_map/ppermute | solution.py:24
  41.9 3.4 %collective-permute-start.5 = (f32[160,1280]{1,0:T(8,128)S(1)}, f32[160,1280]{1,0:T(8,128)}, u32[]{:S(2)}, u32[]{:S(2)}) collective-permute-start(f32[160,1280]{1,0:T(8,128)S(1)} %dynamic-slice_bitcast_fusion), channel_id=1, source_target_pairs={{0,1},{1,0},{2,3},{3,2},{4,5},{5,4},{6,7},{7,6},{8,9},{9,8},{10,11... | collective-permute-start | bytes 2457608 | tf_op jit(solution)/shard_map/ppermute | solution.py:24
  43.3 10.2 %collective-permute-start.20 = (f32[320,256]{1,0:T(8,128)S(1)}, f32[320,256]{1,0:T(8,128)S(1)}, u32[]{:S(2)}, u32[]{:S(2)}) collective-permute-start(f32[320,256]{1,0:T(8,128)S(1)} %constant_dynamic-slice_fusion.3), channel_id=1, source_target_pairs={{0,2},{1,3},{2,0},{3,1},{4,6},{5,7},{6,4},{7,5},{8,10},{9,11},{10,... | collective-permute-start | bytes 983048 | tf_op jit(solution)/shard_map/ppermute | solution.py:24
  53.6 5.9 %collective-permute-start.21 = (f32[160,256]{1,0:T(8,128)S(1)}, f32[160,256]{1,0:T(8,128)S(1)}, u32[]{:S(2)}, u32[]{:S(2)}) collective-permute-start(f32[160,256]{1,0:T(8,128)S(1)} %constant_dynamic-slice_fusion.2), channel_id=1, source_target_pairs={{0,4},{4,0},{8,12},{12,8},{16,20},{20,16},{24,28},{28,24},{1,5},{5... | collective-permute-start | bytes 491528 | tf_op jit(solution)/shard_map/ppermute | solution.py:24
  55.5 10.7 %collective-permute-start.6 = (f32[80,1280]{1,0:T(8,128)S(1)}, f32[80,1280]{1,0:T(8,128)S(1)}, u32[]{:S(2)}, u32[]{:S(2)}) collective-permute-start(f32[80,1280]{1,0:T(8,128)S(1)} %constant_dynamic-slice_fusion.7), channel_id=1, source_target_pairs={{0,2},{1,3},{2,0},{3,1},{4,6},{5,7},{6,4},{7,5},{8,10},{9,11},{10,... | collective-permute-start | bytes 1228808 | tf_op jit(solution)/shard_map/ppermute | solution.py:24
  59.5 7.2 %collective-permute-start.22 = (f32[80,256]{1,0:T(8,128)S(1)}, f32[80,256]{1,0:T(8,128)S(1)}, u32[]{:S(2)}, u32[]{:S(2)}) collective-permute-start(f32[80,256]{1,0:T(8,128)S(1)} %constant_dynamic-slice_fusion.1), channel_id=1, source_target_pairs={{0,8},{4,12},{8,0},{12,4},{16,24},{20,28},{24,16},{28,20},{1,9},{5... | collective-permute-start | bytes 245768 | tf_op jit(solution)/shard_map/ppermute | solution.py:24
  66.3 5.8 %collective-permute-start.7 = (f32[40,1280]{1,0:T(8,128)S(1)}, f32[40,1280]{1,0:T(8,128)S(1)}, u32[]{:S(2)}, u32[]{:S(2)}) collective-permute-start(f32[40,1280]{1,0:T(8,128)S(1)} %constant_dynamic-slice_fusion.6), channel_id=1, source_target_pairs={{0,4},{4,0},{8,12},{12,8},{16,20},{20,16},{24,28},{28,24},{1,5},{5... | collective-permute-start | bytes 614408 | tf_op jit(solution)/shard_map/ppermute | solution.py:24
  66.8 6.9 %collective-permute-start.23 = (f32[40,256]{1,0:T(8,128)S(1)}, f32[40,256]{1,0:T(8,128)S(1)}, u32[]{:S(2)}, u32[]{:S(2)}) collective-permute-start(f32[40,256]{1,0:T(8,128)S(1)} %constant_dynamic-slice_fusion), channel_id=1, source_target_pairs={{0,16},{4,20},{8,24},{12,28},{16,0},{20,4},{24,8},{28,12},{1,17},{... | collective-permute-start | bytes 122888 | tf_op jit(solution)/shard_map/ppermute | solution.py:24
  72.1 5.7 %collective-permute-start.8 = (f32[40,640]{1,0:T(8,128)S(1)}, f32[40,640]{1,0:T(8,128)S(1)}, u32[]{:S(2)}, u32[]{:S(2)}) collective-permute-start(f32[40,640]{1,0:T(8,128)S(1)} %constant_dynamic-slice_fusion.5), channel_id=1, source_target_pairs={{0,8},{4,12},{8,0},{12,4},{16,24},{20,28},{24,16},{28,20},{1,9},{5... | collective-permute-start | bytes 307208 | tf_op jit(solution)/shard_map/ppermute | solution.py:24
  73.7 6.9 %collective-permute-start.24 = (f32[40,256]{1,0:T(8,128)S(1)}, f32[40,256]{1,0:T(8,128)S(1)}, u32[]{:S(2)}, u32[]{:S(2)}) collective-permute-start(f32[40,256]{1,0:T(8,128)S(1)} %dynamic-slice_add_fusion.7), channel_id=1, source_target_pairs={{0,16},{4,20},{8,24},{12,28},{16,0},{20,4},{24,8},{28,12},{1,17},{... | collective-permute-start | bytes 122888 | tf_op jit(solution)/shard_map/ppermute | solution.py:24
  77.8 6.8 %collective-permute-start.9 = (f32[40,640]{1,0:T(8,128)S(1)}, f32[40,640]{1,0:T(8,128)S(1)}, u32[]{:S(2)}, u32[]{:S(2)}) collective-permute-start(f32[40,640]{1,0:T(8,128)S(1)} %dynamic-slice_add_fusion.5), channel_id=1, source_target_pairs={{0,16},{4,20},{8,24},{12,28},{16,0},{20,4},{24,8},{28,12},{1,17},{... | collective-permute-start | bytes 307208 | tf_op jit(solution)/shard_map/ppermute | solution.py:24
  80.5 4.8 %collective-permute-start.25 = (f32[80,256]{1,0:T(8,128)S(1)}, f32[80,256]{1,0:T(8,128)S(1)}, u32[]{:S(2)}, u32[]{:S(2)}) collective-permute-start(f32[80,256]{1,0:T(8,128)S(1)} %maximum_select_fusion.15), channel_id=1, source_target_pairs={{0,8},{4,12},{8,0},{12,4},{16,24},{20,28},{24,16},{28,20},{1,9},{5... | collective-permute-start | bytes 245768 | tf_op jit(solution)/shard_map/ppermute | solution.py:24
  84.7 4.7 %collective-permute-start.10 = (f32[40,640]{1,0:T(8,128)S(1)}, f32[40,640]{1,0:T(8,128)S(1)}, u32[]{:S(2)}, u32[]{:S(2)}) collective-permute-start(f32[40,640]{1,0:T(8,128)S(1)} %add.152), channel_id=1, source_target_pairs={{0,8},{4,12},{8,0},{12,4},{16,24},{20,28},{24,16},{28,20},{1,9},{5... | collective-permute-start | bytes 307208 | tf_op jit(solution)/shard_map/ppermute | solution.py:24
  85.4 5.4 %collective-permute-start.26 = (f32[160,256]{1,0:T(8,128)S(1)}, f32[160,256]{1,0:T(8,128)S(1)}, u32[]{:S(2)}, u32[]{:S(2)}) collective-permute-start(f32[160,256]{1,0:T(8,128)S(1)} %maximum_select_fusion.12), channel_id=1, source_target_pairs={{0,4},{4,0},{8,12},{12,8},{16,20},{20,16},{24,28},{28,24},{1,5},{5... | collective-permute-start | bytes 491528 | tf_op jit(solution)/shard_map/ppermute | solution.py:24
  89.4 5.8 %collective-permute-start.11 = (f32[40,1280]{1,0:T(8,128)S(1)}, f32[40,1280]{1,0:T(8,128)S(1)}, u32[]{:S(2)}, u32[]{:S(2)}) collective-permute-start(f32[40,1280]{1,0:T(8,128)S(1)} %maximum_select_fusion.9), channel_id=1, source_target_pairs={{0,4},{4,0},{8,12},{12,8},{16,20},{20,16},{24,28},{28,24},{1,5},{5... | collective-permute-start | bytes 614408 | tf_op jit(solution)/shard_map/ppermute | solution.py:24
  90.8 8.1 %collective-permute-start.27 = (f32[320,256]{1,0:T(8,128)S(1)}, f32[320,256]{1,0:T(8,128)S(1)}, u32[]{:S(2)}, u32[]{:S(2)}) collective-permute-start(f32[320,256]{1,0:T(8,128)S(1)} %maximum_select_fusion.8), channel_id=1, source_target_pairs={{0,2},{1,3},{2,0},{3,1},{4,6},{5,7},{6,4},{7,5},{8,10},{9,11},{10,... | collective-permute-start | bytes 983048 | tf_op jit(solution)/shard_map/ppermute | solution.py:24
  95.3 8.1 %collective-permute-start.12 = (f32[80,1280]{1,0:T(8,128)S(1)}, f32[80,1280]{1,0:T(8,128)S(1)}, u32[]{:S(2)}, u32[]{:S(2)}) collective-permute-start(f32[80,1280]{1,0:T(8,128)S(1)} %maximum_select_fusion.4), channel_id=1, source_target_pairs={{0,2},{1,3},{2,0},{3,1},{4,6},{5,7},{6,4},{7,5},{8,10},{9,11},{10,... | collective-permute-start | bytes 1228808 | tf_op jit(solution)/shard_map/ppermute | solution.py:24
  99.0 24.7 %collective-permute-start.28 = (f32[640,256]{1,0:T(8,128)S(1)}, f32[640,256]{1,0:T(8,128)}, u32[]{:S(2)}, u32[]{:S(2)}) collective-permute-start(f32[640,256]{1,0:T(8,128)S(1)} %maximum_select_fusion.3), channel_id=1, source_target_pairs={{0,1},{1,0},{2,3},{3,2},{4,5},{5,4},{6,7},{7,6},{8,9},{9,8},{10,11... | collective-permute-start | bytes 1966088 | tf_op jit(solution)/shard_map/ppermute | solution.py:24
  103.4 22.9 %collective-permute-start.13 = (f32[160,1280]{1,0:T(8,128)S(1)}, f32[160,1280]{1,0:T(8,128)S(1)}, u32[]{:S(2)}, u32[]{:S(2)}) collective-permute-start(f32[160,1280]{1,0:T(8,128)S(1)} %maximum_select_fusion.2), channel_id=1, source_target_pairs={{0,1},{1,0},{2,3},{3,2},{4,5},{5,4},{6,7},{7,6},{8,9},{9,8},{10,11... | collective-permute-start | bytes 2457608 | tf_op jit(solution)/shard_map/ppermute | solution.py:24
  103.5 2.3 %collective-permute-start.14 = (f32[1280]{0:T(1024)S(1)}, f32[1280]{0:T(1024)S(1)}, u32[]{:S(2)}, u32[]{:S(2)}) collective-permute-start(f32[1280]{0:T(1024)S(1)} %get-tuple-element.4), channel_id=1, source_target_pairs={{0,1},{1,0},{2,3},{3,2},{4,5},{5,4},{6,7},{7,6},{8,9},{9,8},{10,11... | collective-permute-start | bytes 15368 | tf_op jit(solution)/shard_map/ppermute | solution.py:24
  105.8 3.7 %collective-permute-start.15 = (f32[1280]{0:T(1024)S(1)}, f32[1280]{0:T(1024)S(1)}, u32[]{:S(2)}, u32[]{:S(2)}) collective-permute-start(f32[1280]{0:T(1024)S(1)} %add.153), channel_id=1, source_target_pairs={{0,2},{1,3},{2,0},{3,1},{4,6},{5,7},{6,4},{7,5},{8,10},{9,11},{10,... | collective-permute-start | bytes 15368 | tf_op jit(solution)/shard_map/ppermute | solution.py:24
  109.5 3.7 %collective-permute-start.16 = (f32[1280]{0:T(1024)S(1)}, f32[1280]{0:T(1024)S(1)}, u32[]{:S(2)}, u32[]{:S(2)}) collective-permute-start(f32[1280]{0:T(1024)S(1)} %add.154), channel_id=1, source_target_pairs={{0,4},{4,0},{8,12},{12,8},{16,20},{20,16},{24,28},{28,24},{1,5},{5... | collective-permute-start | bytes 15368 | tf_op jit(solution)/shard_map/ppermute | solution.py:24
  113.1 3.7 %collective-permute-start.17 = (f32[1280]{0:T(1024)S(1)}, f32[1280]{0:T(1024)S(1)}, u32[]{:S(2)}, u32[]{:S(2)}) collective-permute-start(f32[1280]{0:T(1024)S(1)} %add.155), channel_id=1, source_target_pairs={{0,8},{4,12},{8,0},{12,4},{16,24},{20,28},{24,16},{28,20},{1,9},{5... | collective-permute-start | bytes 15368 | tf_op jit(solution)/shard_map/ppermute | solution.py:24
  116.8 6.4 %collective-permute-start.18 = (f32[1280]{0:T(1024)S(1)}, f32[1280]{0:T(1024)S(1)}, u32[]{:S(2)}, u32[]{:S(2)}) collective-permute-start(f32[1280]{0:T(1024)S(1)} %add.156), channel_id=1, source_target_pairs={{0,16},{4,20},{8,24},{12,28},{16,0},{20,4},{24,8},{28,12},{1,17},{... | collective-permute-start | bytes 15368 | tf_op jit(solution)/shard_map/ppermute | solution.py:24
  (3 other events, 4.5 us)

commit v2 on v1

--- a/solution.py
+++ b/solution.py
@@ -124,9 +124,6 @@
         grad_rows = (
             (grad_unit - unit * jnp.sum(unit * grad_unit, axis=1, keepdims=True)) / rnorm
         ).astype(jnp.bfloat16)
-        grad_proj = lax.dot_general(
-            pooled, grad_rows, (((0,), (0,)), ((), ())), preferred_element_type=jnp.float32
-        )
         grad_pooled = lax.dot_general(
             grad_rows, proj_weight, (((1,), (1,)), ((), ())), preferred_element_type=jnp.float32
         )
@@ -135,13 +132,31 @@
         ).reshape(images * POS, channels)
         sig = jax.nn.sigmoid(pre)
         grad_pre = (grad_act * sig * (1.0 + pre * (1.0 - sig))).astype(jnp.bfloat16)
-        grad_shift = jnp.sum(grad_pre.astype(jnp.float32), axis=0)
-        grad_head = lax.dot_general(
-            feature_map, grad_pre, (((0,), (0,)), ((), ())), preferred_element_type=jnp.float32
-        )
+        c_in = feature_map.shape[1]
         if steps:
-            grad_head, grad_proj, grad_shift = all_reduce([grad_head, grad_proj, grad_shift], mesh, steps)
+            ones = jnp.ones((feature_map.shape[0], 1), feature_map.dtype)
+            head_shift = lax.dot_general(
+                jnp.concatenate([feature_map, ones], axis=1), grad_pre, (((0,), (0,)), ((), ())),
+                preferred_element_type=jnp.float32,
+            )
+            proj_t = lax.dot_general(
+                grad_rows, pooled, (((0,), (0,)), ((), ())), preferred_element_type=jnp.float32
+            )
+            used = head_shift.shape[0] + proj_t.shape[0]
+            rows = -(-used // 64) * 64
+            pad = jnp.zeros((rows - used, channels), jnp.float32)
+            (buf,) = all_reduce([jnp.concatenate([head_shift, proj_t, pad], axis=0)], mesh, steps)
+            grad_head = buf[:c_in]
+            grad_shift = buf[c_in]
+            grad_proj = buf[c_in + 1 : used].T
         else:
+            grad_proj = lax.dot_general(
+                pooled, grad_rows, (((0,), (0,)), ((), ())), preferred_element_type=jnp.float32
+            )
+            grad_shift = jnp.sum(grad_pre.astype(jnp.float32), axis=0)
+            grad_head = lax.dot_general(
+                feature_map, grad_pre, (((0,), (0,)), ((), ())), preferred_element_type=jnp.float32
+            )
             grad_head, grad_shift, grad_proj = lax.psum((grad_head, grad_shift, grad_proj), ("blk", "dp"))
         return (loss, grad_head, grad_shift, grad_proj)
 

time: 129 us -> 140 us (1.085)
  waiting for transfers between devices: 55.9 us -> 76.8 us
  starting transfers between devices: 42.6 us -> 29.8 us
  local copies, waits for them, and re-layouts: 3.79 us -> 6.59 us
    ppermute x29 -> x15, waiting for transfers between devices: 55.9 us -> 76.8 us  [swap(): return lax.ppermute(x, ax, [(i, i ^ mask) for i in range(mesh.shape[ax])])]
    ppermute x29 -> x15, starting transfers between devices: 42.6 us -> 29.8 us  [swap(): return lax.ppermute(x, ax, [(i, i ^ mask) for i in range(mesh.shape[ax])])]
    convert_element_type x0 -> x1, other arithmetic: none -> 3.08 us  [body(): grad_pre = (grad_act * sig * (1.0 + pre * (1.0 - sig))).astype(jnp.bfloat16)]
    slice x0 -> x2, local copies, waits for them, and re-layouts: none -> 1.89 us  [the longest x1 1.27 us: body(): grad_head = buf[:c_in]]
    unnamed x12 -> x9, local copies, waits for them, and re-layouts: 2.69 us -> 4.28 us
    select_n x9 -> x5, other arithmetic: 4.04 us -> 2.58 us  [all_reduce(): jnp.where(bit, jnp.concatenate([g, c], axis=d), jnp.concatenate([c, g], a...]
    add x15 -> x5, other arithmetic: 3.45 us -> 3.42 us  [all_reduce(): cur = [kk + g for kk, g in zip(keeps, got)]]
  transfers between devices with their start and end apart: 29 -> 15, of which waited for: 21 -> 15; matrix products, arithmetic and copies ran while one was open for 7% -> 0% of each run, Pallas kernels for 0% -> 0%
where the time goes in v2:
time: 140 us; the launch traced here: 139 us
  waiting for transfers between devices  76.8 us (55%)
  starting transfers between devices  29.8 us (21%)
  other arithmetic  12.5 us (9%)
  matrix products  10.1 us (7%)
  local copies, waits for them, and re-layouts  6.59 us (5%)
  between operations  3.39 us (2%)
    ppermute x15, waiting for transfers between devices, swap(): return lax.ppermute(x, ax, [(i, i ^ mask) for i in range(mesh.shape[ax])])  76.8 us
    ppermute x15, starting transfers between devices, swap(): return lax.ppermute(x, ax, [(i, i ^ mask) for i in range(mesh.shape[ax])])  29.8 us
    dot_general x1, matrix products, body(): jnp.dot(feature_map, head_weight, preferred_element_type=jnp.float32)  4.98 us
    unnamed x9, local copies, waits for them, and re-layouts  4.28 us
    add x5, other arithmetic, all_reduce(): cur = [kk + g for kk, g in zip(keeps, got)]  3.42 us
    convert_element_type x1, other arithmetic, body(): grad_pre = (grad_act * sig * (1.0 + pre * (1.0 - sig))).astype(jnp.bfloat16)  3.08 us
  transfers between devices with their start and end apart: 15, of which 15 were waited for; matrix products, arithmetic and copies ran while one was open for 0% of the time, Pallas kernels for 0%

profile of v2, /device:TPU:0, one launch (start us, length us, event | category | flops | bytes accessed | tf_op | source)
XLA Modules:
  0.0 139.2 jit_solution(9969083919282827922)
XLA Ops:
  1.8 5.0 %fusion.5 = (f32[640,1280]{1,0:T(8,128)}, f32[640,1280]{1,0:T(8,128)}) fusion(f32[1280]{0:T(1024)} %param.6, bf16[640,320]{0,1:T(8,128)(2,1)} %param.4, bf16[320,1280]{1,0:T(8,128)(2,1)S(1)} %copy-done), kind=kOutput, calls=%fused_computation.12 | convolution fusion | flops 528384000 | bytes 7787520 | tf_op jit(solution)/shard_map/dot_general | solution.py:101
  6.8 2.5 %reduce_sum.36 = f32[40,1280]{1,0:T(8,128)S(1)} reduce(f32[40,16,1280]{2,1,0:T(8,128)} %bitcast.65, f32[]{:T(128)} %constant.23.clone.1), dimensions={1}, to_apply=%region_0.1 | reduce | flops 768000 | bytes 3481604 | tf_op jit(solution)/shard_map/reduce_sum | solution.py:103
  9.7 4.1 %collective-permute-start = (bf16[1,40,256]{2,1,0:T(8,128)(2,1)S(1)}, bf16[1,40,256]{2,1,0:T(8,128)(2,1)S(1)}, u32[]{:S(2)}, u32[]{:S(2)}) collective-permute-start(bf16[1,40,256]{2,1,0:T(8,128)(2,1)S(1)} %fusion.51), channel_id=1, source_target_pairs={{0,16},{4,20},{8,24},{12,28},{16,0},{20,4},{24,8},{28,12},{1,17},{... | collective-permute-start | bytes 61448 | tf_op jit(solution)/shard_map/ppermute | solution.py:24
  14.1 1.6 %collective-permute-done = bf16[1,40,256]{2,1,0:T(8,128)(2,1)S(1)} collective-permute-done((bf16[1,40,256]{2,1,0:T(8,128)(2,1)S(1)}, bf16[1,40,256]{2,1,0:T(8,128)(2,1)S(1)}, u32[]{:S(2)}, u32[]{:S(2)}) %collective-permute-start) | collective-permute-done | bytes 20512 | tf_op jit(solution)/shard_map/ppermute | solution.py:24
  15.7 2.0 %collective-permute-start.1 = (bf16[2,1,40,256]{3,2,0,1:T(8,128)(2,1)S(1)}, bf16[2,1,40,256]{3,2,0,1:T(8,128)(2,1)S(1)}, u32[]{:S(2)}, u32[]{:S(2)}) collective-permute-start(bf16[2,1,40,256]{3,2,0,1:T(8,128)(2,1)S(1)} %maximum_select_fusion.12), channel_id=1, source_target_pairs={{0,8},{4,12},{8,0},{12,4},{16,24},{20,28},{24,16},{28,20},{1,9},{5... | collective-permute-start | bytes 122888 | tf_op jit(solution)/shard_map/ppermute | solution.py:24
  17.6 2.1 %collective-permute-done.1 = bf16[2,1,40,256]{3,2,0,1:T(8,128)(2,1)S(1)} collective-permute-done((bf16[2,1,40,256]{3,2,0,1:T(8,128)(2,1)S(1)}, bf16[2,1,40,256]{3,2,0,1:T(8,128)(2,1)S(1)}, u32[]{:S(2)}, u32[]{:S(2)}) %collective-permute-start.1) | collective-permute-done | bytes 40992 | tf_op jit(solution)/shard_map/ppermute | solution.py:24
  19.7 2.0 %collective-permute-start.2 = (bf16[2,2,1,40,256]{4,3,1,0,2:T(8,128)(2,1)S(1)}, bf16[2,2,1,40,256]{4,3,1,0,2:T(8,128)(2,1)S(1)}, u32[]{:S(2)}, u32[]{:S(2)}) collective-permute-start(bf16[2,2,1,40,256]{4,3,1,0,2:T(8,128)(2,1)S(1)} %maximum_select_fusion.10), channel_id=1, source_target_pairs={{0,4},{4,0},{8,12},{12,8},{16,20},{20,16},{24,28},{28,24},{1,5},{5... | collective-permute-start | bytes 245768 | tf_op jit(solution)/shard_map/ppermute | solution.py:24
  21.8 2.5 %collective-permute-done.2 = bf16[2,2,1,40,256]{4,3,1,0,2:T(8,128)(2,1)S(1)} collective-permute-done((bf16[2,2,1,40,256]{4,3,1,0,2:T(8,128)(2,1)S(1)}, bf16[2,2,1,40,256]{4,3,1,0,2:T(8,128)(2,1)S(1)}, u32[]{:S(2)}, u32[]{:S(2)}) %collective-permute-start.2) | collective-permute-done | bytes 81952 | tf_op jit(solution)/shard_map/ppermute | solution.py:24
  24.3 2.0 %collective-permute-start.3 = (bf16[2,2,2,1,40,256]{5,4,2,1,0,3:T(8,128)(2,1)S(1)}, bf16[2,2,2,1,40,256]{5,4,2,1,0,3:T(8,128)(2,1)S(1)}, u32[]{:S(2)}, u32[]{:S(2)}) collective-permute-start(bf16[2,2,2,1,40,256]{5,4,2,1,0,3:T(8,128)(2,1)S(1)} %maximum_select_fusion.8), channel_id=1, source_target_pairs={{0,2},{1,3},{2,0},{3,1},{4,6},{5,7},{6,4},{7,5},{8,10},{9,11},{10,... | collective-permute-start | bytes 491528 | tf_op jit(solution)/shard_map/ppermute | solution.py:24
  26.4 3.3 %collective-permute-done.3 = bf16[2,2,2,1,40,256]{5,4,2,1,0,3:T(8,128)(2,1)S(1)} collective-permute-done((bf16[2,2,2,1,40,256]{5,4,2,1,0,3:T(8,128)(2,1)S(1)}, bf16[2,2,2,1,40,256]{5,4,2,1,0,3:T(8,128)(2,1)S(1)}, u32[]{:S(2)}, u32[]{:S(2)}) %collective-permute-start.3) | collective-permute-done | bytes 163872 | tf_op jit(solution)/shard_map/ppermute | solution.py:24
  31.6 2.5 %fusion.10 = f32[]{:T(128)} fusion(bf16[1280,256]{1,0:T(8,128)(2,1)S(1)} %bitcast.70), kind=kOutput, calls=%fused_computation.21 | convolution fusion | flops 847052800 | bytes 655364 | tf_op jit(solution)/shard_map/dot_general | solution.py:87
  36.2 3.1 %fusion.4 = bf16[640,1280]{1,0:T(8,128)(2,1)S(1)} fusion(f32[640,1280]{1,0:T(8,128)} %get-tuple-element.18, f32[40,1280]{1,0:T(8,128)S(1)} %convolution_multiply_fusion), kind=kLoop, calls=%fused_computation.10 | loop fusion | flops 7372800 | bytes 5120000 | tf_op jit(solution)/shard_map/convert_element_type | solution.py:134
  40.5 1.7 %copy-done.1 = f32[640,1280]{1,0:T(8,128)} copy-done((f32[640,1280]{1,0:T(8,128)}, f32[640,1280]{1,0:T(8,128)S(1)}, u32[]{:S(2)}) %copy-start.1) | copy-done | bytes 3276824
  42.5 3.5 %collective-permute-done.5 = f32[320,1280]{1,0:T(8,128)} collective-permute-done((f32[320,1280]{1,0:T(8,128)S(1)}, f32[320,1280]{1,0:T(8,128)}, u32[]{:S(2)}, u32[]{:S(2)}) %collective-permute-start.5) | collective-permute-done | bytes 1638432 | tf_op jit(solution)/shard_map/ppermute | solution.py:24
  46.0 2.1 %dynamic-slice_add_fusion = f32[320,1280]{1,0:T(8,128)S(1)} fusion(f32[320,1280]{1,0:T(8,128)} %collective-permute-done.5, f32[640,1280]{1,0:T(8,128)} %copy-done.1, s32[]{:T(128)S(6)} %mul.93), kind=kLoop, calls=%fused_computation.20 | loop fusion | flops 409600 | bytes 4915204 | tf_op jit(solution)/shard_map/add | solution.py:71
  48.1 2.0 %collective-permute-start.6 = (f32[160,1280]{1,0:T(8,128)S(1)}, f32[160,1280]{1,0:T(8,128)}, u32[]{:S(2)}, u32[]{:S(2)}) collective-permute-start(f32[160,1280]{1,0:T(8,128)S(1)} %constant_dynamic-slice_fusion.3), channel_id=1, source_target_pairs={{0,2},{1,3},{2,0},{3,1},{4,6},{5,7},{6,4},{7,5},{8,10},{9,11},{10,... | collective-permute-start | bytes 2457608 | tf_op jit(solution)/shard_map/ppermute | solution.py:24
  50.1 18.7 %collective-permute-done.6 = f32[160,1280]{1,0:T(8,128)} collective-permute-done((f32[160,1280]{1,0:T(8,128)S(1)}, f32[160,1280]{1,0:T(8,128)}, u32[]{:S(2)}, u32[]{:S(2)}) %collective-permute-start.6) | collective-permute-done | bytes 819232 | tf_op jit(solution)/shard_map/ppermute | solution.py:24
  70.0 1.8 %collective-permute-start.7 = (f32[80,1280]{1,0:T(8,128)S(1)}, f32[80,1280]{1,0:T(8,128)S(1)}, u32[]{:S(2)}, u32[]{:S(2)}) collective-permute-start(f32[80,1280]{1,0:T(8,128)S(1)} %constant_dynamic-slice_fusion.2), channel_id=1, source_target_pairs={{0,4},{4,0},{8,12},{12,8},{16,20},{20,16},{24,28},{28,24},{1,5},{5... | collective-permute-start | bytes 1228808 | tf_op jit(solution)/shard_map/ppermute | solution.py:24
  71.9 9.1 %collective-permute-done.7 = f32[80,1280]{1,0:T(8,128)S(1)} collective-permute-done((f32[80,1280]{1,0:T(8,128)S(1)}, f32[80,1280]{1,0:T(8,128)S(1)}, u32[]{:S(2)}, u32[]{:S(2)}) %collective-permute-start.7) | collective-permute-done | bytes 409632 | tf_op jit(solution)/shard_map/ppermute | solution.py:24
  81.0 1.6 %collective-permute-start.8 = (f32[40,1280]{1,0:T(8,128)S(1)}, f32[40,1280]{1,0:T(8,128)S(1)}, u32[]{:S(2)}, u32[]{:S(2)}) collective-permute-start(f32[40,1280]{1,0:T(8,128)S(1)} %constant_dynamic-slice_fusion.1), channel_id=1, source_target_pairs={{0,8},{4,12},{8,0},{12,4},{16,24},{20,28},{24,16},{28,20},{1,9},{5... | collective-permute-start | bytes 614408 | tf_op jit(solution)/shard_map/ppermute | solution.py:24
  82.6 4.2 %collective-permute-done.8 = f32[40,1280]{1,0:T(8,128)S(1)} collective-permute-done((f32[40,1280]{1,0:T(8,128)S(1)}, f32[40,1280]{1,0:T(8,128)S(1)}, u32[]{:S(2)}, u32[]{:S(2)}) %collective-permute-start.8) | collective-permute-done | bytes 204832 | tf_op jit(solution)/shard_map/ppermute | solution.py:24
  86.9 2.7 %collective-permute-start.9 = (f32[40,640]{1,0:T(8,128)S(1)}, f32[40,640]{1,0:T(8,128)S(1)}, u32[]{:S(2)}, u32[]{:S(2)}) collective-permute-start(f32[40,640]{1,0:T(8,128)S(1)} %constant_dynamic-slice_fusion), channel_id=1, source_target_pairs={{0,16},{4,20},{8,24},{12,28},{16,0},{20,4},{24,8},{28,12},{1,17},{... | collective-permute-start | bytes 307208 | tf_op jit(solution)/shard_map/ppermute | solution.py:24
  89.6 2.9 %collective-permute-done.9 = f32[40,640]{1,0:T(8,128)S(1)} collective-permute-done((f32[40,640]{1,0:T(8,128)S(1)}, f32[40,640]{1,0:T(8,128)S(1)}, u32[]{:S(2)}, u32[]{:S(2)}) %collective-permute-start.9) | collective-permute-done | bytes 102432 | tf_op jit(solution)/shard_map/ppermute | solution.py:24
  92.5 3.0 %collective-permute-start.10 = (f32[40,640]{1,0:T(8,128)S(1)}, f32[40,640]{1,0:T(8,128)S(1)}, u32[]{:S(2)}, u32[]{:S(2)}) collective-permute-start(f32[40,640]{1,0:T(8,128)S(1)} %dynamic-slice_add_fusion.4), channel_id=1, source_target_pairs={{0,16},{4,20},{8,24},{12,28},{16,0},{20,4},{24,8},{28,12},{1,17},{... | collective-permute-start | bytes 307208 | tf_op jit(solution)/shard_map/ppermute | solution.py:24
  95.6 3.0 %collective-permute-done.10 = f32[40,640]{1,0:T(8,128)S(1)} collective-permute-done((f32[40,640]{1,0:T(8,128)S(1)}, f32[40,640]{1,0:T(8,128)S(1)}, u32[]{:S(2)}, u32[]{:S(2)}) %collective-permute-start.10) | collective-permute-done | bytes 102432 | tf_op jit(solution)/shard_map/ppermute | solution.py:24
  98.6 5.1 %collective-permute-start.11 = (f32[40,1280]{1,0:T(8,128)S(1)}, f32[40,1280]{1,0:T(8,128)S(1)}, u32[]{:S(2)}, u32[]{:S(2)}) collective-permute-start(f32[40,1280]{1,0:T(8,128)S(1)} %maximum_select_fusion.7), channel_id=1, source_target_pairs={{0,8},{4,12},{8,0},{12,4},{16,24},{20,28},{24,16},{28,20},{1,9},{5... | collective-permute-start | bytes 614408 | tf_op jit(solution)/shard_map/ppermute | solution.py:24
  103.7 3.7 %collective-permute-done.11 = f32[40,1280]{1,0:T(8,128)S(1)} collective-permute-done((f32[40,1280]{1,0:T(8,128)S(1)}, f32[40,1280]{1,0:T(8,128)S(1)}, u32[]{:S(2)}, u32[]{:S(2)}) %collective-permute-start.11) | collective-permute-done | bytes 204832 | tf_op jit(solution)/shard_map/ppermute | solution.py:24
  107.5 1.6 %collective-permute-start.12 = (f32[80,1280]{1,0:T(8,128)S(1)}, f32[80,1280]{1,0:T(8,128)S(1)}, u32[]{:S(2)}, u32[]{:S(2)}) collective-permute-start(f32[80,1280]{1,0:T(8,128)S(1)} %maximum_select_fusion.3), channel_id=1, source_target_pairs={{0,4},{4,0},{8,12},{12,8},{16,20},{20,16},{24,28},{28,24},{1,5},{5... | collective-permute-start | bytes 1228808 | tf_op jit(solution)/shard_map/ppermute | solution.py:24
  109.1 6.4 %collective-permute-done.12 = f32[80,1280]{1,0:T(8,128)S(1)} collective-permute-done((f32[80,1280]{1,0:T(8,128)S(1)}, f32[80,1280]{1,0:T(8,128)S(1)}, u32[]{:S(2)}, u32[]{:S(2)}) %collective-permute-start.12) | collective-permute-done | bytes 409632 | tf_op jit(solution)/shard_map/ppermute | solution.py:24
  117.1 11.3 %collective-permute-done.13 = f32[160,1280]{1,0:T(8,128)S(1)} collective-permute-done((f32[160,1280]{1,0:T(8,128)S(1)}, f32[160,1280]{1,0:T(8,128)S(1)}, u32[]{:S(2)}, u32[]{:S(2)}) %collective-permute-start.13) | collective-permute-done | bytes 819232 | tf_op jit(solution)/shard_map/ppermute | solution.py:24
  129.4 2.9 %collective-permute-done.14 = f32[320,1280]{1,0:T(8,128)} collective-permute-done((f32[320,1280]{1,0:T(8,128)S(1)}, f32[320,1280]{1,0:T(8,128)}, u32[]{:S(2)}, u32[]{:S(2)}) %collective-permute-start.14) | collective-permute-done | bytes 1638432 | tf_op jit(solution)/shard_map/ppermute | solution.py:24
  132.3 2.3 %maximum_select_fusion = f32[640,1280]{1,0:T(8,128)S(1)} fusion(f32[320,1280]{1,0:T(8,128)S(1)} %maximum_select_fusion.1, f32[320,1280]{1,0:T(8,128)} %collective-permute-done.14, pred[]{:T(512)S(6)} %ne.10), kind=kLoop, calls=%fused_computation.7 | loop fusion | flops 2457600 | bytes 6553601 | tf_op jit(solution)/shard_map/jit(_where)/select_n | solution.py:82
  (52 shorter events, 13.5 us)
Async XLA Ops:
  0.6 1.2 copy-start
  6.8 2.5 %copy-start.2 = (bf16[1280,256]{1,0:T(8,128)(2,1)S(1)}, bf16[1280,256]{1,0:T(8,128)(2,1)}, u32[]{:S(2)}) copy-start(bf16[1280,256]{1,0:T(8,128)(2,1)} %param.7) | copy-start | bytes 1966084
  9.7 5.9 %collective-permute-start = (bf16[1,40,256]{2,1,0:T(8,128)(2,1)S(1)}, bf16[1,40,256]{2,1,0:T(8,128)(2,1)S(1)}, u32[]{:S(2)}, u32[]{:S(2)}) collective-permute-start(bf16[1,40,256]{2,1,0:T(8,128)(2,1)S(1)} %fusion.51), channel_id=1, source_target_pairs={{0,16},{4,20},{8,24},{12,28},{16,0},{20,4},{24,8},{28,12},{1,17},{... | collective-permute-start | bytes 61448 | tf_op jit(solution)/shard_map/ppermute | solution.py:24
  15.7 4.1 %collective-permute-start.1 = (bf16[2,1,40,256]{3,2,0,1:T(8,128)(2,1)S(1)}, bf16[2,1,40,256]{3,2,0,1:T(8,128)(2,1)S(1)}, u32[]{:S(2)}, u32[]{:S(2)}) collective-permute-start(bf16[2,1,40,256]{3,2,0,1:T(8,128)(2,1)S(1)} %maximum_select_fusion.12), channel_id=1, source_target_pairs={{0,8},{4,12},{8,0},{12,4},{16,24},{20,28},{24,16},{28,20},{1,9},{5... | collective-permute-start | bytes 122888 | tf_op jit(solution)/shard_map/ppermute | solution.py:24
  19.7 4.5 %collective-permute-start.2 = (bf16[2,2,1,40,256]{4,3,1,0,2:T(8,128)(2,1)S(1)}, bf16[2,2,1,40,256]{4,3,1,0,2:T(8,128)(2,1)S(1)}, u32[]{:S(2)}, u32[]{:S(2)}) collective-permute-start(bf16[2,2,1,40,256]{4,3,1,0,2:T(8,128)(2,1)S(1)} %maximum_select_fusion.10), channel_id=1, source_target_pairs={{0,4},{4,0},{8,12},{12,8},{16,20},{20,16},{24,28},{28,24},{1,5},{5... | collective-permute-start | bytes 245768 | tf_op jit(solution)/shard_map/ppermute | solution.py:24
  24.3 5.4 %collective-permute-start.3 = (bf16[2,2,2,1,40,256]{5,4,2,1,0,3:T(8,128)(2,1)S(1)}, bf16[2,2,2,1,40,256]{5,4,2,1,0,3:T(8,128)(2,1)S(1)}, u32[]{:S(2)}, u32[]{:S(2)}) collective-permute-start(bf16[2,2,2,1,40,256]{5,4,2,1,0,3:T(8,128)(2,1)S(1)} %maximum_select_fusion.8), channel_id=1, source_target_pairs={{0,2},{1,3},{2,0},{3,1},{4,6},{5,7},{6,4},{7,5},{8,10},{9,11},{10,... | collective-permute-start | bytes 491528 | tf_op jit(solution)/shard_map/ppermute | solution.py:24
  29.7 1.7 %collective-permute-start.4 = (bf16[2,2,2,2,1,40,256]{6,5,3,2,1,4,0:T(8,128)(2,1)S(1)}, bf16[2,2,2,2,1,40,256]{6,5,3,2,1,4,0:T(8,128)(2,1)S(1)}, u32[]{:S(2)}, u32[]{:S(2)}) collective-permute-start(bf16[2,2,2,2,1,40,256]{6,5,3,2,1,4,0:T(8,128)(2,1)S(1)} %maximum_select_fusion.4), channel_id=1, source_target_pairs={{0,1},{1,0},{2,3},{3,2},{4,5},{5,4},{6,7},{7,6},{8,9},{9,8},{10,11... | collective-permute-start | bytes 983048 | tf_op jit(solution)/shard_map/ppermute | solution.py:24
  35.8 3.5 %copy-start.3 = (bf16[640,320]{0,1:T(8,128)(2,1)S(1)}, bf16[640,320]{0,1:T(8,128)(2,1)}, u32[]{:S(2)}) copy-start(bf16[640,320]{0,1:T(8,128)(2,1)} %param.4) | copy-start | bytes 1228804
  40.5 1.7 %copy-start.1 = (f32[640,1280]{1,0:T(8,128)}, f32[640,1280]{1,0:T(8,128)S(1)}, u32[]{:S(2)}) copy-start(f32[640,1280]{1,0:T(8,128)S(1)} %maximum_maximum_fusion) | copy-start | bytes 9830404
  42.3 3.7 %collective-permute-start.5 = (f32[320,1280]{1,0:T(8,128)S(1)}, f32[320,1280]{1,0:T(8,128)}, u32[]{:S(2)}, u32[]{:S(2)}) collective-permute-start(f32[320,1280]{1,0:T(8,128)S(1)} %constant_dynamic-slice_fusion.4), channel_id=1, source_target_pairs={{0,1},{1,0},{2,3},{3,2},{4,5},{5,4},{6,7},{7,6},{8,9},{9,8},{10,11... | collective-permute-start | bytes 4915208 | tf_op jit(solution)/shard_map/ppermute | solution.py:24
  48.1 20.6 %collective-permute-start.6 = (f32[160,1280]{1,0:T(8,128)S(1)}, f32[160,1280]{1,0:T(8,128)}, u32[]{:S(2)}, u32[]{:S(2)}) collective-permute-start(f32[160,1280]{1,0:T(8,128)S(1)} %constant_dynamic-slice_fusion.3), channel_id=1, source_target_pairs={{0,2},{1,3},{2,0},{3,1},{4,6},{5,7},{6,4},{7,5},{8,10},{9,11},{10,... | collective-permute-start | bytes 2457608 | tf_op jit(solution)/shard_map/ppermute | solution.py:24
  70.0 10.9 %collective-permute-start.7 = (f32[80,1280]{1,0:T(8,128)S(1)}, f32[80,1280]{1,0:T(8,128)S(1)}, u32[]{:S(2)}, u32[]{:S(2)}) collective-permute-start(f32[80,1280]{1,0:T(8,128)S(1)} %constant_dynamic-slice_fusion.2), channel_id=1, source_target_pairs={{0,4},{4,0},{8,12},{12,8},{16,20},{20,16},{24,28},{28,24},{1,5},{5... | collective-permute-start | bytes 1228808 | tf_op jit(solution)/shard_map/ppermute | solution.py:24
  81.0 5.8 %collective-permute-start.8 = (f32[40,1280]{1,0:T(8,128)S(1)}, f32[40,1280]{1,0:T(8,128)S(1)}, u32[]{:S(2)}, u32[]{:S(2)}) collective-permute-start(f32[40,1280]{1,0:T(8,128)S(1)} %constant_dynamic-slice_fusion.1), channel_id=1, source_target_pairs={{0,8},{4,12},{8,0},{12,4},{16,24},{20,28},{24,16},{28,20},{1,9},{5... | collective-permute-start | bytes 614408 | tf_op jit(solution)/shard_map/ppermute | solution.py:24
  86.9 5.6 %collective-permute-start.9 = (f32[40,640]{1,0:T(8,128)S(1)}, f32[40,640]{1,0:T(8,128)S(1)}, u32[]{:S(2)}, u32[]{:S(2)}) collective-permute-start(f32[40,640]{1,0:T(8,128)S(1)} %constant_dynamic-slice_fusion), channel_id=1, source_target_pairs={{0,16},{4,20},{8,24},{12,28},{16,0},{20,4},{24,8},{28,12},{1,17},{... | collective-permute-start | bytes 307208 | tf_op jit(solution)/shard_map/ppermute | solution.py:24
  92.5 6.0 %collective-permute-start.10 = (f32[40,640]{1,0:T(8,128)S(1)}, f32[40,640]{1,0:T(8,128)S(1)}, u32[]{:S(2)}, u32[]{:S(2)}) collective-permute-start(f32[40,640]{1,0:T(8,128)S(1)} %dynamic-slice_add_fusion.4), channel_id=1, source_target_pairs={{0,16},{4,20},{8,24},{12,28},{16,0},{20,4},{24,8},{28,12},{1,17},{... | collective-permute-start | bytes 307208 | tf_op jit(solution)/shard_map/ppermute | solution.py:24
  98.6 8.8 %collective-permute-start.11 = (f32[40,1280]{1,0:T(8,128)S(1)}, f32[40,1280]{1,0:T(8,128)S(1)}, u32[]{:S(2)}, u32[]{:S(2)}) collective-permute-start(f32[40,1280]{1,0:T(8,128)S(1)} %maximum_select_fusion.7), channel_id=1, source_target_pairs={{0,8},{4,12},{8,0},{12,4},{16,24},{20,28},{24,16},{28,20},{1,9},{5... | collective-permute-start | bytes 614408 | tf_op jit(solution)/shard_map/ppermute | solution.py:24
  107.5 8.0 %collective-permute-start.12 = (f32[80,1280]{1,0:T(8,128)S(1)}, f32[80,1280]{1,0:T(8,128)S(1)}, u32[]{:S(2)}, u32[]{:S(2)}) collective-permute-start(f32[80,1280]{1,0:T(8,128)S(1)} %maximum_select_fusion.3), channel_id=1, source_target_pairs={{0,4},{4,0},{8,12},{12,8},{16,20},{20,16},{24,28},{28,24},{1,5},{5... | collective-permute-start | bytes 1228808 | tf_op jit(solution)/shard_map/ppermute | solution.py:24
  115.6 12.9 %collective-permute-start.13 = (f32[160,1280]{1,0:T(8,128)S(1)}, f32[160,1280]{1,0:T(8,128)S(1)}, u32[]{:S(2)}, u32[]{:S(2)}) collective-permute-start(f32[160,1280]{1,0:T(8,128)S(1)} %maximum_select_fusion.2), channel_id=1, source_target_pairs={{0,2},{1,3},{2,0},{3,1},{4,6},{5,7},{6,4},{7,5},{8,10},{9,11},{10,... | collective-permute-start | bytes 2457608 | tf_op jit(solution)/shard_map/ppermute | solution.py:24
  128.6 3.7 %collective-permute-start.14 = (f32[320,1280]{1,0:T(8,128)S(1)}, f32[320,1280]{1,0:T(8,128)}, u32[]{:S(2)}, u32[]{:S(2)}) collective-permute-start(f32[320,1280]{1,0:T(8,128)S(1)} %maximum_select_fusion.1), channel_id=1, source_target_pairs={{0,1},{1,0},{2,3},{3,2},{4,5},{5,4},{6,7},{7,6},{8,9},{9,8},{10,11... | collective-permute-start | bytes 4915208 | tf_op jit(solution)/shard_map/ppermute | solution.py:24

commit v3 on v2

--- a/solution.py
+++ b/solution.py
@@ -41,10 +41,10 @@
 def halving_plan(shape, steps):
     plan, dims = [], list(shape)
     for _ in steps:
-        if len(dims) == 2 and dims[0] % 16 == 0:
+        if dims[0] % 16 == 0:
             plan.append(0)
             dims[0] //= 2
-        elif len(dims) == 2 and dims[1] % 256 == 0:
+        elif dims[1] % 2 == 0 and dims[1] >= 256:
             plan.append(1)
             dims[1] //= 2
         else:
@@ -52,35 +52,52 @@
     return plan
 
 
-def all_reduce(arrays, mesh, steps):
-    plans = [halving_plan(a.shape, steps) for a in arrays]
-    cur = list(arrays)
-    for k, (ax, mask) in enumerate(steps):
-        bit = my_bit(ax, mask).astype(jnp.int32)
-        keeps, sends = [], []
-        for a, plan in zip(cur, plans):
-            d = plan[k]
+def all_reduce(colors, extra, mesh):
+    plans = [halving_plan(a.shape, st) for a, st in colors]
+    cur = [a for a, _ in colors]
+    for k in range(len(colors[0][1])):
+        sends, keeps = [], []
+        for j, (_, st) in enumerate(colors):
+            ax, mask = st[k]
+            bit = my_bit(ax, mask).astype(jnp.int32)
+            a, d = cur[j], plans[j][k]
             if d is None:
-                keeps.append(a)
-                sends.append(a)
+                keep = send = a
             else:
                 h = a.shape[d] // 2
-                keeps.append(lax.dynamic_slice_in_dim(a, bit * h, h, axis=d))
-                sends.append(lax.dynamic_slice_in_dim(a, (1 - bit) * h, h, axis=d))
-        got = swap(sends, mesh, ax, mask)
-        cur = [kk + g for kk, g in zip(keeps, got)]
-    for k in reversed(range(len(steps))):
-        ax, mask = steps[k]
-        idx = [j for j, plan in enumerate(plans) if plans[j][k] is not None]
-        if not idx:
-            continue
-        got = swap([cur[j] for j in idx], mesh, ax, mask)
-        bit = my_bit(ax, mask)
-        for j, g in zip(idx, got):
+                keep = lax.dynamic_slice_in_dim(a, bit * h, h, axis=d)
+                send = lax.dynamic_slice_in_dim(a, (1 - bit) * h, h, axis=d)
+            if j == 0 and extra.size % send.shape[1] == 0:
+                send = jnp.concatenate([send, extra.reshape(-1, send.shape[1])], axis=0)
+            elif j == 0:
+                extra = extra + swap(extra, mesh, ax, mask)
+            keeps.append(keep)
+            sends.append(send)
+        for j, (_, st) in enumerate(colors):
+            ax, mask = st[k]
+            got = swap(sends[j], mesh, ax, mask)
+            if j == 0 and got.shape[0] > keeps[0].shape[0]:
+                rows = keeps[0].shape[0]
+                extra = extra + got[rows:].reshape(extra.shape)
+                got = got[:rows]
+            cur[j] = keeps[j] + got
+    for k in reversed(range(len(colors[0][1]))):
+        for j, (_, st) in enumerate(colors):
             d = plans[j][k]
+            if d is None:
+                continue
+            ax, mask = st[k]
             c = cur[j]
-            cur[j] = jnp.where(bit, jnp.concatenate([g, c], axis=d), jnp.concatenate([c, g], axis=d))
-    return cur
+            g = swap(c, mesh, ax, mask)
+            cur[j] = jnp.where(my_bit(ax, mask), jnp.concatenate([g, c], axis=d), jnp.concatenate([c, g], axis=d))
+    return cur, extra
+
+
+def color_orders(steps):
+    if len(steps) < 4:
+        return steps, steps
+    middle = steps[1:-1]
+    return steps, [steps[0]] + middle[1:] + middle[:1] + [steps[-1]]
 
 
 def pair_terms(rows_z, row_ids, piece, col_ids):
@@ -134,21 +151,17 @@
         grad_pre = (grad_act * sig * (1.0 + pre * (1.0 - sig))).astype(jnp.bfloat16)
         c_in = feature_map.shape[1]
         if steps:
-            ones = jnp.ones((feature_map.shape[0], 1), feature_map.dtype)
-            head_shift = lax.dot_general(
-                jnp.concatenate([feature_map, ones], axis=1), grad_pre, (((0,), (0,)), ((), ())),
-                preferred_element_type=jnp.float32,
+            grad_proj = lax.dot_general(
+                pooled, grad_rows, (((0,), (0,)), ((), ())), preferred_element_type=jnp.float32
             )
-            proj_t = lax.dot_general(
-                grad_rows, pooled, (((0,), (0,)), ((), ())), preferred_element_type=jnp.float32
+            grad_shift = jnp.sum(grad_pre.astype(jnp.float32), axis=0)
+            grad_head = lax.dot_general(
+                feature_map, grad_pre, (((0,), (0,)), ((), ())), preferred_element_type=jnp.float32
             )
-            used = head_shift.shape[0] + proj_t.shape[0]
-            rows = -(-used // 64) * 64
-            pad = jnp.zeros((rows - used, channels), jnp.float32)
-            (buf,) = all_reduce([jnp.concatenate([head_shift, proj_t, pad], axis=0)], mesh, steps)
-            grad_head = buf[:c_in]
-            grad_shift = buf[c_in]
-            grad_proj = buf[c_in + 1 : used].T
+            first, second = color_orders(steps)
+            (grad_head, grad_proj), grad_shift = all_reduce(
+                [(grad_head, first), (grad_proj, second)], grad_shift, mesh
+            )
         else:
             grad_proj = lax.dot_general(
                 pooled, grad_rows, (((0,), (0,)), ((), ())), preferred_element_type=jnp.float32

time: 140 us -> 117 us (0.84)
  waiting for transfers between devices: 76.8 us -> 50.2 us
  starting transfers between devices: 29.8 us -> 34.9 us
  local copies, waits for them, and re-layouts: 6.59 us -> 4.29 us
  other arithmetic: 12.5 us -> 13.9 us
    ppermute x15 -> x25, waiting for transfers between devices: 76.8 us -> 50.2 us  [swap(): return lax.ppermute(x, ax, [(i, i ^ mask) for i in range(mesh.shape[ax])])]
    ppermute x15 -> x25, starting transfers between devices: 29.8 us -> 34.9 us  [swap(): return lax.ppermute(x, ax, [(i, i ^ mask) for i in range(mesh.shape[ax])])]
    convert_element_type x1 -> x0, other arithmetic: 3.08 us -> none  [body(): grad_pre = (grad_act * sig * (1.0 + pre * (1.0 - sig))).astype(jnp.bfloat16)]
    slice x2 -> x3, local copies, waits for them, and re-layouts: 1.89 us -> 0.03 us  [all_reduce(): extra = extra + got[rows:].reshape(extra.shape)]
    unnamed x9 -> x12, local copies, waits for them, and re-layouts: 4.28 us -> 2.54 us
    select_n x5 -> x10, other arithmetic: 2.58 us -> 4.09 us  [all_reduce(): jnp.where(my_bit(ax, mask), jnp.concatenate([g, c], axis=d), jnp.concaten...]
    add x5 -> x13, other arithmetic: 3.42 us -> 3.54 us  [the longest x10 2.92 us: all_reduce(): cur[j] = keeps[j] + got]
  transfers between devices with their start and end apart: 15 -> 25, of which waited for: 15 -> 18; matrix products, arithmetic and copies ran while one was open for 0% -> 9% of each run, Pallas kernels for 0% -> 0%
where the time goes in v3:
time: 117 us
  waiting for transfers between devices  50.2 us (43%)
  starting transfers between devices  34.9 us (30%)
  other arithmetic  13.9 us (12%)
  matrix products  10.1 us (9%)
  local copies, waits for them, and re-layouts  4.29 us (4%)
  between operations  3.57 us (3%)
    ppermute x25, waiting for transfers between devices, swap(): return lax.ppermute(x, ax, [(i, i ^ mask) for i in range(mesh.shape[ax])])  50.2 us
    ppermute x25, starting transfers between devices, swap(): return lax.ppermute(x, ax, [(i, i ^ mask) for i in range(mesh.shape[ax])])  34.9 us
    dot_general x1, matrix products, body(): jnp.dot(feature_map, head_weight, preferred_element_type=jnp.float32)  5.03 us
    select_n x10, other arithmetic, all_reduce(): jnp.where(my_bit(ax, mask), jnp.concatenate([g, c], axis=d), jnp.concaten...  4.09 us
    add x10, other arithmetic, all_reduce(): cur[j] = keeps[j] + got  2.92 us
    unnamed x12, local copies, waits for them, and re-layouts  2.54 us
    reduce_sum x1, other arithmetic, body(): jnp.mean(act.reshape(images, POS, channels), axis=1).astype(jnp.bfloat16)  2.51 us
    dot_general x1, matrix products, pair_terms(): lax.dot_general(rows_z, piece, (((1,), (1,)), ((), ())), preferred_elemen...  2.5 us
  transfers between devices with their start and end apart: 25, of which 18 were waited for; matrix products, arithmetic and copies ran while one was open for 9% of the time, Pallas kernels for 0%

profile of v3, /device:TPU:0, one launch (start us, length us, event | category | flops | bytes accessed | tf_op | source)
XLA Modules:
  0.0 117.0 jit_solution(221591400105982945)
XLA Ops:
  1.8 5.0 %fusion.5 = (f32[640,1280]{1,0:T(8,128)}, f32[640,1280]{1,0:T(8,128)}) fusion(f32[1280]{0:T(1024)} %param.6, bf16[640,320]{0,1:T(8,128)(2,1)} %param.4, bf16[320,1280]{1,0:T(8,128)(2,1)S(1)} %copy-done), kind=kOutput, calls=%fused_computation.11 | convolution fusion | flops 528384000 | bytes 7787520 | tf_op jit(solution)/shard_map/dot_general | solution.py:118
  6.8 2.5 %reduce_sum.49 = f32[40,1280]{1,0:T(8,128)S(1)} reduce(f32[40,16,1280]{2,1,0:T(8,128)} %bitcast.69, f32[]{:T(128)} %constant.52.clone.1), dimensions={1}, to_apply=%region_0.1 | reduce | flops 768000 | bytes 3481604 | tf_op jit(solution)/shard_map/reduce_sum | solution.py:120
  9.8 4.1 %collective-permute-start = (bf16[1,40,256]{2,1,0:T(8,128)(2,1)S(1)}, bf16[1,40,256]{2,1,0:T(8,128)(2,1)S(1)}, u32[]{:S(2)}, u32[]{:S(2)}) collective-permute-start(bf16[1,40,256]{2,1,0:T(8,128)(2,1)S(1)} %fusion.51), channel_id=1, source_target_pairs={{0,16},{4,20},{8,24},{12,28},{16,0},{20,4},{24,8},{28,12},{1,17},{... | collective-permute-start | bytes 61448 | tf_op jit(solution)/shard_map/ppermute | solution.py:24
  14.1 1.6 %collective-permute-done = bf16[1,40,256]{2,1,0:T(8,128)(2,1)S(1)} collective-permute-done((bf16[1,40,256]{2,1,0:T(8,128)(2,1)S(1)}, bf16[1,40,256]{2,1,0:T(8,128)(2,1)S(1)}, u32[]{:S(2)}, u32[]{:S(2)}) %collective-permute-start) | collective-permute-done | bytes 20512 | tf_op jit(solution)/shard_map/ppermute | solution.py:24
  15.7 2.0 %collective-permute-start.1 = (bf16[2,1,40,256]{3,2,0,1:T(8,128)(2,1)S(1)}, bf16[2,1,40,256]{3,2,0,1:T(8,128)(2,1)S(1)}, u32[]{:S(2)}, u32[]{:S(2)}) collective-permute-start(bf16[2,1,40,256]{3,2,0,1:T(8,128)(2,1)S(1)} %maximum_select_fusion.17), channel_id=1, source_target_pairs={{0,8},{4,12},{8,0},{12,4},{16,24},{20,28},{24,16},{28,20},{1,9},{5... | collective-permute-start | bytes 122888 | tf_op jit(solution)/shard_map/ppermute | solution.py:24
  17.7 2.1 %collective-permute-done.1 = bf16[2,1,40,256]{3,2,0,1:T(8,128)(2,1)S(1)} collective-permute-done((bf16[2,1,40,256]{3,2,0,1:T(8,128)(2,1)S(1)}, bf16[2,1,40,256]{3,2,0,1:T(8,128)(2,1)S(1)}, u32[]{:S(2)}, u32[]{:S(2)}) %collective-permute-start.1) | collective-permute-done | bytes 40992 | tf_op jit(solution)/shard_map/ppermute | solution.py:24
  19.8 2.0 %collective-permute-start.2 = (bf16[2,2,1,40,256]{4,3,1,0,2:T(8,128)(2,1)S(1)}, bf16[2,2,1,40,256]{4,3,1,0,2:T(8,128)(2,1)S(1)}, u32[]{:S(2)}, u32[]{:S(2)}) collective-permute-start(bf16[2,2,1,40,256]{4,3,1,0,2:T(8,128)(2,1)S(1)} %maximum_select_fusion.14), channel_id=1, source_target_pairs={{0,4},{4,0},{8,12},{12,8},{16,20},{20,16},{24,28},{28,24},{1,5},{5... | collective-permute-start | bytes 245768 | tf_op jit(solution)/shard_map/ppermute | solution.py:24
  21.8 2.5 %collective-permute-done.2 = bf16[2,2,1,40,256]{4,3,1,0,2:T(8,128)(2,1)S(1)} collective-permute-done((bf16[2,2,1,40,256]{4,3,1,0,2:T(8,128)(2,1)S(1)}, bf16[2,2,1,40,256]{4,3,1,0,2:T(8,128)(2,1)S(1)}, u32[]{:S(2)}, u32[]{:S(2)}) %collective-permute-start.2) | collective-permute-done | bytes 81952 | tf_op jit(solution)/shard_map/ppermute | solution.py:24
  24.3 2.0 %collective-permute-start.3 = (bf16[2,2,2,1,40,256]{5,4,2,1,0,3:T(8,128)(2,1)S(1)}, bf16[2,2,2,1,40,256]{5,4,2,1,0,3:T(8,128)(2,1)S(1)}, u32[]{:S(2)}, u32[]{:S(2)}) collective-permute-start(bf16[2,2,2,1,40,256]{5,4,2,1,0,3:T(8,128)(2,1)S(1)} %maximum_select_fusion.10), channel_id=1, source_target_pairs={{0,2},{1,3},{2,0},{3,1},{4,6},{5,7},{6,4},{7,5},{8,10},{9,11},{10,... | collective-permute-start | bytes 491528 | tf_op jit(solution)/shard_map/ppermute | solution.py:24
  26.3 3.4 %collective-permute-done.3 = bf16[2,2,2,1,40,256]{5,4,2,1,0,3:T(8,128)(2,1)S(1)} collective-permute-done((bf16[2,2,2,1,40,256]{5,4,2,1,0,3:T(8,128)(2,1)S(1)}, bf16[2,2,2,1,40,256]{5,4,2,1,0,3:T(8,128)(2,1)S(1)}, u32[]{:S(2)}, u32[]{:S(2)}) %collective-permute-start.3) | collective-permute-done | bytes 163872 | tf_op jit(solution)/shard_map/ppermute | solution.py:24
  32.4 2.5 %fusion.10 = f32[]{:T(128)} fusion(bf16[1280,256]{1,0:T(8,128)(2,1)S(1)} %bitcast.74), kind=kOutput, calls=%fused_computation.19 | convolution fusion | flops 847052800 | bytes 655364 | tf_op jit(solution)/shard_map/dot_general | solution.py:104
  43.2 2.0 %collective-permute-start.16 = (f32[320,256]{1,0:T(8,128)S(1)}, f32[320,256]{1,0:T(8,128)S(1)}, u32[]{:S(2)}, u32[]{:S(2)}) collective-permute-start(f32[320,256]{1,0:T(8,128)S(1)} %constant_dynamic-slice_fusion.3), channel_id=1, source_target_pairs={{0,4},{4,0},{8,12},{12,8},{16,20},{20,16},{24,28},{28,24},{1,5},{5... | collective-permute-start | bytes 983048 | tf_op jit(solution)/shard_map/ppermute | solution.py:24
  47.5 5.9 %collective-permute-done.16 = f32[320,256]{1,0:T(8,128)S(1)} collective-permute-done((f32[320,256]{1,0:T(8,128)S(1)}, f32[320,256]{1,0:T(8,128)S(1)}, u32[]{:S(2)}, u32[]{:S(2)}) %collective-permute-start.16) | collective-permute-done | bytes 327712 | tf_op jit(solution)/shard_map/ppermute | solution.py:24
  53.5 1.8 %collective-permute-start.17 = (f32[160,256]{1,0:T(8,128)S(1)}, f32[160,256]{1,0:T(8,128)S(1)}, u32[]{:S(2)}, u32[]{:S(2)}) collective-permute-start(f32[160,256]{1,0:T(8,128)S(1)} %constant_dynamic-slice_fusion.2), channel_id=1, source_target_pairs={{0,8},{4,12},{8,0},{12,4},{16,24},{20,28},{24,16},{28,20},{1,9},{5... | collective-permute-start | bytes 491528 | tf_op jit(solution)/shard_map/ppermute | solution.py:24
  57.0 2.3 %collective-permute-done.17 = f32[160,256]{1,0:T(8,128)S(1)} collective-permute-done((f32[160,256]{1,0:T(8,128)S(1)}, f32[160,256]{1,0:T(8,128)S(1)}, u32[]{:S(2)}, u32[]{:S(2)}) %collective-permute-start.17) | collective-permute-done | bytes 163872 | tf_op jit(solution)/shard_map/ppermute | solution.py:24
  59.4 1.6 %collective-permute-start.18 = (f32[80,256]{1,0:T(8,128)S(1)}, f32[80,256]{1,0:T(8,128)S(1)}, u32[]{:S(2)}, u32[]{:S(2)}) collective-permute-start(f32[80,256]{1,0:T(8,128)S(1)} %constant_dynamic-slice_fusion.1), channel_id=1, source_target_pairs={{0,2},{1,3},{2,0},{3,1},{4,6},{5,7},{6,4},{7,5},{8,10},{9,11},{10,... | collective-permute-start | bytes 245768 | tf_op jit(solution)/shard_map/ppermute | solution.py:24
  61.0 6.7 %collective-permute-done.6 = f32[81,1280]{1,0:T(8,128)S(1)} collective-permute-done((f32[81,1280]{1,0:T(8,128)S(1)}, f32[81,1280]{1,0:T(8,128)S(1)}, u32[]{:S(2)}, u32[]{:S(2)}) %collective-permute-start.6) | collective-permute-done | bytes 414752 | tf_op jit(solution)/shard_map/ppermute | solution.py:24
  69.5 4.6 %collective-permute-done.7 = f32[41,1280]{1,0:T(8,128)S(1)} collective-permute-done((f32[41,1280]{1,0:T(8,128)S(1)}, f32[41,1280]{1,0:T(8,128)S(1)}, u32[]{:S(2)}, u32[]{:S(2)}) %collective-permute-start.7) | collective-permute-done | bytes 209952 | tf_op jit(solution)/shard_map/ppermute | solution.py:24
  74.9 2.5 %collective-permute-start.19 = (f32[40,256]{1,0:T(8,128)S(1)}, f32[40,256]{1,0:T(8,128)S(1)}, u32[]{:S(2)}, u32[]{:S(2)}) collective-permute-start(f32[40,256]{1,0:T(8,128)S(1)} %constant_dynamic-slice_fusion), channel_id=1, source_target_pairs={{0,16},{4,20},{8,24},{12,28},{16,0},{20,4},{24,8},{28,12},{1,17},{... | collective-permute-start | bytes 122888 | tf_op jit(solution)/shard_map/ppermute | solution.py:24
  77.5 2.9 %collective-permute-done.8 = f32[42,640]{1,0:T(8,128)S(1)} collective-permute-done((f32[42,640]{1,0:T(8,128)S(1)}, f32[42,640]{1,0:T(8,128)S(1)}, u32[]{:S(2)}, u32[]{:S(2)}) %collective-permute-start.8) | collective-permute-done | bytes 107552 | tf_op jit(solution)/shard_map/ppermute | solution.py:24
  80.7 2.0 %collective-permute-start.9 = (f32[44,320]{1,0:T(8,128)S(1)}, f32[44,320]{1,0:T(8,128)S(1)}, u32[]{:S(2)}, u32[]{:S(2)}) collective-permute-start(f32[44,320]{1,0:T(8,128)S(1)} %pad_maximum_fusion.8), channel_id=1, source_target_pairs={{0,16},{4,20},{8,24},{12,28},{16,0},{20,4},{24,8},{28,12},{1,17},{... | collective-permute-start | bytes 168968 | tf_op jit(solution)/shard_map/ppermute | solution.py:24
  83.7 2.4 %collective-permute-done.9 = f32[44,320]{1,0:T(8,128)S(1)} collective-permute-done((f32[44,320]{1,0:T(8,128)S(1)}, f32[44,320]{1,0:T(8,128)S(1)}, u32[]{:S(2)}, u32[]{:S(2)}) %collective-permute-start.9) | collective-permute-done | bytes 56352 | tf_op jit(solution)/shard_map/ppermute | solution.py:24
  86.3 1.8 %collective-permute-start.10 = (f32[40,320]{1,0:T(8,128)S(1)}, f32[40,320]{1,0:T(8,128)S(1)}, u32[]{:S(2)}, u32[]{:S(2)}) collective-permute-start(f32[40,320]{1,0:T(8,128)S(1)} %slice_add_fusion.4), channel_id=1, source_target_pairs={{0,16},{4,20},{8,24},{12,28},{16,0},{20,4},{24,8},{28,12},{1,17},{... | collective-permute-start | bytes 153608 | tf_op jit(solution)/shard_map/ppermute | solution.py:24
  89.7 2.1 %collective-permute-done.10 = f32[40,320]{1,0:T(8,128)S(1)} collective-permute-done((f32[40,320]{1,0:T(8,128)S(1)}, f32[40,320]{1,0:T(8,128)S(1)}, u32[]{:S(2)}, u32[]{:S(2)}) %collective-permute-start.10) | collective-permute-done | bytes 51232 | tf_op jit(solution)/shard_map/ppermute | solution.py:24
  94.0 2.5 %collective-permute-done.11 = f32[40,640]{1,0:T(8,128)S(1)} collective-permute-done((f32[40,640]{1,0:T(8,128)S(1)}, f32[40,640]{1,0:T(8,128)S(1)}, u32[]{:S(2)}, u32[]{:S(2)}) %collective-permute-start.11) | collective-permute-done | bytes 102432 | tf_op jit(solution)/shard_map/ppermute | solution.py:24
  96.6 1.6 %collective-permute-start.12 = (f32[40,1280]{1,0:T(8,128)S(1)}, f32[40,1280]{1,0:T(8,128)S(1)}, u32[]{:S(2)}, u32[]{:S(2)}) collective-permute-start(f32[40,1280]{1,0:T(8,128)S(1)} %maximum_select_fusion.9), channel_id=1, source_target_pairs={{0,4},{4,0},{8,12},{12,8},{16,20},{20,16},{24,28},{28,24},{1,5},{5... | collective-permute-start | bytes 614408 | tf_op jit(solution)/shard_map/ppermute | solution.py:24
  98.4 1.6 %collective-permute-start.23 = (f32[320,256]{1,0:T(8,128)S(1)}, f32[320,256]{1,0:T(8,128)S(1)}, u32[]{:S(2)}, u32[]{:S(2)}) collective-permute-start(f32[320,256]{1,0:T(8,128)S(1)} %maximum_select_fusion.8), channel_id=1, source_target_pairs={{0,4},{4,0},{8,12},{12,8},{16,20},{20,16},{24,28},{28,24},{1,5},{5... | collective-permute-start | bytes 983048 | tf_op jit(solution)/shard_map/ppermute | solution.py:24
  100.0 2.4 %collective-permute-done.12 = f32[40,1280]{1,0:T(8,128)S(1)} collective-permute-done((f32[40,1280]{1,0:T(8,128)S(1)}, f32[40,1280]{1,0:T(8,128)S(1)}, u32[]{:S(2)}, u32[]{:S(2)}) %collective-permute-start.12) | collective-permute-done | bytes 204832 | tf_op jit(solution)/shard_map/ppermute | solution.py:24
  102.5 1.6 %collective-permute-start.13 = (f32[80,1280]{1,0:T(8,128)S(1)}, f32[80,1280]{1,0:T(8,128)S(1)}, u32[]{:S(2)}, u32[]{:S(2)}) collective-permute-start(f32[80,1280]{1,0:T(8,128)S(1)} %maximum_select_fusion.4), channel_id=1, source_target_pairs={{0,2},{1,3},{2,0},{3,1},{4,6},{5,7},{6,4},{7,5},{8,10},{9,11},{10,... | collective-permute-start | bytes 1228808 | tf_op jit(solution)/shard_map/ppermute | solution.py:24
  104.1 1.9 %collective-permute-done.23 = f32[320,256]{1,0:T(8,128)S(1)} collective-permute-done((f32[320,256]{1,0:T(8,128)S(1)}, f32[320,256]{1,0:T(8,128)S(1)}, u32[]{:S(2)}, u32[]{:S(2)}) %collective-permute-start.23) | collective-permute-done | bytes 327712 | tf_op jit(solution)/shard_map/ppermute | solution.py:24
  106.1 4.4 %collective-permute-done.13 = f32[80,1280]{1,0:T(8,128)S(1)} collective-permute-done((f32[80,1280]{1,0:T(8,128)S(1)}, f32[80,1280]{1,0:T(8,128)S(1)}, u32[]{:S(2)}, u32[]{:S(2)}) %collective-permute-start.13) | collective-permute-done | bytes 409632 | tf_op jit(solution)/shard_map/ppermute | solution.py:24
  112.0 2.5 %maximum_select_fusion.1 = f32[1280,256]{1,0:T(8,128)} fusion(f32[640,256]{1,0:T(8,128)S(1)} %maximum_select_fusion.3, f32[640,256]{1,0:T(8,128)} %collective-permute-done.24, pred[]{:T(512)S(6)} %ne.10), kind=kLoop, calls=%fused_computation.20 | loop fusion | flops 983040 | bytes 2621441 | tf_op jit(solution)/shard_map/jit(_where)/select_n | solution.py:92
  (109 shorter events, 26.4 us)
Async XLA Ops:
  0.6 1.2 copy-start
  6.8 2.5 %copy-start.2 = (bf16[1280,256]{1,0:T(8,128)(2,1)S(1)}, bf16[1280,256]{1,0:T(8,128)(2,1)}, u32[]{:S(2)}) copy-start(bf16[1280,256]{1,0:T(8,128)(2,1)} %param.7) | copy-start | bytes 1966084
  9.8 5.9 %collective-permute-start = (bf16[1,40,256]{2,1,0:T(8,128)(2,1)S(1)}, bf16[1,40,256]{2,1,0:T(8,128)(2,1)S(1)}, u32[]{:S(2)}, u32[]{:S(2)}) collective-permute-start(bf16[1,40,256]{2,1,0:T(8,128)(2,1)S(1)} %fusion.51), channel_id=1, source_target_pairs={{0,16},{4,20},{8,24},{12,28},{16,0},{20,4},{24,8},{28,12},{1,17},{... | collective-permute-start | bytes 61448 | tf_op jit(solution)/shard_map/ppermute | solution.py:24
  15.7 4.1 %collective-permute-start.1 = (bf16[2,1,40,256]{3,2,0,1:T(8,128)(2,1)S(1)}, bf16[2,1,40,256]{3,2,0,1:T(8,128)(2,1)S(1)}, u32[]{:S(2)}, u32[]{:S(2)}) collective-permute-start(bf16[2,1,40,256]{3,2,0,1:T(8,128)(2,1)S(1)} %maximum_select_fusion.17), channel_id=1, source_target_pairs={{0,8},{4,12},{8,0},{12,4},{16,24},{20,28},{24,16},{28,20},{1,9},{5... | collective-permute-start | bytes 122888 | tf_op jit(solution)/shard_map/ppermute | solution.py:24
  19.8 4.5 %collective-permute-start.2 = (bf16[2,2,1,40,256]{4,3,1,0,2:T(8,128)(2,1)S(1)}, bf16[2,2,1,40,256]{4,3,1,0,2:T(8,128)(2,1)S(1)}, u32[]{:S(2)}, u32[]{:S(2)}) collective-permute-start(bf16[2,2,1,40,256]{4,3,1,0,2:T(8,128)(2,1)S(1)} %maximum_select_fusion.14), channel_id=1, source_target_pairs={{0,4},{4,0},{8,12},{12,8},{16,20},{20,16},{24,28},{28,24},{1,5},{5... | collective-permute-start | bytes 245768 | tf_op jit(solution)/shard_map/ppermute | solution.py:24
  24.3 5.4 %collective-permute-start.3 = (bf16[2,2,2,1,40,256]{5,4,2,1,0,3:T(8,128)(2,1)S(1)}, bf16[2,2,2,1,40,256]{5,4,2,1,0,3:T(8,128)(2,1)S(1)}, u32[]{:S(2)}, u32[]{:S(2)}) collective-permute-start(bf16[2,2,2,1,40,256]{5,4,2,1,0,3:T(8,128)(2,1)S(1)} %maximum_select_fusion.10), channel_id=1, source_target_pairs={{0,2},{1,3},{2,0},{3,1},{4,6},{5,7},{6,4},{7,5},{8,10},{9,11},{10,... | collective-permute-start | bytes 491528 | tf_op jit(solution)/shard_map/ppermute | solution.py:24
  29.7 1.7 %collective-permute-start.4 = (bf16[2,2,2,2,1,40,256]{6,5,3,2,1,4,0:T(8,128)(2,1)S(1)}, bf16[2,2,2,2,1,40,256]{6,5,3,2,1,4,0:T(8,128)(2,1)S(1)}, u32[]{:S(2)}, u32[]{:S(2)}) collective-permute-start(bf16[2,2,2,2,1,40,256]{6,5,3,2,1,4,0:T(8,128)(2,1)S(1)} %maximum_select_fusion.5), channel_id=1, source_target_pairs={{0,1},{1,0},{2,3},{3,2},{4,5},{5,4},{6,7},{7,6},{8,9},{9,8},{10,11... | collective-permute-start | bytes 983048 | tf_op jit(solution)/shard_map/ppermute | solution.py:24
  32.4 3.2 %copy-start.4 = (bf16[2,2,2,2,2,1,40,256]{7,6,4,3,2,5,1,0:T(8,128)(2,1)S(1)}, bf16[2,2,2,2,2,1,40,256]{7,6,4,3,2,5,1,0:T(8,128)(2,1)}, u32[]{:S(2)}) copy-start(bf16[2,2,2,2,2,1,40,256]{7,6,4,3,2,5,1,0:T(8,128)(2,1)} %get-tuple-element.10) | copy-start | bytes 1966084
  36.3 2.2 %copy-start.1 = (f32[640,1280]{1,0:T(8,128)S(1)}, f32[640,1280]{1,0:T(8,128)}, u32[]{:S(2)}) copy-start(f32[640,1280]{1,0:T(8,128)} %get-tuple-element.20) | copy-start | bytes 9830404
  37.1 2.8 %copy-start.5 = (bf16[640,320]{0,1:T(8,128)(2,1)S(1)}, bf16[640,320]{0,1:T(8,128)(2,1)}, u32[]{:S(2)}) copy-start(bf16[640,320]{0,1:T(8,128)(2,1)} %param.4) | copy-start | bytes 1228804
  38.0 4.0 %collective-permute-start.15 = (f32[640,256]{1,0:T(8,128)}, f32[640,256]{1,0:T(8,128)}, u32[]{:S(2)}, u32[]{:S(2)}) collective-permute-start(f32[640,256]{1,0:T(8,128)} %constant_dynamic-slice_fusion.4), channel_id=1, source_target_pairs={{0,1},{1,0},{2,3},{3,2},{4,5},{5,4},{6,7},{7,6},{8,9},{9,8},{10,11... | collective-permute-start | bytes 1966088 | tf_op jit(solution)/shard_map/ppermute | solution.py:24
  40.6 1.2 copy-start.3
  41.8 3.4 %collective-permute-start.5 = (f32[161,1280]{1,0:T(8,128)S(1)}, f32[161,1280]{1,0:T(8,128)}, u32[]{:S(2)}, u32[]{:S(2)}) collective-permute-start(f32[161,1280]{1,0:T(8,128)S(1)} %pad_maximum_fusion), channel_id=1, source_target_pairs={{0,1},{1,0},{2,3},{3,2},{4,5},{5,4},{6,7},{7,6},{8,9},{9,8},{10,11... | collective-permute-start | bytes 2472968 | tf_op jit(solution)/shard_map/ppermute | solution.py:24
  43.2 10.2 %collective-permute-start.16 = (f32[320,256]{1,0:T(8,128)S(1)}, f32[320,256]{1,0:T(8,128)S(1)}, u32[]{:S(2)}, u32[]{:S(2)}) collective-permute-start(f32[320,256]{1,0:T(8,128)S(1)} %constant_dynamic-slice_fusion.3), channel_id=1, source_target_pairs={{0,4},{4,0},{8,12},{12,8},{16,20},{20,16},{24,28},{28,24},{1,5},{5... | collective-permute-start | bytes 983048 | tf_op jit(solution)/shard_map/ppermute | solution.py:24
  53.5 5.9 %collective-permute-start.17 = (f32[160,256]{1,0:T(8,128)S(1)}, f32[160,256]{1,0:T(8,128)S(1)}, u32[]{:S(2)}, u32[]{:S(2)}) collective-permute-start(f32[160,256]{1,0:T(8,128)S(1)} %constant_dynamic-slice_fusion.2), channel_id=1, source_target_pairs={{0,8},{4,12},{8,0},{12,4},{16,24},{20,28},{24,16},{28,20},{1,9},{5... | collective-permute-start | bytes 491528 | tf_op jit(solution)/shard_map/ppermute | solution.py:24
  55.3 12.4 %collective-permute-start.6 = (f32[81,1280]{1,0:T(8,128)S(1)}, f32[81,1280]{1,0:T(8,128)S(1)}, u32[]{:S(2)}, u32[]{:S(2)}) collective-permute-start(f32[81,1280]{1,0:T(8,128)S(1)} %pad_maximum_fusion.5), channel_id=1, source_target_pairs={{0,2},{1,3},{2,0},{3,1},{4,6},{5,7},{6,4},{7,5},{8,10},{9,11},{10,... | collective-permute-start | bytes 1244168 | tf_op jit(solution)/shard_map/ppermute | solution.py:24
  59.4 10.0 %collective-permute-start.18 = (f32[80,256]{1,0:T(8,128)S(1)}, f32[80,256]{1,0:T(8,128)S(1)}, u32[]{:S(2)}, u32[]{:S(2)}) collective-permute-start(f32[80,256]{1,0:T(8,128)S(1)} %constant_dynamic-slice_fusion.1), channel_id=1, source_target_pairs={{0,2},{1,3},{2,0},{3,1},{4,6},{5,7},{6,4},{7,5},{8,10},{9,11},{10,... | collective-permute-start | bytes 245768 | tf_op jit(solution)/shard_map/ppermute | solution.py:24
  67.9 6.3 %collective-permute-start.7 = (f32[41,1280]{1,0:T(8,128)S(1)}, f32[41,1280]{1,0:T(8,128)S(1)}, u32[]{:S(2)}, u32[]{:S(2)}) collective-permute-start(f32[41,1280]{1,0:T(8,128)S(1)} %pad_maximum_fusion.6), channel_id=1, source_target_pairs={{0,4},{4,0},{8,12},{12,8},{16,20},{20,16},{24,28},{28,24},{1,5},{5... | collective-permute-start | bytes 629768 | tf_op jit(solution)/shard_map/ppermute | solution.py:24
  74.3 6.2 %collective-permute-start.8 = (f32[42,640]{1,0:T(8,128)S(1)}, f32[42,640]{1,0:T(8,128)S(1)}, u32[]{:S(2)}, u32[]{:S(2)}) collective-permute-start(f32[42,640]{1,0:T(8,128)S(1)} %pad_maximum_fusion.7), channel_id=1, source_target_pairs={{0,8},{4,12},{8,0},{12,4},{16,24},{20,28},{24,16},{28,20},{1,9},{5... | collective-permute-start | bytes 322568 | tf_op jit(solution)/shard_map/ppermute | solution.py:24
  74.9 7.8 %collective-permute-start.19 = (f32[40,256]{1,0:T(8,128)S(1)}, f32[40,256]{1,0:T(8,128)S(1)}, u32[]{:S(2)}, u32[]{:S(2)}) collective-permute-start(f32[40,256]{1,0:T(8,128)S(1)} %constant_dynamic-slice_fusion), channel_id=1, source_target_pairs={{0,16},{4,20},{8,24},{12,28},{16,0},{20,4},{24,8},{28,12},{1,17},{... | collective-permute-start | bytes 122888 | tf_op jit(solution)/shard_map/ppermute | solution.py:24
  80.7 5.5 %collective-permute-start.9 = (f32[44,320]{1,0:T(8,128)S(1)}, f32[44,320]{1,0:T(8,128)S(1)}, u32[]{:S(2)}, u32[]{:S(2)}) collective-permute-start(f32[44,320]{1,0:T(8,128)S(1)} %pad_maximum_fusion.8), channel_id=1, source_target_pairs={{0,16},{4,20},{8,24},{12,28},{16,0},{20,4},{24,8},{28,12},{1,17},{... | collective-permute-start | bytes 168968 | tf_op jit(solution)/shard_map/ppermute | solution.py:24
  82.7 5.5 %collective-permute-start.20 = (f32[40,256]{1,0:T(8,128)S(1)}, f32[40,256]{1,0:T(8,128)S(1)}, u32[]{:S(2)}, u32[]{:S(2)}) collective-permute-start(f32[40,256]{1,0:T(8,128)S(1)} %dynamic-slice_add_fusion.4), channel_id=1, source_target_pairs={{0,16},{4,20},{8,24},{12,28},{16,0},{20,4},{24,8},{28,12},{1,17},{... | collective-permute-start | bytes 122888 | tf_op jit(solution)/shard_map/ppermute | solution.py:24
  86.3 5.5 %collective-permute-start.10 = (f32[40,320]{1,0:T(8,128)S(1)}, f32[40,320]{1,0:T(8,128)S(1)}, u32[]{:S(2)}, u32[]{:S(2)}) collective-permute-start(f32[40,320]{1,0:T(8,128)S(1)} %slice_add_fusion.4), channel_id=1, source_target_pairs={{0,16},{4,20},{8,24},{12,28},{16,0},{20,4},{24,8},{28,12},{1,17},{... | collective-permute-start | bytes 153608 | tf_op jit(solution)/shard_map/ppermute | solution.py:24
  88.1 4.5 %collective-permute-start.21 = (f32[80,256]{1,0:T(8,128)S(1)}, f32[80,256]{1,0:T(8,128)S(1)}, u32[]{:S(2)}, u32[]{:S(2)}) collective-permute-start(f32[80,256]{1,0:T(8,128)S(1)} %maximum_select_fusion.16), channel_id=1, source_target_pairs={{0,2},{1,3},{2,0},{3,1},{4,6},{5,7},{6,4},{7,5},{8,10},{9,11},{10,... | collective-permute-start | bytes 245768 | tf_op jit(solution)/shard_map/ppermute | solution.py:24
  91.9 4.7 %collective-permute-start.11 = (f32[40,640]{1,0:T(8,128)S(1)}, f32[40,640]{1,0:T(8,128)S(1)}, u32[]{:S(2)}, u32[]{:S(2)}) collective-permute-start(f32[40,640]{1,0:T(8,128)S(1)} %maximum_select_fusion.13), channel_id=1, source_target_pairs={{0,8},{4,12},{8,0},{12,4},{16,24},{20,28},{24,16},{28,20},{1,9},{5... | collective-permute-start | bytes 307208 | tf_op jit(solution)/shard_map/ppermute | solution.py:24
  92.7 5.7 %collective-permute-start.22 = (f32[160,256]{1,0:T(8,128)S(1)}, f32[160,256]{1,0:T(8,128)S(1)}, u32[]{:S(2)}, u32[]{:S(2)}) collective-permute-start(f32[160,256]{1,0:T(8,128)S(1)} %maximum_select_fusion.12), channel_id=1, source_target_pairs={{0,8},{4,12},{8,0},{12,4},{16,24},{20,28},{24,16},{28,20},{1,9},{5... | collective-permute-start | bytes 491528 | tf_op jit(solution)/shard_map/ppermute | solution.py:24
  96.6 5.8 %collective-permute-start.12 = (f32[40,1280]{1,0:T(8,128)S(1)}, f32[40,1280]{1,0:T(8,128)S(1)}, u32[]{:S(2)}, u32[]{:S(2)}) collective-permute-start(f32[40,1280]{1,0:T(8,128)S(1)} %maximum_select_fusion.9), channel_id=1, source_target_pairs={{0,4},{4,0},{8,12},{12,8},{16,20},{20,16},{24,28},{28,24},{1,5},{5... | collective-permute-start | bytes 614408 | tf_op jit(solution)/shard_map/ppermute | solution.py:24
  98.4 7.6 %collective-permute-start.23 = (f32[320,256]{1,0:T(8,128)S(1)}, f32[320,256]{1,0:T(8,128)S(1)}, u32[]{:S(2)}, u32[]{:S(2)}) collective-permute-start(f32[320,256]{1,0:T(8,128)S(1)} %maximum_select_fusion.8), channel_id=1, source_target_pairs={{0,4},{4,0},{8,12},{12,8},{16,20},{20,16},{24,28},{28,24},{1,5},{5... | collective-permute-start | bytes 983048 | tf_op jit(solution)/shard_map/ppermute | solution.py:24
  102.5 8.0 %collective-permute-start.13 = (f32[80,1280]{1,0:T(8,128)S(1)}, f32[80,1280]{1,0:T(8,128)S(1)}, u32[]{:S(2)}, u32[]{:S(2)}) collective-permute-start(f32[80,1280]{1,0:T(8,128)S(1)} %maximum_select_fusion.4), channel_id=1, source_target_pairs={{0,2},{1,3},{2,0},{3,1},{4,6},{5,7},{6,4},{7,5},{8,10},{9,11},{10,... | collective-permute-start | bytes 1228808 | tf_op jit(solution)/shard_map/ppermute | solution.py:24
  106.0 6.0 %collective-permute-start.24 = (f32[640,256]{1,0:T(8,128)S(1)}, f32[640,256]{1,0:T(8,128)}, u32[]{:S(2)}, u32[]{:S(2)}) collective-permute-start(f32[640,256]{1,0:T(8,128)S(1)} %maximum_select_fusion.3), channel_id=1, source_target_pairs={{0,1},{1,0},{2,3},{3,2},{4,5},{5,4},{6,7},{7,6},{8,9},{9,8},{10,11... | collective-permute-start | bytes 1966088 | tf_op jit(solution)/shard_map/ppermute | solution.py:24
  110.6 4.0 %collective-permute-start.14 = (f32[160,1280]{1,0:T(8,128)S(1)}, f32[160,1280]{1,0:T(8,128)S(1)}, u32[]{:S(2)}, u32[]{:S(2)}) collective-permute-start(f32[160,1280]{1,0:T(8,128)S(1)} %maximum_select_fusion.2), channel_id=1, source_target_pairs={{0,1},{1,0},{2,3},{3,2},{4,5},{5,4},{6,7},{7,6},{8,9},{9,8},{10,11... | collective-permute-start | bytes 2457608 | tf_op jit(solution)/shard_map/ppermute | solution.py:24

commit v4 on v2

--- a/solution.py
+++ b/solution.py
@@ -41,10 +41,10 @@
 def halving_plan(shape, steps):
     plan, dims = [], list(shape)
     for _ in steps:
-        if len(dims) == 2 and dims[0] % 16 == 0:
+        if dims[0] % 16 == 0:
             plan.append(0)
             dims[0] //= 2
-        elif len(dims) == 2 and dims[1] % 256 == 0:
+        elif dims[1] % 2 == 0 and dims[1] >= 256:
             plan.append(1)
             dims[1] //= 2
         else:
@@ -52,34 +52,45 @@
     return plan
 
 
-def all_reduce(arrays, mesh, steps):
-    plans = [halving_plan(a.shape, steps) for a in arrays]
-    cur = list(arrays)
-    for k, (ax, mask) in enumerate(steps):
-        bit = my_bit(ax, mask).astype(jnp.int32)
-        keeps, sends = [], []
-        for a, plan in zip(cur, plans):
-            d = plan[k]
-            if d is None:
-                keeps.append(a)
-                sends.append(a)
-            else:
-                h = a.shape[d] // 2
-                keeps.append(lax.dynamic_slice_in_dim(a, bit * h, h, axis=d))
-                sends.append(lax.dynamic_slice_in_dim(a, (1 - bit) * h, h, axis=d))
-        got = swap(sends, mesh, ax, mask)
-        cur = [kk + g for kk, g in zip(keeps, got)]
+def combined_masks(steps, dp_size):
+    masks = [mask if ax == "dp" else mask * dp_size for ax, mask in steps]
+    if len(masks) < 4:
+        return masks, masks
+    middle = masks[1:-1]
+    return masks, [masks[0]] + middle[1:] + middle[:1] + [masks[-1]]
+
+
+def packed_all_reduce(buf, mesh, steps):
+    axes = ("blk", "dp")
+    n = mesh.shape["blk"] * mesh.shape["dp"]
+    first, second = combined_masks(steps, mesh.shape["dp"])
+    me = lax.axis_index(axes)
+    group = (me & first[0]) != 0
+    plan = halving_plan(buf.shape, steps)
+
+    def partner_perm(k):
+        return [(i, i ^ (second[k] if i & first[0] else first[k])) for i in range(n)]
+
+    def bit_of(k):
+        return (me & jnp.where(group, second[k], first[k])) != 0
+
+    cur = buf
+    for k in range(len(steps)):
+        d = plan[k]
+        bit = bit_of(k).astype(jnp.int32)
+        if d is None:
+            keep = send = cur
+        else:
+            h = cur.shape[d] // 2
+            keep = lax.dynamic_slice_in_dim(cur, bit * h, h, axis=d)
+            send = lax.dynamic_slice_in_dim(cur, (1 - bit) * h, h, axis=d)
+        cur = keep + lax.ppermute(send, axes, partner_perm(k))
     for k in reversed(range(len(steps))):
-        ax, mask = steps[k]
-        idx = [j for j, plan in enumerate(plans) if plans[j][k] is not None]
-        if not idx:
+        d = plan[k]
+        if d is None:
             continue
-        got = swap([cur[j] for j in idx], mesh, ax, mask)
-        bit = my_bit(ax, mask)
-        for j, g in zip(idx, got):
-            d = plans[j][k]
-            c = cur[j]
-            cur[j] = jnp.where(bit, jnp.concatenate([g, c], axis=d), jnp.concatenate([c, g], axis=d))
+        g = lax.ppermute(cur, axes, partner_perm(k))
+        cur = jnp.where(bit_of(k), jnp.concatenate([g, cur], axis=d), jnp.concatenate([cur, g], axis=d))
     return cur
 
 
@@ -134,21 +145,22 @@
         grad_pre = (grad_act * sig * (1.0 + pre * (1.0 - sig))).astype(jnp.bfloat16)
         c_in = feature_map.shape[1]
         if steps:
-            ones = jnp.ones((feature_map.shape[0], 1), feature_map.dtype)
-            head_shift = lax.dot_general(
-                jnp.concatenate([feature_map, ones], axis=1), grad_pre, (((0,), (0,)), ((), ())),
-                preferred_element_type=jnp.float32,
+            grad_shift = jnp.sum(grad_pre.astype(jnp.float32), axis=0)
+            grad_head = lax.dot_general(
+                feature_map, grad_pre, (((0,), (0,)), ((), ())), preferred_element_type=jnp.float32
             )
             proj_t = lax.dot_general(
                 grad_rows, pooled, (((0,), (0,)), ((), ())), preferred_element_type=jnp.float32
             )
-            used = head_shift.shape[0] + proj_t.shape[0]
+            used = c_in + proj_t.shape[0] + 1
             rows = -(-used // 64) * 64
-            pad = jnp.zeros((rows - used, channels), jnp.float32)
-            (buf,) = all_reduce([jnp.concatenate([head_shift, proj_t, pad], axis=0)], mesh, steps)
-            grad_head = buf[:c_in]
-            grad_shift = buf[c_in]
-            grad_proj = buf[c_in + 1 : used].T
+            packed = jnp.concatenate(
+                [grad_head, proj_t, grad_shift[None], jnp.zeros((rows - used, channels), jnp.float32)], axis=0
+            )
+            packed = packed_all_reduce(packed, mesh, steps)
+            grad_head = packed[:c_in]
+            grad_proj = packed[c_in : used - 1].T
+            grad_shift = packed[used - 1]
         else:
             grad_proj = lax.dot_general(
                 pooled, grad_rows, (((0,), (0,)), ((), ())), preferred_element_type=jnp.float32

time: 140 us -> 134 us (0.957)
  waiting for transfers between devices: 76.8 us -> 70.7 us
    ppermute x15 -> x5, waiting for transfers between devices: 76.8 us -> 11 us  [swap(): return lax.ppermute(x, ax, [(i, i ^ mask) for i in range(mesh.shape[ax])])]
    ppermute x0 -> x10, waiting for transfers between devices: none -> 59.7 us  [the longest x5 33.2 us: packed_all_reduce(): g = lax.ppermute(cur, axes, partner_perm(k))]
    ppermute x0 -> x10, starting transfers between devices: none -> 20.1 us  [the longest x5 10.9 us: packed_all_reduce(): g = lax.ppermute(cur, axes, partner_perm(k))]
    ppermute x15 -> x5, starting transfers between devices: 29.8 us -> 10.1 us  [swap(): return lax.ppermute(x, ax, [(i, i ^ mask) for i in range(mesh.shape[ax])])]
    reduce_sum x0 -> x1, other arithmetic: none -> 3.19 us  [body(): grad_shift = jnp.sum(grad_pre.astype(jnp.float32), axis=0)]
    convert_element_type x1 -> x0, other arithmetic: 3.08 us -> none  [body(): grad_pre = (grad_act * sig * (1.0 + pre * (1.0 - sig))).astype(jnp.bfloat16)]
where the time goes in v4:
time: 134 us
  waiting for transfers between devices  70.7 us (53%)
  starting transfers between devices  30.3 us (23%)
  other arithmetic  12.6 us (9%)
  matrix products  10.1 us (8%)
  local copies, waits for them, and re-layouts  6.6 us (5%)
  between operations  3.4 us (3%)
    ppermute x5, waiting for transfers between devices, packed_all_reduce(): g = lax.ppermute(cur, axes, partner_perm(k))  33.2 us
    ppermute x5, waiting for transfers between devices, packed_all_reduce(): cur = keep + lax.ppermute(send, axes, partner_perm(k))  26.5 us
    ppermute x5, waiting for transfers between devices, swap(): return lax.ppermute(x, ax, [(i, i ^ mask) for i in range(mesh.shape[ax])])  11 us
    ppermute x5, starting transfers between devices, packed_all_reduce(): g = lax.ppermute(cur, axes, partner_perm(k))  10.9 us
    ppermute x5, starting transfers between devices, swap(): return lax.ppermute(x, ax, [(i, i ^ mask) for i in range(mesh.shape[ax])])  10.1 us
    ppermute x5, starting transfers between devices, packed_all_reduce(): cur = keep + lax.ppermute(send, axes, partner_perm(k))  9.19 us
    dot_general x1, matrix products, body(): jnp.dot(feature_map, head_weight, preferred_element_type=jnp.float32)  4.99 us
    unnamed x9, local copies, waits for them, and re-layouts  4.29 us
  transfers between devices with their start and end apart: 15, of which 15 were waited for; matrix products, arithmetic and copies ran while one was open for 0% of the time, Pallas kernels for 0%

profile of v4, /device:TPU:0, one launch (start us, length us, event | category | flops | bytes accessed | tf_op | source)
XLA Modules:
  0.0 133.6 jit_solution(734733465641683275)
XLA Ops:
  1.8 5.0 %fusion.5 = (f32[640,1280]{1,0:T(8,128)}, f32[640,1280]{1,0:T(8,128)}) fusion(f32[1280]{0:T(1024)} %param.6, bf16[640,320]{0,1:T(8,128)(2,1)} %param.4, bf16[320,1280]{1,0:T(8,128)(2,1)S(1)} %copy-done), kind=kOutput, calls=%fused_computation.13 | convolution fusion | flops 528384000 | bytes 7787520 | tf_op jit(solution)/shard_map/dot_general | solution.py:112
  6.8 2.5 %reduce_sum.45 = f32[40,1280]{1,0:T(8,128)S(1)} reduce(f32[40,16,1280]{2,1,0:T(8,128)} %bitcast.69, f32[]{:T(128)} %constant.24.clone.1), dimensions={1}, to_apply=%region_0.1 | reduce | flops 768000 | bytes 3481604 | tf_op jit(solution)/shard_map/reduce_sum | solution.py:114
  9.8 4.1 %collective-permute-start = (bf16[1,40,256]{2,1,0:T(8,128)(2,1)S(1)}, bf16[1,40,256]{2,1,0:T(8,128)(2,1)S(1)}, u32[]{:S(2)}, u32[]{:S(2)}) collective-permute-start(bf16[1,40,256]{2,1,0:T(8,128)(2,1)S(1)} %fusion.50), channel_id=1, source_target_pairs={{0,16},{4,20},{8,24},{12,28},{16,0},{20,4},{24,8},{28,12},{1,17},{... | collective-permute-start | bytes 61448 | tf_op jit(solution)/shard_map/ppermute | solution.py:24
  14.1 1.6 %collective-permute-done = bf16[1,40,256]{2,1,0:T(8,128)(2,1)S(1)} collective-permute-done((bf16[1,40,256]{2,1,0:T(8,128)(2,1)S(1)}, bf16[1,40,256]{2,1,0:T(8,128)(2,1)S(1)}, u32[]{:S(2)}, u32[]{:S(2)}) %collective-permute-start) | collective-permute-done | bytes 20512 | tf_op jit(solution)/shard_map/ppermute | solution.py:24
  15.7 2.0 %collective-permute-start.1 = (bf16[2,1,40,256]{3,2,0,1:T(8,128)(2,1)S(1)}, bf16[2,1,40,256]{3,2,0,1:T(8,128)(2,1)S(1)}, u32[]{:S(2)}, u32[]{:S(2)}) collective-permute-start(bf16[2,1,40,256]{3,2,0,1:T(8,128)(2,1)S(1)} %maximum_select_fusion.12), channel_id=1, source_target_pairs={{0,8},{4,12},{8,0},{12,4},{16,24},{20,28},{24,16},{28,20},{1,9},{5... | collective-permute-start | bytes 122888 | tf_op jit(solution)/shard_map/ppermute | solution.py:24
  17.6 2.1 %collective-permute-done.1 = bf16[2,1,40,256]{3,2,0,1:T(8,128)(2,1)S(1)} collective-permute-done((bf16[2,1,40,256]{3,2,0,1:T(8,128)(2,1)S(1)}, bf16[2,1,40,256]{3,2,0,1:T(8,128)(2,1)S(1)}, u32[]{:S(2)}, u32[]{:S(2)}) %collective-permute-start.1) | collective-permute-done | bytes 40992 | tf_op jit(solution)/shard_map/ppermute | solution.py:24
  19.8 2.0 %collective-permute-start.2 = (bf16[2,2,1,40,256]{4,3,1,0,2:T(8,128)(2,1)S(1)}, bf16[2,2,1,40,256]{4,3,1,0,2:T(8,128)(2,1)S(1)}, u32[]{:S(2)}, u32[]{:S(2)}) collective-permute-start(bf16[2,2,1,40,256]{4,3,1,0,2:T(8,128)(2,1)S(1)} %maximum_select_fusion.10), channel_id=1, source_target_pairs={{0,4},{4,0},{8,12},{12,8},{16,20},{20,16},{24,28},{28,24},{1,5},{5... | collective-permute-start | bytes 245768 | tf_op jit(solution)/shard_map/ppermute | solution.py:24
  21.8 2.5 %collective-permute-done.2 = bf16[2,2,1,40,256]{4,3,1,0,2:T(8,128)(2,1)S(1)} collective-permute-done((bf16[2,2,1,40,256]{4,3,1,0,2:T(8,128)(2,1)S(1)}, bf16[2,2,1,40,256]{4,3,1,0,2:T(8,128)(2,1)S(1)}, u32[]{:S(2)}, u32[]{:S(2)}) %collective-permute-start.2) | collective-permute-done | bytes 81952 | tf_op jit(solution)/shard_map/ppermute | solution.py:24
  24.3 2.0 %collective-permute-start.3 = (bf16[2,2,2,1,40,256]{5,4,2,1,0,3:T(8,128)(2,1)S(1)}, bf16[2,2,2,1,40,256]{5,4,2,1,0,3:T(8,128)(2,1)S(1)}, u32[]{:S(2)}, u32[]{:S(2)}) collective-permute-start(bf16[2,2,2,1,40,256]{5,4,2,1,0,3:T(8,128)(2,1)S(1)} %maximum_select_fusion.8), channel_id=1, source_target_pairs={{0,2},{1,3},{2,0},{3,1},{4,6},{5,7},{6,4},{7,5},{8,10},{9,11},{10,... | collective-permute-start | bytes 491528 | tf_op jit(solution)/shard_map/ppermute | solution.py:24
  26.4 3.3 %collective-permute-done.3 = bf16[2,2,2,1,40,256]{5,4,2,1,0,3:T(8,128)(2,1)S(1)} collective-permute-done((bf16[2,2,2,1,40,256]{5,4,2,1,0,3:T(8,128)(2,1)S(1)}, bf16[2,2,2,1,40,256]{5,4,2,1,0,3:T(8,128)(2,1)S(1)}, u32[]{:S(2)}, u32[]{:S(2)}) %collective-permute-start.3) | collective-permute-done | bytes 163872 | tf_op jit(solution)/shard_map/ppermute | solution.py:24
  31.6 2.5 %fusion.10 = f32[]{:T(128)} fusion(bf16[1280,256]{1,0:T(8,128)(2,1)S(1)} %bitcast.74), kind=kOutput, calls=%fused_computation.23 | convolution fusion | flops 847052800 | bytes 655364 | tf_op jit(solution)/shard_map/dot_general | solution.py:98
  36.2 3.2 %convert_reduce_fusion = (f32[1280]{0:T(1024)S(1)}, bf16[640,1280]{1,0:T(8,128)(2,1)S(1)}) fusion(f32[640,1280]{1,0:T(8,128)} %get-tuple-element.20, f32[40,1280]{1,0:T(8,128)S(1)} %convolution_multiply_fusion), kind=kLoop, calls=%fused_computation.11 | loop fusion | flops 9009920 | bytes 5125120 | tf_op jit(solution)/shard_map/reduce_sum | solution.py:148
  40.6 1.7 %copy-done.1 = f32[640,1280]{1,0:T(8,128)} copy-done((f32[640,1280]{1,0:T(8,128)}, f32[640,1280]{1,0:T(8,128)S(1)}, u32[]{:S(2)}) %copy-start.1) | copy-done | bytes 3276824
  42.6 3.5 %collective-permute-done.5 = f32[320,1280]{1,0:T(8,128)} collective-permute-done((f32[320,1280]{1,0:T(8,128)S(1)}, f32[320,1280]{1,0:T(8,128)}, u32[]{:S(2)}, u32[]{:S(2)}) %collective-permute-start.5) | collective-permute-done | bytes 1638432 | tf_op jit(solution)/shard_map/ppermute | solution.py:87
  46.0 2.1 %dynamic-slice_add_fusion = f32[320,1280]{1,0:T(8,128)S(1)} fusion(f32[320,1280]{1,0:T(8,128)} %collective-permute-done.5, f32[640,1280]{1,0:T(8,128)} %copy-done.1, s32[]{:T(128)S(6)} %mul.97), kind=kLoop, calls=%fused_computation.22 | loop fusion | flops 409600 | bytes 4915204 | tf_op jit(solution)/shard_map/add | solution.py:87
  48.2 2.0 %collective-permute-start.6 = (f32[160,1280]{1,0:T(8,128)S(1)}, f32[160,1280]{1,0:T(8,128)}, u32[]{:S(2)}, u32[]{:S(2)}) collective-permute-start(f32[160,1280]{1,0:T(8,128)S(1)} %constant_dynamic-slice_fusion.3), channel_id=1, source_target_pairs={{0,2},{1,5},{2,0},{3,7},{4,6},{5,1},{6,4},{7,3},{8,10},{9,13},{10,... | collective-permute-start | bytes 2457608 | tf_op jit(solution)/shard_map/ppermute | solution.py:87
  50.2 10.5 %collective-permute-done.6 = f32[160,1280]{1,0:T(8,128)} collective-permute-done((f32[160,1280]{1,0:T(8,128)S(1)}, f32[160,1280]{1,0:T(8,128)}, u32[]{:S(2)}, u32[]{:S(2)}) %collective-permute-start.6) | collective-permute-done | bytes 819232 | tf_op jit(solution)/shard_map/ppermute | solution.py:87
  62.0 2.0 %collective-permute-start.7 = (f32[80,1280]{1,0:T(8,128)S(1)}, f32[80,1280]{1,0:T(8,128)S(1)}, u32[]{:S(2)}, u32[]{:S(2)}) collective-permute-start(f32[80,1280]{1,0:T(8,128)S(1)} %constant_dynamic-slice_fusion.2), channel_id=1, source_target_pairs={{0,4},{1,9},{2,6},{3,11},{4,0},{5,13},{6,2},{7,15},{8,12},{9,1},{1... | collective-permute-start | bytes 1228808 | tf_op jit(solution)/shard_map/ppermute | solution.py:87
  64.0 6.0 %collective-permute-done.7 = f32[80,1280]{1,0:T(8,128)S(1)} collective-permute-done((f32[80,1280]{1,0:T(8,128)S(1)}, f32[80,1280]{1,0:T(8,128)S(1)}, u32[]{:S(2)}, u32[]{:S(2)}) %collective-permute-start.7) | collective-permute-done | bytes 409632 | tf_op jit(solution)/shard_map/ppermute | solution.py:87
  70.1 2.0 %collective-permute-start.8 = (f32[40,1280]{1,0:T(8,128)S(1)}, f32[40,1280]{1,0:T(8,128)S(1)}, u32[]{:S(2)}, u32[]{:S(2)}) collective-permute-start(f32[40,1280]{1,0:T(8,128)S(1)} %constant_dynamic-slice_fusion.1), channel_id=1, source_target_pairs={{0,8},{1,3},{2,10},{3,1},{4,12},{5,7},{6,14},{7,5},{8,0},{9,11},{1... | collective-permute-start | bytes 614408 | tf_op jit(solution)/shard_map/ppermute | solution.py:87
  72.1 3.9 %collective-permute-done.8 = f32[40,1280]{1,0:T(8,128)S(1)} collective-permute-done((f32[40,1280]{1,0:T(8,128)S(1)}, f32[40,1280]{1,0:T(8,128)S(1)}, u32[]{:S(2)}, u32[]{:S(2)}) %collective-permute-start.8) | collective-permute-done | bytes 204832 | tf_op jit(solution)/shard_map/ppermute | solution.py:87
  76.0 3.0 %collective-permute-start.9 = (f32[40,640]{1,0:T(8,128)S(1)}, f32[40,640]{1,0:T(8,128)S(1)}, u32[]{:S(2)}, u32[]{:S(2)}) collective-permute-start(f32[40,640]{1,0:T(8,128)S(1)} %constant_dynamic-slice_fusion), channel_id=1, source_target_pairs={{0,16},{1,17},{2,18},{3,19},{4,20},{5,21},{6,22},{7,23},{8,24},{9,... | collective-permute-start | bytes 307208 | tf_op jit(solution)/shard_map/ppermute | solution.py:87
  79.0 2.6 %collective-permute-done.9 = f32[40,640]{1,0:T(8,128)S(1)} collective-permute-done((f32[40,640]{1,0:T(8,128)S(1)}, f32[40,640]{1,0:T(8,128)S(1)}, u32[]{:S(2)}, u32[]{:S(2)}) %collective-permute-start.9) | collective-permute-done | bytes 102432 | tf_op jit(solution)/shard_map/ppermute | solution.py:87
  81.7 3.4 %collective-permute-start.10 = (f32[40,640]{1,0:T(8,128)S(1)}, f32[40,640]{1,0:T(8,128)S(1)}, u32[]{:S(2)}, u32[]{:S(2)}) collective-permute-start(f32[40,640]{1,0:T(8,128)S(1)} %dynamic-slice_add_fusion.4), channel_id=1, source_target_pairs={{0,16},{1,17},{2,18},{3,19},{4,20},{5,21},{6,22},{7,23},{8,24},{9,... | collective-permute-start | bytes 307208 | tf_op jit(solution)/shard_map/ppermute | solution.py:92
  85.0 2.6 %collective-permute-done.10 = f32[40,640]{1,0:T(8,128)S(1)} collective-permute-done((f32[40,640]{1,0:T(8,128)S(1)}, f32[40,640]{1,0:T(8,128)S(1)}, u32[]{:S(2)}, u32[]{:S(2)}) %collective-permute-start.10) | collective-permute-done | bytes 102432 | tf_op jit(solution)/shard_map/ppermute | solution.py:92
  87.7 4.4 %collective-permute-start.11 = (f32[40,1280]{1,0:T(8,128)S(1)}, f32[40,1280]{1,0:T(8,128)S(1)}, u32[]{:S(2)}, u32[]{:S(2)}) collective-permute-start(f32[40,1280]{1,0:T(8,128)S(1)} %maximum_select_fusion.7), channel_id=1, source_target_pairs={{0,8},{1,3},{2,10},{3,1},{4,12},{5,7},{6,14},{7,5},{8,0},{9,11},{1... | collective-permute-start | bytes 614408 | tf_op jit(solution)/shard_map/ppermute | solution.py:92
  92.1 5.9 %collective-permute-done.11 = f32[40,1280]{1,0:T(8,128)S(1)} collective-permute-done((f32[40,1280]{1,0:T(8,128)S(1)}, f32[40,1280]{1,0:T(8,128)S(1)}, u32[]{:S(2)}, u32[]{:S(2)}) %collective-permute-start.11) | collective-permute-done | bytes 204832 | tf_op jit(solution)/shard_map/ppermute | solution.py:92
  98.0 1.6 %collective-permute-start.12 = (f32[80,1280]{1,0:T(8,128)S(1)}, f32[80,1280]{1,0:T(8,128)S(1)}, u32[]{:S(2)}, u32[]{:S(2)}) collective-permute-start(f32[80,1280]{1,0:T(8,128)S(1)} %maximum_select_fusion.3), channel_id=1, source_target_pairs={{0,4},{1,9},{2,6},{3,11},{4,0},{5,13},{6,2},{7,15},{8,12},{9,1},{1... | collective-permute-start | bytes 1228808 | tf_op jit(solution)/shard_map/ppermute | solution.py:92
  99.6 10.8 %collective-permute-done.12 = f32[80,1280]{1,0:T(8,128)S(1)} collective-permute-done((f32[80,1280]{1,0:T(8,128)S(1)}, f32[80,1280]{1,0:T(8,128)S(1)}, u32[]{:S(2)}, u32[]{:S(2)}) %collective-permute-start.12) | collective-permute-done | bytes 409632 | tf_op jit(solution)/shard_map/ppermute | solution.py:92
  112.1 10.8 %collective-permute-done.13 = f32[160,1280]{1,0:T(8,128)S(1)} collective-permute-done((f32[160,1280]{1,0:T(8,128)S(1)}, f32[160,1280]{1,0:T(8,128)S(1)}, u32[]{:S(2)}, u32[]{:S(2)}) %collective-permute-start.13) | collective-permute-done | bytes 819232 | tf_op jit(solution)/shard_map/ppermute | solution.py:92
  123.8 2.9 %collective-permute-done.14 = f32[320,1280]{1,0:T(8,128)} collective-permute-done((f32[320,1280]{1,0:T(8,128)S(1)}, f32[320,1280]{1,0:T(8,128)}, u32[]{:S(2)}, u32[]{:S(2)}) %collective-permute-start.14) | collective-permute-done | bytes 1638432 | tf_op jit(solution)/shard_map/ppermute | solution.py:92
  126.7 2.3 %maximum_select_fusion = f32[640,1280]{1,0:T(8,128)S(1)} fusion(f32[320,1280]{1,0:T(8,128)S(1)} %maximum_select_fusion.1, f32[320,1280]{1,0:T(8,128)} %collective-permute-done.14, pred[]{:T(512)S(6)} %ne.46), kind=kLoop, calls=%fused_computation.7 | loop fusion | flops 2457600 | bytes 6553601 | tf_op jit(solution)/shard_map/jit(_where)/select_n | solution.py:93
  (53 shorter events, 13.4 us)
Async XLA Ops:
  0.6 1.2 copy-start
  6.8 2.5 %copy-start.2 = (bf16[1280,256]{1,0:T(8,128)(2,1)S(1)}, bf16[1280,256]{1,0:T(8,128)(2,1)}, u32[]{:S(2)}) copy-start(bf16[1280,256]{1,0:T(8,128)(2,1)} %param.7) | copy-start | bytes 1966084
  9.8 5.9 %collective-permute-start = (bf16[1,40,256]{2,1,0:T(8,128)(2,1)S(1)}, bf16[1,40,256]{2,1,0:T(8,128)(2,1)S(1)}, u32[]{:S(2)}, u32[]{:S(2)}) collective-permute-start(bf16[1,40,256]{2,1,0:T(8,128)(2,1)S(1)} %fusion.50), channel_id=1, source_target_pairs={{0,16},{4,20},{8,24},{12,28},{16,0},{20,4},{24,8},{28,12},{1,17},{... | collective-permute-start | bytes 61448 | tf_op jit(solution)/shard_map/ppermute | solution.py:24
  15.7 4.1 %collective-permute-start.1 = (bf16[2,1,40,256]{3,2,0,1:T(8,128)(2,1)S(1)}, bf16[2,1,40,256]{3,2,0,1:T(8,128)(2,1)S(1)}, u32[]{:S(2)}, u32[]{:S(2)}) collective-permute-start(bf16[2,1,40,256]{3,2,0,1:T(8,128)(2,1)S(1)} %maximum_select_fusion.12), channel_id=1, source_target_pairs={{0,8},{4,12},{8,0},{12,4},{16,24},{20,28},{24,16},{28,20},{1,9},{5... | collective-permute-start | bytes 122888 | tf_op jit(solution)/shard_map/ppermute | solution.py:24
  19.8 4.5 %collective-permute-start.2 = (bf16[2,2,1,40,256]{4,3,1,0,2:T(8,128)(2,1)S(1)}, bf16[2,2,1,40,256]{4,3,1,0,2:T(8,128)(2,1)S(1)}, u32[]{:S(2)}, u32[]{:S(2)}) collective-permute-start(bf16[2,2,1,40,256]{4,3,1,0,2:T(8,128)(2,1)S(1)} %maximum_select_fusion.10), channel_id=1, source_target_pairs={{0,4},{4,0},{8,12},{12,8},{16,20},{20,16},{24,28},{28,24},{1,5},{5... | collective-permute-start | bytes 245768 | tf_op jit(solution)/shard_map/ppermute | solution.py:24
  24.3 5.4 %collective-permute-start.3 = (bf16[2,2,2,1,40,256]{5,4,2,1,0,3:T(8,128)(2,1)S(1)}, bf16[2,2,2,1,40,256]{5,4,2,1,0,3:T(8,128)(2,1)S(1)}, u32[]{:S(2)}, u32[]{:S(2)}) collective-permute-start(bf16[2,2,2,1,40,256]{5,4,2,1,0,3:T(8,128)(2,1)S(1)} %maximum_select_fusion.8), channel_id=1, source_target_pairs={{0,2},{1,3},{2,0},{3,1},{4,6},{5,7},{6,4},{7,5},{8,10},{9,11},{10,... | collective-permute-start | bytes 491528 | tf_op jit(solution)/shard_map/ppermute | solution.py:24
  29.7 1.7 %collective-permute-start.4 = (bf16[2,2,2,2,1,40,256]{6,5,3,2,1,4,0:T(8,128)(2,1)S(1)}, bf16[2,2,2,2,1,40,256]{6,5,3,2,1,4,0:T(8,128)(2,1)S(1)}, u32[]{:S(2)}, u32[]{:S(2)}) collective-permute-start(bf16[2,2,2,2,1,40,256]{6,5,3,2,1,4,0:T(8,128)(2,1)S(1)} %maximum_select_fusion.4), channel_id=1, source_target_pairs={{0,1},{1,0},{2,3},{3,2},{4,5},{5,4},{6,7},{7,6},{8,9},{9,8},{10,11... | collective-permute-start | bytes 983048 | tf_op jit(solution)/shard_map/ppermute | solution.py:24
  35.8 3.6 %copy-start.3 = (bf16[640,320]{0,1:T(8,128)(2,1)S(1)}, bf16[640,320]{0,1:T(8,128)(2,1)}, u32[]{:S(2)}) copy-start(bf16[640,320]{0,1:T(8,128)(2,1)} %param.4) | copy-start | bytes 1228804
  40.5 1.7 %copy-start.1 = (f32[640,1280]{1,0:T(8,128)}, f32[640,1280]{1,0:T(8,128)S(1)}, u32[]{:S(2)}) copy-start(f32[640,1280]{1,0:T(8,128)S(1)} %maximum_maximum_fusion) | copy-start | bytes 9830404
  42.3 3.7 %collective-permute-start.5 = (f32[320,1280]{1,0:T(8,128)S(1)}, f32[320,1280]{1,0:T(8,128)}, u32[]{:S(2)}, u32[]{:S(2)}) collective-permute-start(f32[320,1280]{1,0:T(8,128)S(1)} %constant_dynamic-slice_fusion.4), channel_id=1, source_target_pairs={{0,1},{1,0},{2,3},{3,2},{4,5},{5,4},{6,7},{7,6},{8,9},{9,8},{10,11... | collective-permute-start | bytes 4915208 | tf_op jit(solution)/shard_map/ppermute | solution.py:87
  48.2 12.5 %collective-permute-start.6 = (f32[160,1280]{1,0:T(8,128)S(1)}, f32[160,1280]{1,0:T(8,128)}, u32[]{:S(2)}, u32[]{:S(2)}) collective-permute-start(f32[160,1280]{1,0:T(8,128)S(1)} %constant_dynamic-slice_fusion.3), channel_id=1, source_target_pairs={{0,2},{1,5},{2,0},{3,7},{4,6},{5,1},{6,4},{7,3},{8,10},{9,13},{10,... | collective-permute-start | bytes 2457608 | tf_op jit(solution)/shard_map/ppermute | solution.py:87
  62.0 8.0 %collective-permute-start.7 = (f32[80,1280]{1,0:T(8,128)S(1)}, f32[80,1280]{1,0:T(8,128)S(1)}, u32[]{:S(2)}, u32[]{:S(2)}) collective-permute-start(f32[80,1280]{1,0:T(8,128)S(1)} %constant_dynamic-slice_fusion.2), channel_id=1, source_target_pairs={{0,4},{1,9},{2,6},{3,11},{4,0},{5,13},{6,2},{7,15},{8,12},{9,1},{1... | collective-permute-start | bytes 1228808 | tf_op jit(solution)/shard_map/ppermute | solution.py:87
  70.1 5.8 %collective-permute-start.8 = (f32[40,1280]{1,0:T(8,128)S(1)}, f32[40,1280]{1,0:T(8,128)S(1)}, u32[]{:S(2)}, u32[]{:S(2)}) collective-permute-start(f32[40,1280]{1,0:T(8,128)S(1)} %constant_dynamic-slice_fusion.1), channel_id=1, source_target_pairs={{0,8},{1,3},{2,10},{3,1},{4,12},{5,7},{6,14},{7,5},{8,0},{9,11},{1... | collective-permute-start | bytes 614408 | tf_op jit(solution)/shard_map/ppermute | solution.py:87
  76.0 5.7 %collective-permute-start.9 = (f32[40,640]{1,0:T(8,128)S(1)}, f32[40,640]{1,0:T(8,128)S(1)}, u32[]{:S(2)}, u32[]{:S(2)}) collective-permute-start(f32[40,640]{1,0:T(8,128)S(1)} %constant_dynamic-slice_fusion), channel_id=1, source_target_pairs={{0,16},{1,17},{2,18},{3,19},{4,20},{5,21},{6,22},{7,23},{8,24},{9,... | collective-permute-start | bytes 307208 | tf_op jit(solution)/shard_map/ppermute | solution.py:87
  81.7 6.0 %collective-permute-start.10 = (f32[40,640]{1,0:T(8,128)S(1)}, f32[40,640]{1,0:T(8,128)S(1)}, u32[]{:S(2)}, u32[]{:S(2)}) collective-permute-start(f32[40,640]{1,0:T(8,128)S(1)} %dynamic-slice_add_fusion.4), channel_id=1, source_target_pairs={{0,16},{1,17},{2,18},{3,19},{4,20},{5,21},{6,22},{7,23},{8,24},{9,... | collective-permute-start | bytes 307208 | tf_op jit(solution)/shard_map/ppermute | solution.py:92
  87.7 10.3 %collective-permute-start.11 = (f32[40,1280]{1,0:T(8,128)S(1)}, f32[40,1280]{1,0:T(8,128)S(1)}, u32[]{:S(2)}, u32[]{:S(2)}) collective-permute-start(f32[40,1280]{1,0:T(8,128)S(1)} %maximum_select_fusion.7), channel_id=1, source_target_pairs={{0,8},{1,3},{2,10},{3,1},{4,12},{5,7},{6,14},{7,5},{8,0},{9,11},{1... | collective-permute-start | bytes 614408 | tf_op jit(solution)/shard_map/ppermute | solution.py:92
  98.0 12.4 %collective-permute-start.12 = (f32[80,1280]{1,0:T(8,128)S(1)}, f32[80,1280]{1,0:T(8,128)S(1)}, u32[]{:S(2)}, u32[]{:S(2)}) collective-permute-start(f32[80,1280]{1,0:T(8,128)S(1)} %maximum_select_fusion.3), channel_id=1, source_target_pairs={{0,4},{1,9},{2,6},{3,11},{4,0},{5,13},{6,2},{7,15},{8,12},{9,1},{1... | collective-permute-start | bytes 1228808 | tf_op jit(solution)/shard_map/ppermute | solution.py:92
  110.5 12.4 %collective-permute-start.13 = (f32[160,1280]{1,0:T(8,128)S(1)}, f32[160,1280]{1,0:T(8,128)S(1)}, u32[]{:S(2)}, u32[]{:S(2)}) collective-permute-start(f32[160,1280]{1,0:T(8,128)S(1)} %maximum_select_fusion.2), channel_id=1, source_target_pairs={{0,2},{1,5},{2,0},{3,7},{4,6},{5,1},{6,4},{7,3},{8,10},{9,13},{10,... | collective-permute-start | bytes 2457608 | tf_op jit(solution)/shard_map/ppermute | solution.py:92
  123.0 3.7 %collective-permute-start.14 = (f32[320,1280]{1,0:T(8,128)S(1)}, f32[320,1280]{1,0:T(8,128)}, u32[]{:S(2)}, u32[]{:S(2)}) collective-permute-start(f32[320,1280]{1,0:T(8,128)S(1)} %maximum_select_fusion.1), channel_id=1, source_target_pairs={{0,1},{1,0},{2,3},{3,2},{4,5},{5,4},{6,7},{7,6},{8,9},{9,8},{10,11... | collective-permute-start | bytes 4915208 | tf_op jit(solution)/shard_map/ppermute | solution.py:92

commit v5 on v3

--- a/solution.py
+++ b/solution.py
@@ -1,6 +1,7 @@
 import jax
 import jax.numpy as jnp
 from jax import lax
+from jax.experimental import pallas as pl
 from jax.sharding import PartitionSpec as P
 
 POS = 16
@@ -109,15 +110,42 @@
     return kern
 
 
+def pooled_kernel(fm_ref, w_ref, shift_ref, out_ref):
+    pre = jnp.dot(fm_ref[...], w_ref[...], preferred_element_type=jnp.float32) + shift_ref[...]
+    act = pre * jax.nn.sigmoid(pre)
+    images, channels = out_ref.shape
+    out_ref[...] = jnp.mean(act.reshape(images, POS, channels), axis=1).astype(out_ref.dtype)
+
+
+def pooled_of(feature_map, head_weight, head_shift, block_rows=128):
+    rows, c_in = feature_map.shape
+    channels = head_weight.shape[1]
+    block_rows = block_rows if rows % block_rows == 0 else rows
+    return pl.pallas_call(
+        pooled_kernel,
+        out_shape=jax.ShapeDtypeStruct((rows // POS, channels), jnp.bfloat16),
+        grid=(rows // block_rows,),
+        in_specs=[
+            pl.BlockSpec((block_rows, c_in), lambda i: (i, 0)),
+            pl.BlockSpec((c_in, channels), lambda i: (0, 0)),
+            pl.BlockSpec((1, channels), lambda i: (0, 0)),
+        ],
+        out_specs=pl.BlockSpec((block_rows // POS, channels), lambda i: (i, 0)),
+        cost_estimate=pl.CostEstimate(
+            flops=2 * rows * c_in * channels,
+            transcendentals=rows * channels,
+            bytes_accessed=2 * (rows * c_in + c_in * channels + rows // POS * channels) + 4 * channels,
+        ),
+    )(feature_map, head_weight, head_shift.reshape(1, channels))
+
+
 def make_body(mesh):
     steps = exchange_steps(mesh)
 
     def body(feature_map, head_weight, head_shift, proj_weight):
         images = feature_map.shape[0] // POS
         channels = head_weight.shape[1]
-        pre = jnp.dot(feature_map, head_weight, preferred_element_type=jnp.float32) + head_shift
-        act = jax.nn.silu(pre)
-        pooled = jnp.mean(act.reshape(images, POS, channels), axis=1).astype(jnp.bfloat16)
+        pooled = pooled_of(feature_map, head_weight, head_shift)
         proj = jnp.dot(pooled, proj_weight, preferred_element_type=jnp.float32)
         rnorm = jnp.sqrt(jnp.sum(proj * proj, axis=1, keepdims=True) + 1e-06)
         unit = proj / rnorm
@@ -147,6 +175,7 @@
         grad_act = jnp.broadcast_to(
             (grad_pooled / POS)[:, None, :], (images, POS, channels)
         ).reshape(images * POS, channels)
+        pre = jnp.dot(feature_map, head_weight, preferred_element_type=jnp.float32) + head_shift
         sig = jax.nn.sigmoid(pre)
         grad_pre = (grad_act * sig * (1.0 + pre * (1.0 - sig))).astype(jnp.bfloat16)
         c_in = feature_map.shape[1]

time: 117 us -> 118 us (level)
  other arithmetic: 13.9 us -> 8.8 us
  Pallas kernels: 0 us -> 4.8 us
  matrix products: 10.1 us -> 7.93 us
  waiting for transfers between devices: 50.2 us -> 51.9 us
    pallas_call x0 -> x1, Pallas kernels: none -> 4.8 us  [pooled_of(): pl.pallas_call(pooled_kernel, out_shape=jax.ShapeDtypeStruct((rows // POS...]
    reduce_sum x2 -> x0, other arithmetic: 3.87 us -> none  [the longest x1 2.51 us: body(): jnp.mean(act.reshape(images, POS, channels), axis=1).astype(jnp.bfloat16)]
    dot_general x1, matrix products: 5.03 us -> 1.96 us  [body(): jnp.dot(feature_map, head_weight, preferred_element_type=jnp.float32)]
    ppermute x25, waiting for transfers between devices: 50.2 us -> 51.9 us  [swap(): return lax.ppermute(x, ax, [(i, i ^ mask) for i in range(mesh.shape[ax])])]
    add x10, other arithmetic: 2.92 us -> 1.59 us  [all_reduce(): cur[j] = keeps[j] + got]
    reshape x0 -> x1, local copies, waits for them, and re-layouts: none -> 1.29 us  [pooled_of(): head_shift.reshape(1, channels)]
    unnamed x12 -> x17, local copies, waits for them, and re-layouts: 2.54 us -> 2.19 us
  transfers between devices with their start and end apart: 25 -> 25, of which waited for: 18 -> 19; matrix products, arithmetic and copies ran while one was open for 9% -> 6% of each run, Pallas kernels for 0% -> 0%
where the time goes in v5:
time: 118 us; the launch traced here: 117 us
  waiting for transfers between devices  51.9 us (44%)
  starting transfers between devices  34.7 us (29%)
  other arithmetic  8.8 us (7%)
  matrix products  7.93 us (7%)
  local copies, waits for them, and re-layouts  5.35 us (5%)
  Pallas kernels  4.8 us (4%)
  between operations  3.63 us (3%)
    ppermute x25, waiting for transfers between devices, swap(): return lax.ppermute(x, ax, [(i, i ^ mask) for i in range(mesh.shape[ax])])  51.9 us
    ppermute x25, starting transfers between devices, swap(): return lax.ppermute(x, ax, [(i, i ^ mask) for i in range(mesh.shape[ax])])  34.7 us
    pallas_call x1, Pallas kernels, pooled_of(): pl.pallas_call(pooled_kernel, out_shape=jax.ShapeDtypeStruct((rows // POS...  4.8 us
    select_n x10, other arithmetic, all_reduce(): jnp.where(my_bit(ax, mask), jnp.concatenate([g, c], axis=d), jnp.concaten...  4.17 us
    dot_general x1, matrix products, pair_terms(): lax.dot_general(rows_z, piece, (((1,), (1,)), ((), ())), preferred_elemen...  2.5 us
  transfers between devices with their start and end apart: 25, of which 19 were waited for; matrix products, arithmetic and copies ran while one was open for 6% of the time, Pallas kernels for 0%

profile of v5, /device:TPU:0, one launch (start us, length us, event | category | flops | bytes accessed | tf_op | source)
XLA Modules:
  0.0 117.1 jit_solution(7437797380966876850)
XLA Ops:
  0.6 2.1 %copy.8.fm_ref = bf16[640,320]{1,0:T(8,128)(2,1)} copy(bf16[640,320]{0,1:T(8,128)(2,1)} %param.4) | data formatting | bytes 819200 | tf_op args[0]
  4.0 4.8 %shard_map.75 = bf16[40,1280]{1,0:T(8,128)(2,1)} custom-call(bf16[640,320]{1,0:T(8,128)(2,1)} %copy.8.fm_ref, bf16[320,1280]{1,0:T(8,128)(2,1)} %w_ref.1, f32[1,1280]{1,0:T(1,128)} %reshape.1211.shift_ref), custom_call_target="tpu_custom_call" | custom-call | flops 524288000 | bytes 1336320 | tf_op jit(solution)/shard_map/pallas_call | solution.py:124
  10.2 4.1 %collective-permute-start = (bf16[1,40,256]{2,1,0:T(8,128)(2,1)S(1)}, bf16[1,40,256]{2,1,0:T(8,128)(2,1)S(1)}, u32[]{:S(2)}, u32[]{:S(2)}) collective-permute-start(bf16[1,40,256]{2,1,0:T(8,128)(2,1)S(1)} %fusion.48), channel_id=1, source_target_pairs={{0,16},{4,20},{8,24},{12,28},{16,0},{20,4},{24,8},{28,12},{1,17},{... | collective-permute-start | bytes 61448 | tf_op jit(solution)/shard_map/ppermute | solution.py:25
  14.5 1.6 %collective-permute-done = bf16[1,40,256]{2,1,0:T(8,128)(2,1)S(1)} collective-permute-done((bf16[1,40,256]{2,1,0:T(8,128)(2,1)S(1)}, bf16[1,40,256]{2,1,0:T(8,128)(2,1)S(1)}, u32[]{:S(2)}, u32[]{:S(2)}) %collective-permute-start) | collective-permute-done | bytes 20512 | tf_op jit(solution)/shard_map/ppermute | solution.py:25
  16.1 2.0 %collective-permute-start.1 = (bf16[2,1,40,256]{3,2,0,1:T(8,128)(2,1)S(1)}, bf16[2,1,40,256]{3,2,0,1:T(8,128)(2,1)S(1)}, u32[]{:S(2)}, u32[]{:S(2)}) collective-permute-start(bf16[2,1,40,256]{3,2,0,1:T(8,128)(2,1)S(1)} %maximum_select_fusion.17), channel_id=1, source_target_pairs={{0,8},{4,12},{8,0},{12,4},{16,24},{20,28},{24,16},{28,20},{1,9},{5... | collective-permute-start | bytes 122888 | tf_op jit(solution)/shard_map/ppermute | solution.py:25
  18.0 2.1 %collective-permute-done.1 = bf16[2,1,40,256]{3,2,0,1:T(8,128)(2,1)S(1)} collective-permute-done((bf16[2,1,40,256]{3,2,0,1:T(8,128)(2,1)S(1)}, bf16[2,1,40,256]{3,2,0,1:T(8,128)(2,1)S(1)}, u32[]{:S(2)}, u32[]{:S(2)}) %collective-permute-start.1) | collective-permute-done | bytes 40992 | tf_op jit(solution)/shard_map/ppermute | solution.py:25
  20.1 2.0 %collective-permute-start.2 = (bf16[2,2,1,40,256]{4,3,1,0,2:T(8,128)(2,1)S(1)}, bf16[2,2,1,40,256]{4,3,1,0,2:T(8,128)(2,1)S(1)}, u32[]{:S(2)}, u32[]{:S(2)}) collective-permute-start(bf16[2,2,1,40,256]{4,3,1,0,2:T(8,128)(2,1)S(1)} %maximum_select_fusion.14), channel_id=1, source_target_pairs={{0,4},{4,0},{8,12},{12,8},{16,20},{20,16},{24,28},{28,24},{1,5},{5... | collective-permute-start | bytes 245768 | tf_op jit(solution)/shard_map/ppermute | solution.py:25
  22.2 2.5 %collective-permute-done.2 = bf16[2,2,1,40,256]{4,3,1,0,2:T(8,128)(2,1)S(1)} collective-permute-done((bf16[2,2,1,40,256]{4,3,1,0,2:T(8,128)(2,1)S(1)}, bf16[2,2,1,40,256]{4,3,1,0,2:T(8,128)(2,1)S(1)}, u32[]{:S(2)}, u32[]{:S(2)}) %collective-permute-start.2) | collective-permute-done | bytes 81952 | tf_op jit(solution)/shard_map/ppermute | solution.py:25
  24.7 2.0 %collective-permute-start.3 = (bf16[2,2,2,1,40,256]{5,4,2,1,0,3:T(8,128)(2,1)S(1)}, bf16[2,2,2,1,40,256]{5,4,2,1,0,3:T(8,128)(2,1)S(1)}, u32[]{:S(2)}, u32[]{:S(2)}) collective-permute-start(bf16[2,2,2,1,40,256]{5,4,2,1,0,3:T(8,128)(2,1)S(1)} %maximum_select_fusion.10), channel_id=1, source_target_pairs={{0,2},{1,3},{2,0},{3,1},{4,6},{5,7},{6,4},{7,5},{8,10},{9,11},{10,... | collective-permute-start | bytes 491528 | tf_op jit(solution)/shard_map/ppermute | solution.py:25
  26.7 3.4 %collective-permute-done.3 = bf16[2,2,2,1,40,256]{5,4,2,1,0,3:T(8,128)(2,1)S(1)} collective-permute-done((bf16[2,2,2,1,40,256]{5,4,2,1,0,3:T(8,128)(2,1)S(1)}, bf16[2,2,2,1,40,256]{5,4,2,1,0,3:T(8,128)(2,1)S(1)}, u32[]{:S(2)}, u32[]{:S(2)}) %collective-permute-start.3) | collective-permute-done | bytes 163872 | tf_op jit(solution)/shard_map/ppermute | solution.py:25
  32.8 2.5 %fusion.9 = f32[]{:T(128)} fusion(bf16[1280,256]{1,0:T(8,128)(2,1)S(1)} %bitcast.73), kind=kOutput, calls=%fused_computation.17 | convolution fusion | flops 847052800 | bytes 655364 | tf_op jit(solution)/shard_map/dot_general | solution.py:105
  37.5 2.0 %convert_reduce_fusion = (f32[1280]{0:T(1024)S(1)}, bf16[640,1280]{1,0:T(8,128)(2,1)S(1)}) fusion(f32[1280]{0:T(1024)S(1)} %copy-done.7, bf16[640,320]{0,1:T(8,128)(2,1)S(1)} %copy-done.1, bf16[320,1280]{1,0:T(8,128)(2,1)S(1)} %copy-done.4, f32[40,1280]{1,0:T(8,128)S(1)} %convolution_multiply_fusion), kind=kOutput, calls=%fused_computation.9 | convolution fusion | flops 534117120 | bytes 3082240 | tf_op jit(solution)/shard_map/dot_general | solution.py:178
  42.1 1.6 %collective-permute-done.15 = f32[640,256]{1,0:T(8,128)S(1)} collective-permute-done((f32[640,256]{1,0:T(8,128)}, f32[640,256]{1,0:T(8,128)S(1)}, u32[]{:S(2)}, u32[]{:S(2)}) %collective-permute-start.15) | collective-permute-done | bytes 655392 | tf_op jit(solution)/shard_map/ppermute | solution.py:25
  43.8 2.0 %collective-permute-start.16 = (f32[320,256]{1,0:T(8,128)S(1)}, f32[320,256]{1,0:T(8,128)S(1)}, u32[]{:S(2)}, u32[]{:S(2)}) collective-permute-start(f32[320,256]{1,0:T(8,128)S(1)} %constant_dynamic-slice_fusion.3), channel_id=1, source_target_pairs={{0,4},{4,0},{8,12},{12,8},{16,20},{20,16},{24,28},{28,24},{1,5},{5... | collective-permute-start | bytes 983048 | tf_op jit(solution)/shard_map/ppermute | solution.py:25
  47.9 5.9 %collective-permute-done.16 = f32[320,256]{1,0:T(8,128)S(1)} collective-permute-done((f32[320,256]{1,0:T(8,128)S(1)}, f32[320,256]{1,0:T(8,128)S(1)}, u32[]{:S(2)}, u32[]{:S(2)}) %collective-permute-start.16) | collective-permute-done | bytes 327712 | tf_op jit(solution)/shard_map/ppermute | solution.py:25
  53.9 1.8 %collective-permute-start.17 = (f32[160,256]{1,0:T(8,128)S(1)}, f32[160,256]{1,0:T(8,128)S(1)}, u32[]{:S(2)}, u32[]{:S(2)}) collective-permute-start(f32[160,256]{1,0:T(8,128)S(1)} %constant_dynamic-slice_fusion.2), channel_id=1, source_target_pairs={{0,8},{4,12},{8,0},{12,4},{16,24},{20,28},{24,16},{28,20},{1,9},{5... | collective-permute-start | bytes 491528 | tf_op jit(solution)/shard_map/ppermute | solution.py:25
  57.4 2.1 %collective-permute-done.17 = f32[160,256]{1,0:T(8,128)S(1)} collective-permute-done((f32[160,256]{1,0:T(8,128)S(1)}, f32[160,256]{1,0:T(8,128)S(1)}, u32[]{:S(2)}, u32[]{:S(2)}) %collective-permute-start.17) | collective-permute-done | bytes 163872 | tf_op jit(solution)/shard_map/ppermute | solution.py:25
  59.6 1.6 %collective-permute-start.18 = (f32[80,256]{1,0:T(8,128)S(1)}, f32[80,256]{1,0:T(8,128)S(1)}, u32[]{:S(2)}, u32[]{:S(2)}) collective-permute-start(f32[80,256]{1,0:T(8,128)S(1)} %constant_dynamic-slice_fusion.1), channel_id=1, source_target_pairs={{0,2},{1,3},{2,0},{3,1},{4,6},{5,7},{6,4},{7,5},{8,10},{9,11},{10,... | collective-permute-start | bytes 245768 | tf_op jit(solution)/shard_map/ppermute | solution.py:25
  61.2 6.7 %collective-permute-done.6 = f32[81,1280]{1,0:T(8,128)S(1)} collective-permute-done((f32[81,1280]{1,0:T(8,128)S(1)}, f32[81,1280]{1,0:T(8,128)S(1)}, u32[]{:S(2)}, u32[]{:S(2)}) %collective-permute-start.6) | collective-permute-done | bytes 414752 | tf_op jit(solution)/shard_map/ppermute | solution.py:25
  68.0 1.6 %collective-permute-start.7 = (f32[41,1280]{1,0:T(8,128)S(1)}, f32[41,1280]{1,0:T(8,128)S(1)}, u32[]{:S(2)}, u32[]{:S(2)}) collective-permute-start(f32[41,1280]{1,0:T(8,128)S(1)} %pad_maximum_fusion.6), channel_id=1, source_target_pairs={{0,4},{4,0},{8,12},{12,8},{16,20},{20,16},{24,28},{28,24},{1,5},{5... | collective-permute-start | bytes 629768 | tf_op jit(solution)/shard_map/ppermute | solution.py:25
  69.6 4.7 %collective-permute-done.7 = f32[41,1280]{1,0:T(8,128)S(1)} collective-permute-done((f32[41,1280]{1,0:T(8,128)S(1)}, f32[41,1280]{1,0:T(8,128)S(1)}, u32[]{:S(2)}, u32[]{:S(2)}) %collective-permute-start.7) | collective-permute-done | bytes 209952 | tf_op jit(solution)/shard_map/ppermute | solution.py:25
  75.0 2.5 %collective-permute-start.19 = (f32[40,256]{1,0:T(8,128)S(1)}, f32[40,256]{1,0:T(8,128)S(1)}, u32[]{:S(2)}, u32[]{:S(2)}) collective-permute-start(f32[40,256]{1,0:T(8,128)S(1)} %constant_dynamic-slice_fusion), channel_id=1, source_target_pairs={{0,16},{4,20},{8,24},{12,28},{16,0},{20,4},{24,8},{28,12},{1,17},{... | collective-permute-start | bytes 122888 | tf_op jit(solution)/shard_map/ppermute | solution.py:25
  77.7 2.9 %collective-permute-done.8 = f32[42,640]{1,0:T(8,128)S(1)} collective-permute-done((f32[42,640]{1,0:T(8,128)S(1)}, f32[42,640]{1,0:T(8,128)S(1)}, u32[]{:S(2)}, u32[]{:S(2)}) %collective-permute-start.8) | collective-permute-done | bytes 107552 | tf_op jit(solution)/shard_map/ppermute | solution.py:25
  80.8 2.0 %collective-permute-start.9 = (f32[44,320]{1,0:T(8,128)S(1)}, f32[44,320]{1,0:T(8,128)S(1)}, u32[]{:S(2)}, u32[]{:S(2)}) collective-permute-start(f32[44,320]{1,0:T(8,128)S(1)} %pad_maximum_fusion.8), channel_id=1, source_target_pairs={{0,16},{4,20},{8,24},{12,28},{16,0},{20,4},{24,8},{28,12},{1,17},{... | collective-permute-start | bytes 168968 | tf_op jit(solution)/shard_map/ppermute | solution.py:25
  83.9 2.3 %collective-permute-done.9 = f32[44,320]{1,0:T(8,128)S(1)} collective-permute-done((f32[44,320]{1,0:T(8,128)S(1)}, f32[44,320]{1,0:T(8,128)S(1)}, u32[]{:S(2)}, u32[]{:S(2)}) %collective-permute-start.9) | collective-permute-done | bytes 56352 | tf_op jit(solution)/shard_map/ppermute | solution.py:25
  86.3 2.0 %collective-permute-start.10 = (f32[40,320]{1,0:T(8,128)S(1)}, f32[40,320]{1,0:T(8,128)S(1)}, u32[]{:S(2)}, u32[]{:S(2)}) collective-permute-start(f32[40,320]{1,0:T(8,128)S(1)} %slice_add_fusion.4), channel_id=1, source_target_pairs={{0,16},{4,20},{8,24},{12,28},{16,0},{20,4},{24,8},{28,12},{1,17},{... | collective-permute-start | bytes 153608 | tf_op jit(solution)/shard_map/ppermute | solution.py:25
  89.9 1.9 %collective-permute-done.10 = f32[40,320]{1,0:T(8,128)S(1)} collective-permute-done((f32[40,320]{1,0:T(8,128)S(1)}, f32[40,320]{1,0:T(8,128)S(1)}, u32[]{:S(2)}, u32[]{:S(2)}) %collective-permute-start.10) | collective-permute-done | bytes 51232 | tf_op jit(solution)/shard_map/ppermute | solution.py:25
  94.1 2.5 %collective-permute-done.11 = f32[40,640]{1,0:T(8,128)S(1)} collective-permute-done((f32[40,640]{1,0:T(8,128)S(1)}, f32[40,640]{1,0:T(8,128)S(1)}, u32[]{:S(2)}, u32[]{:S(2)}) %collective-permute-start.11) | collective-permute-done | bytes 102432 | tf_op jit(solution)/shard_map/ppermute | solution.py:25
  99.9 2.6 %collective-permute-done.12 = f32[40,1280]{1,0:T(8,128)S(1)} collective-permute-done((f32[40,1280]{1,0:T(8,128)S(1)}, f32[40,1280]{1,0:T(8,128)S(1)}, u32[]{:S(2)}, u32[]{:S(2)}) %collective-permute-start.12) | collective-permute-done | bytes 204832 | tf_op jit(solution)/shard_map/ppermute | solution.py:25
  103.9 2.1 %collective-permute-done.23 = f32[320,256]{1,0:T(8,128)S(1)} collective-permute-done((f32[320,256]{1,0:T(8,128)S(1)}, f32[320,256]{1,0:T(8,128)S(1)}, u32[]{:S(2)}, u32[]{:S(2)}) %collective-permute-start.23) | collective-permute-done | bytes 327712 | tf_op jit(solution)/shard_map/ppermute | solution.py:25
  106.2 4.4 %collective-permute-done.13 = f32[80,1280]{1,0:T(8,128)S(1)} collective-permute-done((f32[80,1280]{1,0:T(8,128)S(1)}, f32[80,1280]{1,0:T(8,128)S(1)}, u32[]{:S(2)}, u32[]{:S(2)}) %collective-permute-start.13) | collective-permute-done | bytes 409632 | tf_op jit(solution)/shard_map/ppermute | solution.py:25
  112.1 2.6 %maximum_select_fusion.1 = f32[1280,256]{1,0:T(8,128)} fusion(f32[640,256]{1,0:T(8,128)S(1)} %maximum_select_fusion.3, f32[640,256]{1,0:T(8,128)} %collective-permute-done.24, pred[]{:T(512)S(6)} %ne.10), kind=kLoop, calls=%fused_computation.18 | loop fusion | flops 983040 | bytes 2621441 | tf_op jit(solution)/shard_map/jit(_where)/select_n | solution.py:93
  (114 shorter events, 26.7 us)
Async XLA Ops:
  0.6 8.2 %copy-start = (bf16[1280,256]{1,0:T(8,128)(2,1)S(1)}, bf16[1280,256]{1,0:T(8,128)(2,1)}, u32[]{:S(2)}) copy-start(bf16[1280,256]{1,0:T(8,128)(2,1)} %param.7) | copy-start | bytes 1966084
  10.2 5.9 %collective-permute-start = (bf16[1,40,256]{2,1,0:T(8,128)(2,1)S(1)}, bf16[1,40,256]{2,1,0:T(8,128)(2,1)S(1)}, u32[]{:S(2)}, u32[]{:S(2)}) collective-permute-start(bf16[1,40,256]{2,1,0:T(8,128)(2,1)S(1)} %fusion.48), channel_id=1, source_target_pairs={{0,16},{4,20},{8,24},{12,28},{16,0},{20,4},{24,8},{28,12},{1,17},{... | collective-permute-start | bytes 61448 | tf_op jit(solution)/shard_map/ppermute | solution.py:25
  16.1 4.1 %collective-permute-start.1 = (bf16[2,1,40,256]{3,2,0,1:T(8,128)(2,1)S(1)}, bf16[2,1,40,256]{3,2,0,1:T(8,128)(2,1)S(1)}, u32[]{:S(2)}, u32[]{:S(2)}) collective-permute-start(bf16[2,1,40,256]{3,2,0,1:T(8,128)(2,1)S(1)} %maximum_select_fusion.17), channel_id=1, source_target_pairs={{0,8},{4,12},{8,0},{12,4},{16,24},{20,28},{24,16},{28,20},{1,9},{5... | collective-permute-start | bytes 122888 | tf_op jit(solution)/shard_map/ppermute | solution.py:25
  20.1 4.5 %collective-permute-start.2 = (bf16[2,2,1,40,256]{4,3,1,0,2:T(8,128)(2,1)S(1)}, bf16[2,2,1,40,256]{4,3,1,0,2:T(8,128)(2,1)S(1)}, u32[]{:S(2)}, u32[]{:S(2)}) collective-permute-start(bf16[2,2,1,40,256]{4,3,1,0,2:T(8,128)(2,1)S(1)} %maximum_select_fusion.14), channel_id=1, source_target_pairs={{0,4},{4,0},{8,12},{12,8},{16,20},{20,16},{24,28},{28,24},{1,5},{5... | collective-permute-start | bytes 245768 | tf_op jit(solution)/shard_map/ppermute | solution.py:25
  24.7 5.4 %collective-permute-start.3 = (bf16[2,2,2,1,40,256]{5,4,2,1,0,3:T(8,128)(2,1)S(1)}, bf16[2,2,2,1,40,256]{5,4,2,1,0,3:T(8,128)(2,1)S(1)}, u32[]{:S(2)}, u32[]{:S(2)}) collective-permute-start(bf16[2,2,2,1,40,256]{5,4,2,1,0,3:T(8,128)(2,1)S(1)} %maximum_select_fusion.10), channel_id=1, source_target_pairs={{0,2},{1,3},{2,0},{3,1},{4,6},{5,7},{6,4},{7,5},{8,10},{9,11},{10,... | collective-permute-start | bytes 491528 | tf_op jit(solution)/shard_map/ppermute | solution.py:25
  30.1 1.7 %collective-permute-start.4 = (bf16[2,2,2,2,1,40,256]{6,5,3,2,1,4,0:T(8,128)(2,1)S(1)}, bf16[2,2,2,2,1,40,256]{6,5,3,2,1,4,0:T(8,128)(2,1)S(1)}, u32[]{:S(2)}, u32[]{:S(2)}) collective-permute-start(bf16[2,2,2,2,1,40,256]{6,5,3,2,1,4,0:T(8,128)(2,1)S(1)} %maximum_select_fusion.5), channel_id=1, source_target_pairs={{0,1},{1,0},{2,3},{3,2},{4,5},{5,4},{6,7},{7,6},{8,9},{9,8},{10,11... | collective-permute-start | bytes 983048 | tf_op jit(solution)/shard_map/ppermute | solution.py:25
  32.8 3.2 %copy-start.5 = (bf16[2,2,2,2,2,1,40,256]{7,6,4,3,2,5,1,0:T(8,128)(2,1)S(1)}, bf16[2,2,2,2,2,1,40,256]{7,6,4,3,2,5,1,0:T(8,128)(2,1)}, u32[]{:S(2)}) copy-start(bf16[2,2,2,2,2,1,40,256]{7,6,4,3,2,5,1,0:T(8,128)(2,1)} %get-tuple-element.8) | copy-start | bytes 1966084
  35.3 1.8 %copy-start.6 = (bf16[40,1280]{1,0:T(8,128)(2,1)S(1)}, bf16[40,1280]{1,0:T(8,128)(2,1)}, u32[]{:S(2)}) copy-start(bf16[40,1280]{1,0:T(8,128)(2,1)} %shard_map.75) | copy-start | bytes 307204
  36.0 1.5 %copy-start.1 = (bf16[640,320]{0,1:T(8,128)(2,1)S(1)}, bf16[640,320]{0,1:T(8,128)(2,1)}, u32[]{:S(2)}) copy-start(bf16[640,320]{0,1:T(8,128)(2,1)} %param.4) | copy-start | bytes 1228804
  36.0 1.5 %copy-start.4 = (bf16[320,1280]{1,0:T(8,128)(2,1)S(1)}, bf16[320,1280]{1,0:T(8,128)(2,1)}, u32[]{:S(2)}) copy-start(bf16[320,1280]{1,0:T(8,128)(2,1)} %w_ref.1) | copy-start | bytes 2457604
  36.1 1.5 %copy-start.7 = (f32[1280]{0:T(1024)S(1)}, f32[1280]{0:T(1024)}, u32[]{:S(2)}) copy-start(f32[1280]{0:T(1024)} %param.6) | copy-start | bytes 15364
  41.3 2.3 %collective-permute-start.15 = (f32[640,256]{1,0:T(8,128)}, f32[640,256]{1,0:T(8,128)S(1)}, u32[]{:S(2)}, u32[]{:S(2)}) collective-permute-start(f32[640,256]{1,0:T(8,128)} %constant_dynamic-slice_fusion.4), channel_id=1, source_target_pairs={{0,1},{1,0},{2,3},{3,2},{4,5},{5,4},{6,7},{7,6},{8,9},{9,8},{10,11... | collective-permute-start | bytes 1966088 | tf_op jit(solution)/shard_map/ppermute | solution.py:25
  41.7 4.1 %collective-permute-start.5 = (f32[161,1280]{1,0:T(8,128)S(1)}, f32[161,1280]{1,0:T(8,128)}, u32[]{:S(2)}, u32[]{:S(2)}) collective-permute-start(f32[161,1280]{1,0:T(8,128)S(1)} %pad_maximum_fusion), channel_id=1, source_target_pairs={{0,1},{1,0},{2,3},{3,2},{4,5},{5,4},{6,7},{7,6},{8,9},{9,8},{10,11... | collective-permute-start | bytes 2472968 | tf_op jit(solution)/shard_map/ppermute | solution.py:25
  42.1 3.7 %copy-start.3 = (f32[1280,320]{0,1:T(8,128)S(1)}, f32[1280,320]{0,1:T(8,128)}, u32[]{:S(2)}) copy-start(f32[1280,320]{0,1:T(8,128)} %copy-done.2) | copy-start | bytes 4915204
  43.8 10.0 %collective-permute-start.16 = (f32[320,256]{1,0:T(8,128)S(1)}, f32[320,256]{1,0:T(8,128)S(1)}, u32[]{:S(2)}, u32[]{:S(2)}) collective-permute-start(f32[320,256]{1,0:T(8,128)S(1)} %constant_dynamic-slice_fusion.3), channel_id=1, source_target_pairs={{0,4},{4,0},{8,12},{12,8},{16,20},{20,16},{24,28},{28,24},{1,5},{5... | collective-permute-start | bytes 983048 | tf_op jit(solution)/shard_map/ppermute | solution.py:25
  53.9 5.6 %collective-permute-start.17 = (f32[160,256]{1,0:T(8,128)S(1)}, f32[160,256]{1,0:T(8,128)S(1)}, u32[]{:S(2)}, u32[]{:S(2)}) collective-permute-start(f32[160,256]{1,0:T(8,128)S(1)} %constant_dynamic-slice_fusion.2), channel_id=1, source_target_pairs={{0,8},{4,12},{8,0},{12,4},{16,24},{20,28},{24,16},{28,20},{1,9},{5... | collective-permute-start | bytes 491528 | tf_op jit(solution)/shard_map/ppermute | solution.py:25
  55.7 12.2 %collective-permute-start.6 = (f32[81,1280]{1,0:T(8,128)S(1)}, f32[81,1280]{1,0:T(8,128)S(1)}, u32[]{:S(2)}, u32[]{:S(2)}) collective-permute-start(f32[81,1280]{1,0:T(8,128)S(1)} %pad_maximum_fusion.5), channel_id=1, source_target_pairs={{0,2},{1,3},{2,0},{3,1},{4,6},{5,7},{6,4},{7,5},{8,10},{9,11},{10,... | collective-permute-start | bytes 1244168 | tf_op jit(solution)/shard_map/ppermute | solution.py:25
  59.6 10.0 %collective-permute-start.18 = (f32[80,256]{1,0:T(8,128)S(1)}, f32[80,256]{1,0:T(8,128)S(1)}, u32[]{:S(2)}, u32[]{:S(2)}) collective-permute-start(f32[80,256]{1,0:T(8,128)S(1)} %constant_dynamic-slice_fusion.1), channel_id=1, source_target_pairs={{0,2},{1,3},{2,0},{3,1},{4,6},{5,7},{6,4},{7,5},{8,10},{9,11},{10,... | collective-permute-start | bytes 245768 | tf_op jit(solution)/shard_map/ppermute | solution.py:25
  68.0 6.3 %collective-permute-start.7 = (f32[41,1280]{1,0:T(8,128)S(1)}, f32[41,1280]{1,0:T(8,128)S(1)}, u32[]{:S(2)}, u32[]{:S(2)}) collective-permute-start(f32[41,1280]{1,0:T(8,128)S(1)} %pad_maximum_fusion.6), channel_id=1, source_target_pairs={{0,4},{4,0},{8,12},{12,8},{16,20},{20,16},{24,28},{28,24},{1,5},{5... | collective-permute-start | bytes 629768 | tf_op jit(solution)/shard_map/ppermute | solution.py:25
  74.4 6.2 %collective-permute-start.8 = (f32[42,640]{1,0:T(8,128)S(1)}, f32[42,640]{1,0:T(8,128)S(1)}, u32[]{:S(2)}, u32[]{:S(2)}) collective-permute-start(f32[42,640]{1,0:T(8,128)S(1)} %pad_maximum_fusion.7), channel_id=1, source_target_pairs={{0,8},{4,12},{8,0},{12,4},{16,24},{20,28},{24,16},{28,20},{1,9},{5... | collective-permute-start | bytes 322568 | tf_op jit(solution)/shard_map/ppermute | solution.py:25
  75.0 7.8 %collective-permute-start.19 = (f32[40,256]{1,0:T(8,128)S(1)}, f32[40,256]{1,0:T(8,128)S(1)}, u32[]{:S(2)}, u32[]{:S(2)}) collective-permute-start(f32[40,256]{1,0:T(8,128)S(1)} %constant_dynamic-slice_fusion), channel_id=1, source_target_pairs={{0,16},{4,20},{8,24},{12,28},{16,0},{20,4},{24,8},{28,12},{1,17},{... | collective-permute-start | bytes 122888 | tf_op jit(solution)/shard_map/ppermute | solution.py:25
  80.8 5.4 %collective-permute-start.9 = (f32[44,320]{1,0:T(8,128)S(1)}, f32[44,320]{1,0:T(8,128)S(1)}, u32[]{:S(2)}, u32[]{:S(2)}) collective-permute-start(f32[44,320]{1,0:T(8,128)S(1)} %pad_maximum_fusion.8), channel_id=1, source_target_pairs={{0,16},{4,20},{8,24},{12,28},{16,0},{20,4},{24,8},{28,12},{1,17},{... | collective-permute-start | bytes 168968 | tf_op jit(solution)/shard_map/ppermute | solution.py:25
  82.8 5.5 %collective-permute-start.20 = (f32[40,256]{1,0:T(8,128)S(1)}, f32[40,256]{1,0:T(8,128)S(1)}, u32[]{:S(2)}, u32[]{:S(2)}) collective-permute-start(f32[40,256]{1,0:T(8,128)S(1)} %dynamic-slice_add_fusion.4), channel_id=1, source_target_pairs={{0,16},{4,20},{8,24},{12,28},{16,0},{20,4},{24,8},{28,12},{1,17},{... | collective-permute-start | bytes 122888 | tf_op jit(solution)/shard_map/ppermute | solution.py:25
  86.3 5.5 %collective-permute-start.10 = (f32[40,320]{1,0:T(8,128)S(1)}, f32[40,320]{1,0:T(8,128)S(1)}, u32[]{:S(2)}, u32[]{:S(2)}) collective-permute-start(f32[40,320]{1,0:T(8,128)S(1)} %slice_add_fusion.4), channel_id=1, source_target_pairs={{0,16},{4,20},{8,24},{12,28},{16,0},{20,4},{24,8},{28,12},{1,17},{... | collective-permute-start | bytes 153608 | tf_op jit(solution)/shard_map/ppermute | solution.py:25
  88.3 4.5 %collective-permute-start.21 = (f32[80,256]{1,0:T(8,128)S(1)}, f32[80,256]{1,0:T(8,128)S(1)}, u32[]{:S(2)}, u32[]{:S(2)}) collective-permute-start(f32[80,256]{1,0:T(8,128)S(1)} %maximum_select_fusion.16), channel_id=1, source_target_pairs={{0,2},{1,3},{2,0},{3,1},{4,6},{5,7},{6,4},{7,5},{8,10},{9,11},{10,... | collective-permute-start | bytes 245768 | tf_op jit(solution)/shard_map/ppermute | solution.py:25
  91.9 4.7 %collective-permute-start.11 = (f32[40,640]{1,0:T(8,128)S(1)}, f32[40,640]{1,0:T(8,128)S(1)}, u32[]{:S(2)}, u32[]{:S(2)}) collective-permute-start(f32[40,640]{1,0:T(8,128)S(1)} %maximum_select_fusion.13), channel_id=1, source_target_pairs={{0,8},{4,12},{8,0},{12,4},{16,24},{20,28},{24,16},{28,20},{1,9},{5... | collective-permute-start | bytes 307208 | tf_op jit(solution)/shard_map/ppermute | solution.py:25
  92.8 5.6 %collective-permute-start.22 = (f32[160,256]{1,0:T(8,128)S(1)}, f32[160,256]{1,0:T(8,128)S(1)}, u32[]{:S(2)}, u32[]{:S(2)}) collective-permute-start(f32[160,256]{1,0:T(8,128)S(1)} %maximum_select_fusion.12), channel_id=1, source_target_pairs={{0,8},{4,12},{8,0},{12,4},{16,24},{20,28},{24,16},{28,20},{1,9},{5... | collective-permute-start | bytes 491528 | tf_op jit(solution)/shard_map/ppermute | solution.py:25
  96.7 5.8 %collective-permute-start.12 = (f32[40,1280]{1,0:T(8,128)S(1)}, f32[40,1280]{1,0:T(8,128)S(1)}, u32[]{:S(2)}, u32[]{:S(2)}) collective-permute-start(f32[40,1280]{1,0:T(8,128)S(1)} %maximum_select_fusion.9), channel_id=1, source_target_pairs={{0,4},{4,0},{8,12},{12,8},{16,20},{20,16},{24,28},{28,24},{1,5},{5... | collective-permute-start | bytes 614408 | tf_op jit(solution)/shard_map/ppermute | solution.py:25
  98.4 7.6 %collective-permute-start.23 = (f32[320,256]{1,0:T(8,128)S(1)}, f32[320,256]{1,0:T(8,128)S(1)}, u32[]{:S(2)}, u32[]{:S(2)}) collective-permute-start(f32[320,256]{1,0:T(8,128)S(1)} %maximum_select_fusion.8), channel_id=1, source_target_pairs={{0,4},{4,0},{8,12},{12,8},{16,20},{20,16},{24,28},{28,24},{1,5},{5... | collective-permute-start | bytes 983048 | tf_op jit(solution)/shard_map/ppermute | solution.py:25
  102.5 8.0 %collective-permute-start.13 = (f32[80,1280]{1,0:T(8,128)S(1)}, f32[80,1280]{1,0:T(8,128)S(1)}, u32[]{:S(2)}, u32[]{:S(2)}) collective-permute-start(f32[80,1280]{1,0:T(8,128)S(1)} %maximum_select_fusion.4), channel_id=1, source_target_pairs={{0,2},{1,3},{2,0},{3,1},{4,6},{5,7},{6,4},{7,5},{8,10},{9,11},{10,... | collective-permute-start | bytes 1228808 | tf_op jit(solution)/shard_map/ppermute | solution.py:25
  106.1 6.0 %collective-permute-start.24 = (f32[640,256]{1,0:T(8,128)S(1)}, f32[640,256]{1,0:T(8,128)}, u32[]{:S(2)}, u32[]{:S(2)}) collective-permute-start(f32[640,256]{1,0:T(8,128)S(1)} %maximum_select_fusion.3), channel_id=1, source_target_pairs={{0,1},{1,0},{2,3},{3,2},{4,5},{5,4},{6,7},{7,6},{8,9},{9,8},{10,11... | collective-permute-start | bytes 1966088 | tf_op jit(solution)/shard_map/ppermute | solution.py:25
  110.6 4.0 %collective-permute-start.14 = (f32[160,1280]{1,0:T(8,128)S(1)}, f32[160,1280]{1,0:T(8,128)S(1)}, u32[]{:S(2)}, u32[]{:S(2)}) collective-permute-start(f32[160,1280]{1,0:T(8,128)S(1)} %maximum_select_fusion.2), channel_id=1, source_target_pairs={{0,1},{1,0},{2,3},{3,2},{4,5},{5,4},{6,7},{7,6},{8,9},{9,8},{10,11... | collective-permute-start | bytes 2457608 | tf_op jit(solution)/shard_map/ppermute | solution.py:25
  (1 other events, 1.4 us)

commit v6 on v5

--- a/solution.py
+++ b/solution.py
@@ -110,8 +110,10 @@
     return kern
 
 
-def pooled_kernel(fm_ref, w_ref, shift_ref, out_ref):
-    pre = jnp.dot(fm_ref[...], w_ref[...], preferred_element_type=jnp.float32) + shift_ref[...]
+def pooled_kernel(fm_t_ref, w_ref, shift_ref, out_ref):
+    pre = lax.dot_general(
+        fm_t_ref[...], w_ref[...], (((0,), (0,)), ((), ())), preferred_element_type=jnp.float32
+    ) + shift_ref[...][None, :]
     act = pre * jax.nn.sigmoid(pre)
     images, channels = out_ref.shape
     out_ref[...] = jnp.mean(act.reshape(images, POS, channels), axis=1).astype(out_ref.dtype)
@@ -126,9 +128,9 @@
         out_shape=jax.ShapeDtypeStruct((rows // POS, channels), jnp.bfloat16),
         grid=(rows // block_rows,),
         in_specs=[
-            pl.BlockSpec((block_rows, c_in), lambda i: (i, 0)),
+            pl.BlockSpec((c_in, block_rows), lambda i: (0, i)),
             pl.BlockSpec((c_in, channels), lambda i: (0, 0)),
-            pl.BlockSpec((1, channels), lambda i: (0, 0)),
+            pl.BlockSpec((channels,), lambda i: (0,)),
         ],
         out_specs=pl.BlockSpec((block_rows // POS, channels), lambda i: (i, 0)),
         cost_estimate=pl.CostEstimate(
@@ -136,7 +138,7 @@
             transcendentals=rows * channels,
             bytes_accessed=2 * (rows * c_in + c_in * channels + rows // POS * channels) + 4 * channels,
         ),
-    )(feature_map, head_weight, head_shift.reshape(1, channels))
+    )(feature_map.T, head_weight, head_shift)
 
 
 def make_body(mesh):

time: 118 us -> 114 us (0.966)
  local copies, waits for them, and re-layouts: 5.35 us -> 2.28 us
    unnamed x17 -> x14, local copies, waits for them, and re-layouts: 2.19 us -> 0.41 us
    reshape x1 -> x0, local copies, waits for them, and re-layouts: 1.29 us -> none  [pooled_of(): head_shift.reshape(1, channels)]
where the time goes in v6:
time: 114 us; the launch traced here: 113 us
  waiting for transfers between devices  52 us (46%)
  starting transfers between devices  34.6 us (30%)
  matrix products  7.92 us (7%)
  other arithmetic  7.92 us (7%)
  Pallas kernels  5 us (4%)
  between operations  3.61 us (3%)
  local copies, waits for them, and re-layouts  2.28 us (2%)
    ppermute x25, waiting for transfers between devices, swap(): return lax.ppermute(x, ax, [(i, i ^ mask) for i in range(mesh.shape[ax])])  52 us
    ppermute x25, starting transfers between devices, swap(): return lax.ppermute(x, ax, [(i, i ^ mask) for i in range(mesh.shape[ax])])  34.6 us
    pallas_call x1, Pallas kernels, pooled_of(): pl.pallas_call(pooled_kernel, out_shape=jax.ShapeDtypeStruct((rows // POS...  5 us
    select_n x10, other arithmetic, all_reduce(): jnp.where(my_bit(ax, mask), jnp.concatenate([g, c], axis=d), jnp.concaten...  4.13 us
    dot_general x1, matrix products, pair_terms(): lax.dot_general(rows_z, piece, (((1,), (1,)), ((), ())), preferred_elemen...  2.5 us
  transfers between devices with their start and end apart: 25, of which 19 were waited for; matrix products, arithmetic and copies ran while one was open for 6% of the time, Pallas kernels for 0%

profile of v6, /device:TPU:0, one launch (start us, length us, event | category | flops | bytes accessed | tf_op | source)
XLA Modules:
  0.0 113.3 jit_solution(8049320974958315714)
XLA Ops:
  0.6 5.0 %shard_map.75 = bf16[40,1280]{1,0:T(8,128)(2,1)} custom-call(bf16[320,640]{1,0:T(8,128)(2,1)} %bitcast.75, bf16[320,1280]{1,0:T(8,128)(2,1)} %w_ref.1, f32[1280]{0:T(1024)} %shift_ref.1), custom_call_target="tpu_custom_call" | custom-call | flops 524288000 | bytes 1336320 | tf_op jit(solution)/shard_map/pallas_call | solution.py:126
  7.0 4.1 %collective-permute-start = (bf16[1,40,256]{2,1,0:T(8,128)(2,1)S(1)}, bf16[1,40,256]{2,1,0:T(8,128)(2,1)S(1)}, u32[]{:S(2)}, u32[]{:S(2)}) collective-permute-start(bf16[1,40,256]{2,1,0:T(8,128)(2,1)S(1)} %fusion.48), channel_id=1, source_target_pairs={{0,16},{4,20},{8,24},{12,28},{16,0},{20,4},{24,8},{28,12},{1,17},{... | collective-permute-start | bytes 61448 | tf_op jit(solution)/shard_map/ppermute | solution.py:25
  11.3 1.6 %collective-permute-done = bf16[1,40,256]{2,1,0:T(8,128)(2,1)S(1)} collective-permute-done((bf16[1,40,256]{2,1,0:T(8,128)(2,1)S(1)}, bf16[1,40,256]{2,1,0:T(8,128)(2,1)S(1)}, u32[]{:S(2)}, u32[]{:S(2)}) %collective-permute-start) | collective-permute-done | bytes 20512 | tf_op jit(solution)/shard_map/ppermute | solution.py:25
  12.9 2.0 %collective-permute-start.1 = (bf16[2,1,40,256]{3,2,0,1:T(8,128)(2,1)S(1)}, bf16[2,1,40,256]{3,2,0,1:T(8,128)(2,1)S(1)}, u32[]{:S(2)}, u32[]{:S(2)}) collective-permute-start(bf16[2,1,40,256]{3,2,0,1:T(8,128)(2,1)S(1)} %maximum_select_fusion.17), channel_id=1, source_target_pairs={{0,8},{4,12},{8,0},{12,4},{16,24},{20,28},{24,16},{28,20},{1,9},{5... | collective-permute-start | bytes 122888 | tf_op jit(solution)/shard_map/ppermute | solution.py:25
  14.9 2.1 %collective-permute-done.1 = bf16[2,1,40,256]{3,2,0,1:T(8,128)(2,1)S(1)} collective-permute-done((bf16[2,1,40,256]{3,2,0,1:T(8,128)(2,1)S(1)}, bf16[2,1,40,256]{3,2,0,1:T(8,128)(2,1)S(1)}, u32[]{:S(2)}, u32[]{:S(2)}) %collective-permute-start.1) | collective-permute-done | bytes 40992 | tf_op jit(solution)/shard_map/ppermute | solution.py:25
  17.0 2.0 %collective-permute-start.2 = (bf16[2,2,1,40,256]{4,3,1,0,2:T(8,128)(2,1)S(1)}, bf16[2,2,1,40,256]{4,3,1,0,2:T(8,128)(2,1)S(1)}, u32[]{:S(2)}, u32[]{:S(2)}) collective-permute-start(bf16[2,2,1,40,256]{4,3,1,0,2:T(8,128)(2,1)S(1)} %maximum_select_fusion.14), channel_id=1, source_target_pairs={{0,4},{4,0},{8,12},{12,8},{16,20},{20,16},{24,28},{28,24},{1,5},{5... | collective-permute-start | bytes 245768 | tf_op jit(solution)/shard_map/ppermute | solution.py:25
  19.0 2.5 %collective-permute-done.2 = bf16[2,2,1,40,256]{4,3,1,0,2:T(8,128)(2,1)S(1)} collective-permute-done((bf16[2,2,1,40,256]{4,3,1,0,2:T(8,128)(2,1)S(1)}, bf16[2,2,1,40,256]{4,3,1,0,2:T(8,128)(2,1)S(1)}, u32[]{:S(2)}, u32[]{:S(2)}) %collective-permute-start.2) | collective-permute-done | bytes 81952 | tf_op jit(solution)/shard_map/ppermute | solution.py:25
  21.5 2.0 %collective-permute-start.3 = (bf16[2,2,2,1,40,256]{5,4,2,1,0,3:T(8,128)(2,1)S(1)}, bf16[2,2,2,1,40,256]{5,4,2,1,0,3:T(8,128)(2,1)S(1)}, u32[]{:S(2)}, u32[]{:S(2)}) collective-permute-start(bf16[2,2,2,1,40,256]{5,4,2,1,0,3:T(8,128)(2,1)S(1)} %maximum_select_fusion.10), channel_id=1, source_target_pairs={{0,2},{1,3},{2,0},{3,1},{4,6},{5,7},{6,4},{7,5},{8,10},{9,11},{10,... | collective-permute-start | bytes 491528 | tf_op jit(solution)/shard_map/ppermute | solution.py:25
  23.5 3.4 %collective-permute-done.3 = bf16[2,2,2,1,40,256]{5,4,2,1,0,3:T(8,128)(2,1)S(1)} collective-permute-done((bf16[2,2,2,1,40,256]{5,4,2,1,0,3:T(8,128)(2,1)S(1)}, bf16[2,2,2,1,40,256]{5,4,2,1,0,3:T(8,128)(2,1)S(1)}, u32[]{:S(2)}, u32[]{:S(2)}) %collective-permute-start.3) | collective-permute-done | bytes 163872 | tf_op jit(solution)/shard_map/ppermute | solution.py:25
  28.8 2.5 %fusion.9 = f32[]{:T(128)} fusion(bf16[1280,256]{1,0:T(8,128)(2,1)S(1)} %bitcast.74), kind=kOutput, calls=%fused_computation.17 | convolution fusion | flops 847052800 | bytes 655364 | tf_op jit(solution)/shard_map/dot_general | solution.py:105
  33.8 2.0 %convert_reduce_fusion = (f32[1280]{0:T(1024)S(1)}, bf16[640,1280]{1,0:T(8,128)(2,1)S(1)}) fusion(f32[1280]{0:T(1024)S(1)} %copy-done.6, bf16[640,320]{0,1:T(8,128)(2,1)S(1)} %copy-done.4, bf16[320,1280]{1,0:T(8,128)(2,1)S(1)} %copy-done.3, f32[40,1280]{1,0:T(8,128)S(1)} %convolution_multiply_fusion), kind=kOutput, calls=%fused_computation.9 | convolution fusion | flops 534117120 | bytes 3082240 | tf_op jit(solution)/shard_map/dot_general | solution.py:180
  38.3 1.6 %collective-permute-done.15 = f32[640,256]{1,0:T(8,128)S(1)} collective-permute-done((f32[640,256]{1,0:T(8,128)}, f32[640,256]{1,0:T(8,128)S(1)}, u32[]{:S(2)}, u32[]{:S(2)}) %collective-permute-start.15) | collective-permute-done | bytes 655392 | tf_op jit(solution)/shard_map/ppermute | solution.py:25
  40.1 2.0 %collective-permute-start.16 = (f32[320,256]{1,0:T(8,128)S(1)}, f32[320,256]{1,0:T(8,128)S(1)}, u32[]{:S(2)}, u32[]{:S(2)}) collective-permute-start(f32[320,256]{1,0:T(8,128)S(1)} %constant_dynamic-slice_fusion.3), channel_id=1, source_target_pairs={{0,4},{4,0},{8,12},{12,8},{16,20},{20,16},{24,28},{28,24},{1,5},{5... | collective-permute-start | bytes 983048 | tf_op jit(solution)/shard_map/ppermute | solution.py:25
  44.1 5.9 %collective-permute-done.16 = f32[320,256]{1,0:T(8,128)S(1)} collective-permute-done((f32[320,256]{1,0:T(8,128)S(1)}, f32[320,256]{1,0:T(8,128)S(1)}, u32[]{:S(2)}, u32[]{:S(2)}) %collective-permute-start.16) | collective-permute-done | bytes 327712 | tf_op jit(solution)/shard_map/ppermute | solution.py:25
  50.1 1.8 %collective-permute-start.17 = (f32[160,256]{1,0:T(8,128)S(1)}, f32[160,256]{1,0:T(8,128)S(1)}, u32[]{:S(2)}, u32[]{:S(2)}) collective-permute-start(f32[160,256]{1,0:T(8,128)S(1)} %constant_dynamic-slice_fusion.2), channel_id=1, source_target_pairs={{0,8},{4,12},{8,0},{12,4},{16,24},{20,28},{24,16},{28,20},{1,9},{5... | collective-permute-start | bytes 491528 | tf_op jit(solution)/shard_map/ppermute | solution.py:25
  53.7 2.1 %collective-permute-done.17 = f32[160,256]{1,0:T(8,128)S(1)} collective-permute-done((f32[160,256]{1,0:T(8,128)S(1)}, f32[160,256]{1,0:T(8,128)S(1)}, u32[]{:S(2)}, u32[]{:S(2)}) %collective-permute-start.17) | collective-permute-done | bytes 163872 | tf_op jit(solution)/shard_map/ppermute | solution.py:25
  55.8 1.6 %collective-permute-start.18 = (f32[80,256]{1,0:T(8,128)S(1)}, f32[80,256]{1,0:T(8,128)S(1)}, u32[]{:S(2)}, u32[]{:S(2)}) collective-permute-start(f32[80,256]{1,0:T(8,128)S(1)} %constant_dynamic-slice_fusion.1), channel_id=1, source_target_pairs={{0,2},{1,3},{2,0},{3,1},{4,6},{5,7},{6,4},{7,5},{8,10},{9,11},{10,... | collective-permute-start | bytes 245768 | tf_op jit(solution)/shard_map/ppermute | solution.py:25
  57.4 6.7 %collective-permute-done.6 = f32[81,1280]{1,0:T(8,128)S(1)} collective-permute-done((f32[81,1280]{1,0:T(8,128)S(1)}, f32[81,1280]{1,0:T(8,128)S(1)}, u32[]{:S(2)}, u32[]{:S(2)}) %collective-permute-start.6) | collective-permute-done | bytes 414752 | tf_op jit(solution)/shard_map/ppermute | solution.py:25
  64.3 1.6 %collective-permute-start.7 = (f32[41,1280]{1,0:T(8,128)S(1)}, f32[41,1280]{1,0:T(8,128)S(1)}, u32[]{:S(2)}, u32[]{:S(2)}) collective-permute-start(f32[41,1280]{1,0:T(8,128)S(1)} %pad_maximum_fusion.6), channel_id=1, source_target_pairs={{0,4},{4,0},{8,12},{12,8},{16,20},{20,16},{24,28},{28,24},{1,5},{5... | collective-permute-start | bytes 629768 | tf_op jit(solution)/shard_map/ppermute | solution.py:25
  65.9 4.6 %collective-permute-done.7 = f32[41,1280]{1,0:T(8,128)S(1)} collective-permute-done((f32[41,1280]{1,0:T(8,128)S(1)}, f32[41,1280]{1,0:T(8,128)S(1)}, u32[]{:S(2)}, u32[]{:S(2)}) %collective-permute-start.7) | collective-permute-done | bytes 209952 | tf_op jit(solution)/shard_map/ppermute | solution.py:25
  71.3 2.5 %collective-permute-start.19 = (f32[40,256]{1,0:T(8,128)S(1)}, f32[40,256]{1,0:T(8,128)S(1)}, u32[]{:S(2)}, u32[]{:S(2)}) collective-permute-start(f32[40,256]{1,0:T(8,128)S(1)} %constant_dynamic-slice_fusion), channel_id=1, source_target_pairs={{0,16},{4,20},{8,24},{12,28},{16,0},{20,4},{24,8},{28,12},{1,17},{... | collective-permute-start | bytes 122888 | tf_op jit(solution)/shard_map/ppermute | solution.py:25
  74.0 2.9 %collective-permute-done.8 = f32[42,640]{1,0:T(8,128)S(1)} collective-permute-done((f32[42,640]{1,0:T(8,128)S(1)}, f32[42,640]{1,0:T(8,128)S(1)}, u32[]{:S(2)}, u32[]{:S(2)}) %collective-permute-start.8) | collective-permute-done | bytes 107552 | tf_op jit(solution)/shard_map/ppermute | solution.py:25
  77.1 2.0 %collective-permute-start.9 = (f32[44,320]{1,0:T(8,128)S(1)}, f32[44,320]{1,0:T(8,128)S(1)}, u32[]{:S(2)}, u32[]{:S(2)}) collective-permute-start(f32[44,320]{1,0:T(8,128)S(1)} %pad_maximum_fusion.8), channel_id=1, source_target_pairs={{0,16},{4,20},{8,24},{12,28},{16,0},{20,4},{24,8},{28,12},{1,17},{... | collective-permute-start | bytes 168968 | tf_op jit(solution)/shard_map/ppermute | solution.py:25
  80.2 2.3 %collective-permute-done.9 = f32[44,320]{1,0:T(8,128)S(1)} collective-permute-done((f32[44,320]{1,0:T(8,128)S(1)}, f32[44,320]{1,0:T(8,128)S(1)}, u32[]{:S(2)}, u32[]{:S(2)}) %collective-permute-start.9) | collective-permute-done | bytes 56352 | tf_op jit(solution)/shard_map/ppermute | solution.py:25
  82.6 2.0 %collective-permute-start.10 = (f32[40,320]{1,0:T(8,128)S(1)}, f32[40,320]{1,0:T(8,128)S(1)}, u32[]{:S(2)}, u32[]{:S(2)}) collective-permute-start(f32[40,320]{1,0:T(8,128)S(1)} %slice_add_fusion.4), channel_id=1, source_target_pairs={{0,16},{4,20},{8,24},{12,28},{16,0},{20,4},{24,8},{28,12},{1,17},{... | collective-permute-start | bytes 153608 | tf_op jit(solution)/shard_map/ppermute | solution.py:25
  84.6 1.6 %collective-permute-start.21 = (f32[80,256]{1,0:T(8,128)S(1)}, f32[80,256]{1,0:T(8,128)S(1)}, u32[]{:S(2)}, u32[]{:S(2)}) collective-permute-start(f32[80,256]{1,0:T(8,128)S(1)} %maximum_select_fusion.16), channel_id=1, source_target_pairs={{0,2},{1,3},{2,0},{3,1},{4,6},{5,7},{6,4},{7,5},{8,10},{9,11},{10,... | collective-permute-start | bytes 245768 | tf_op jit(solution)/shard_map/ppermute | solution.py:25
  86.1 2.0 %collective-permute-done.10 = f32[40,320]{1,0:T(8,128)S(1)} collective-permute-done((f32[40,320]{1,0:T(8,128)S(1)}, f32[40,320]{1,0:T(8,128)S(1)}, u32[]{:S(2)}, u32[]{:S(2)}) %collective-permute-start.10) | collective-permute-done | bytes 51232 | tf_op jit(solution)/shard_map/ppermute | solution.py:25
  90.4 2.5 %collective-permute-done.11 = f32[40,640]{1,0:T(8,128)S(1)} collective-permute-done((f32[40,640]{1,0:T(8,128)S(1)}, f32[40,640]{1,0:T(8,128)S(1)}, u32[]{:S(2)}, u32[]{:S(2)}) %collective-permute-start.11) | collective-permute-done | bytes 102432 | tf_op jit(solution)/shard_map/ppermute | solution.py:25
  96.1 2.6 %collective-permute-done.12 = f32[40,1280]{1,0:T(8,128)S(1)} collective-permute-done((f32[40,1280]{1,0:T(8,128)S(1)}, f32[40,1280]{1,0:T(8,128)S(1)}, u32[]{:S(2)}, u32[]{:S(2)}) %collective-permute-start.12) | collective-permute-done | bytes 204832 | tf_op jit(solution)/shard_map/ppermute | solution.py:25
  100.2 2.1 %collective-permute-done.23 = f32[320,256]{1,0:T(8,128)S(1)} collective-permute-done((f32[320,256]{1,0:T(8,128)S(1)}, f32[320,256]{1,0:T(8,128)S(1)}, u32[]{:S(2)}, u32[]{:S(2)}) %collective-permute-start.23) | collective-permute-done | bytes 327712 | tf_op jit(solution)/shard_map/ppermute | solution.py:25
  102.4 4.4 %collective-permute-done.13 = f32[80,1280]{1,0:T(8,128)S(1)} collective-permute-done((f32[80,1280]{1,0:T(8,128)S(1)}, f32[80,1280]{1,0:T(8,128)S(1)}, u32[]{:S(2)}, u32[]{:S(2)}) %collective-permute-start.13) | collective-permute-done | bytes 409632 | tf_op jit(solution)/shard_map/ppermute | solution.py:25
  108.4 2.5 %maximum_select_fusion.1 = f32[1280,256]{1,0:T(8,128)} fusion(f32[640,256]{1,0:T(8,128)S(1)} %maximum_select_fusion.3, f32[640,256]{1,0:T(8,128)} %collective-permute-done.24, pred[]{:T(512)S(6)} %ne.10), kind=kLoop, calls=%fused_computation.18 | loop fusion | flops 983040 | bytes 2621441 | tf_op jit(solution)/shard_map/jit(_where)/select_n | solution.py:93
  (110 shorter events, 23.3 us)
Async XLA Ops:
  0.6 5.0 %copy-start = (bf16[1280,256]{1,0:T(8,128)(2,1)S(1)}, bf16[1280,256]{1,0:T(8,128)(2,1)}, u32[]{:S(2)}) copy-start(bf16[1280,256]{1,0:T(8,128)(2,1)} %param.7) | copy-start | bytes 1966084
  7.0 5.9 %collective-permute-start = (bf16[1,40,256]{2,1,0:T(8,128)(2,1)S(1)}, bf16[1,40,256]{2,1,0:T(8,128)(2,1)S(1)}, u32[]{:S(2)}, u32[]{:S(2)}) collective-permute-start(bf16[1,40,256]{2,1,0:T(8,128)(2,1)S(1)} %fusion.48), channel_id=1, source_target_pairs={{0,16},{4,20},{8,24},{12,28},{16,0},{20,4},{24,8},{28,12},{1,17},{... | collective-permute-start | bytes 61448 | tf_op jit(solution)/shard_map/ppermute | solution.py:25
  12.9 4.1 %collective-permute-start.1 = (bf16[2,1,40,256]{3,2,0,1:T(8,128)(2,1)S(1)}, bf16[2,1,40,256]{3,2,0,1:T(8,128)(2,1)S(1)}, u32[]{:S(2)}, u32[]{:S(2)}) collective-permute-start(bf16[2,1,40,256]{3,2,0,1:T(8,128)(2,1)S(1)} %maximum_select_fusion.17), channel_id=1, source_target_pairs={{0,8},{4,12},{8,0},{12,4},{16,24},{20,28},{24,16},{28,20},{1,9},{5... | collective-permute-start | bytes 122888 | tf_op jit(solution)/shard_map/ppermute | solution.py:25
  17.0 4.5 %collective-permute-start.2 = (bf16[2,2,1,40,256]{4,3,1,0,2:T(8,128)(2,1)S(1)}, bf16[2,2,1,40,256]{4,3,1,0,2:T(8,128)(2,1)S(1)}, u32[]{:S(2)}, u32[]{:S(2)}) collective-permute-start(bf16[2,2,1,40,256]{4,3,1,0,2:T(8,128)(2,1)S(1)} %maximum_select_fusion.14), channel_id=1, source_target_pairs={{0,4},{4,0},{8,12},{12,8},{16,20},{20,16},{24,28},{28,24},{1,5},{5... | collective-permute-start | bytes 245768 | tf_op jit(solution)/shard_map/ppermute | solution.py:25
  21.5 5.4 %collective-permute-start.3 = (bf16[2,2,2,1,40,256]{5,4,2,1,0,3:T(8,128)(2,1)S(1)}, bf16[2,2,2,1,40,256]{5,4,2,1,0,3:T(8,128)(2,1)S(1)}, u32[]{:S(2)}, u32[]{:S(2)}) collective-permute-start(bf16[2,2,2,1,40,256]{5,4,2,1,0,3:T(8,128)(2,1)S(1)} %maximum_select_fusion.10), channel_id=1, source_target_pairs={{0,2},{1,3},{2,0},{3,1},{4,6},{5,7},{6,4},{7,5},{8,10},{9,11},{10,... | collective-permute-start | bytes 491528 | tf_op jit(solution)/shard_map/ppermute | solution.py:25
  27.0 1.7 %collective-permute-start.4 = (bf16[2,2,2,2,1,40,256]{6,5,3,2,1,4,0:T(8,128)(2,1)S(1)}, bf16[2,2,2,2,1,40,256]{6,5,3,2,1,4,0:T(8,128)(2,1)S(1)}, u32[]{:S(2)}, u32[]{:S(2)}) collective-permute-start(bf16[2,2,2,2,1,40,256]{6,5,3,2,1,4,0:T(8,128)(2,1)S(1)} %maximum_select_fusion.5), channel_id=1, source_target_pairs={{0,1},{1,0},{2,3},{3,2},{4,5},{5,4},{6,7},{7,6},{8,9},{9,8},{10,11... | collective-permute-start | bytes 983048 | tf_op jit(solution)/shard_map/ppermute | solution.py:25
  31.3 1.8 %copy-start.5 = (bf16[40,1280]{1,0:T(8,128)(2,1)S(1)}, bf16[40,1280]{1,0:T(8,128)(2,1)}, u32[]{:S(2)}) copy-start(bf16[40,1280]{1,0:T(8,128)(2,1)} %shard_map.75) | copy-start | bytes 307204
  32.0 1.5 %copy-start.3 = (bf16[320,1280]{1,0:T(8,128)(2,1)S(1)}, bf16[320,1280]{1,0:T(8,128)(2,1)}, u32[]{:S(2)}) copy-start(bf16[320,1280]{1,0:T(8,128)(2,1)} %w_ref.1) | copy-start | bytes 2457604
  32.1 1.5 %copy-start.6 = (f32[1280]{0:T(1024)S(1)}, f32[1280]{0:T(1024)}, u32[]{:S(2)}) copy-start(f32[1280]{0:T(1024)} %shift_ref.1) | copy-start | bytes 15364
  32.7 1.1 copy-start.4
  36.6 1.4 %copy-start.1 = (f32[1280,320]{0,1:T(8,128)}, f32[1280,320]{0,1:T(8,128)S(1)}, u32[]{:S(2)}) copy-start(f32[1280,320]{0,1:T(8,128)S(1)} %fusion.32) | copy-start | bytes 4915204
  37.6 2.3 %collective-permute-start.15 = (f32[640,256]{1,0:T(8,128)}, f32[640,256]{1,0:T(8,128)S(1)}, u32[]{:S(2)}, u32[]{:S(2)}) collective-permute-start(f32[640,256]{1,0:T(8,128)} %constant_dynamic-slice_fusion.4), channel_id=1, source_target_pairs={{0,1},{1,0},{2,3},{3,2},{4,5},{5,4},{6,7},{7,6},{8,9},{9,8},{10,11... | collective-permute-start | bytes 1966088 | tf_op jit(solution)/shard_map/ppermute | solution.py:25
  38.0 4.1 %collective-permute-start.5 = (f32[161,1280]{1,0:T(8,128)S(1)}, f32[161,1280]{1,0:T(8,128)}, u32[]{:S(2)}, u32[]{:S(2)}) collective-permute-start(f32[161,1280]{1,0:T(8,128)S(1)} %pad_maximum_fusion), channel_id=1, source_target_pairs={{0,1},{1,0},{2,3},{3,2},{4,5},{5,4},{6,7},{7,6},{8,9},{9,8},{10,11... | collective-permute-start | bytes 2472968 | tf_op jit(solution)/shard_map/ppermute | solution.py:25
  38.3 3.7 %copy-start.2 = (f32[1280,320]{0,1:T(8,128)S(1)}, f32[1280,320]{0,1:T(8,128)}, u32[]{:S(2)}) copy-start(f32[1280,320]{0,1:T(8,128)} %copy-done.1) | copy-start | bytes 4915204
  40.1 10.0 %collective-permute-start.16 = (f32[320,256]{1,0:T(8,128)S(1)}, f32[320,256]{1,0:T(8,128)S(1)}, u32[]{:S(2)}, u32[]{:S(2)}) collective-permute-start(f32[320,256]{1,0:T(8,128)S(1)} %constant_dynamic-slice_fusion.3), channel_id=1, source_target_pairs={{0,4},{4,0},{8,12},{12,8},{16,20},{20,16},{24,28},{28,24},{1,5},{5... | collective-permute-start | bytes 983048 | tf_op jit(solution)/shard_map/ppermute | solution.py:25
  50.1 5.6 %collective-permute-start.17 = (f32[160,256]{1,0:T(8,128)S(1)}, f32[160,256]{1,0:T(8,128)S(1)}, u32[]{:S(2)}, u32[]{:S(2)}) collective-permute-start(f32[160,256]{1,0:T(8,128)S(1)} %constant_dynamic-slice_fusion.2), channel_id=1, source_target_pairs={{0,8},{4,12},{8,0},{12,4},{16,24},{20,28},{24,16},{28,20},{1,9},{5... | collective-permute-start | bytes 491528 | tf_op jit(solution)/shard_map/ppermute | solution.py:25
  51.9 12.2 %collective-permute-start.6 = (f32[81,1280]{1,0:T(8,128)S(1)}, f32[81,1280]{1,0:T(8,128)S(1)}, u32[]{:S(2)}, u32[]{:S(2)}) collective-permute-start(f32[81,1280]{1,0:T(8,128)S(1)} %pad_maximum_fusion.5), channel_id=1, source_target_pairs={{0,2},{1,3},{2,0},{3,1},{4,6},{5,7},{6,4},{7,5},{8,10},{9,11},{10,... | collective-permute-start | bytes 1244168 | tf_op jit(solution)/shard_map/ppermute | solution.py:25
  55.8 10.0 %collective-permute-start.18 = (f32[80,256]{1,0:T(8,128)S(1)}, f32[80,256]{1,0:T(8,128)S(1)}, u32[]{:S(2)}, u32[]{:S(2)}) collective-permute-start(f32[80,256]{1,0:T(8,128)S(1)} %constant_dynamic-slice_fusion.1), channel_id=1, source_target_pairs={{0,2},{1,3},{2,0},{3,1},{4,6},{5,7},{6,4},{7,5},{8,10},{9,11},{10,... | collective-permute-start | bytes 245768 | tf_op jit(solution)/shard_map/ppermute | solution.py:25
  64.3 6.3 %collective-permute-start.7 = (f32[41,1280]{1,0:T(8,128)S(1)}, f32[41,1280]{1,0:T(8,128)S(1)}, u32[]{:S(2)}, u32[]{:S(2)}) collective-permute-start(f32[41,1280]{1,0:T(8,128)S(1)} %pad_maximum_fusion.6), channel_id=1, source_target_pairs={{0,4},{4,0},{8,12},{12,8},{16,20},{20,16},{24,28},{28,24},{1,5},{5... | collective-permute-start | bytes 629768 | tf_op jit(solution)/shard_map/ppermute | solution.py:25
  70.7 6.2 %collective-permute-start.8 = (f32[42,640]{1,0:T(8,128)S(1)}, f32[42,640]{1,0:T(8,128)S(1)}, u32[]{:S(2)}, u32[]{:S(2)}) collective-permute-start(f32[42,640]{1,0:T(8,128)S(1)} %pad_maximum_fusion.7), channel_id=1, source_target_pairs={{0,8},{4,12},{8,0},{12,4},{16,24},{20,28},{24,16},{28,20},{1,9},{5... | collective-permute-start | bytes 322568 | tf_op jit(solution)/shard_map/ppermute | solution.py:25
  71.3 7.8 %collective-permute-start.19 = (f32[40,256]{1,0:T(8,128)S(1)}, f32[40,256]{1,0:T(8,128)S(1)}, u32[]{:S(2)}, u32[]{:S(2)}) collective-permute-start(f32[40,256]{1,0:T(8,128)S(1)} %constant_dynamic-slice_fusion), channel_id=1, source_target_pairs={{0,16},{4,20},{8,24},{12,28},{16,0},{20,4},{24,8},{28,12},{1,17},{... | collective-permute-start | bytes 122888 | tf_op jit(solution)/shard_map/ppermute | solution.py:25
  77.1 5.4 %collective-permute-start.9 = (f32[44,320]{1,0:T(8,128)S(1)}, f32[44,320]{1,0:T(8,128)S(1)}, u32[]{:S(2)}, u32[]{:S(2)}) collective-permute-start(f32[44,320]{1,0:T(8,128)S(1)} %pad_maximum_fusion.8), channel_id=1, source_target_pairs={{0,16},{4,20},{8,24},{12,28},{16,0},{20,4},{24,8},{28,12},{1,17},{... | collective-permute-start | bytes 168968 | tf_op jit(solution)/shard_map/ppermute | solution.py:25
  79.1 5.5 %collective-permute-start.20 = (f32[40,256]{1,0:T(8,128)S(1)}, f32[40,256]{1,0:T(8,128)S(1)}, u32[]{:S(2)}, u32[]{:S(2)}) collective-permute-start(f32[40,256]{1,0:T(8,128)S(1)} %dynamic-slice_add_fusion.4), channel_id=1, source_target_pairs={{0,16},{4,20},{8,24},{12,28},{16,0},{20,4},{24,8},{28,12},{1,17},{... | collective-permute-start | bytes 122888 | tf_op jit(solution)/shard_map/ppermute | solution.py:25
  82.6 5.5 %collective-permute-start.10 = (f32[40,320]{1,0:T(8,128)S(1)}, f32[40,320]{1,0:T(8,128)S(1)}, u32[]{:S(2)}, u32[]{:S(2)}) collective-permute-start(f32[40,320]{1,0:T(8,128)S(1)} %slice_add_fusion.4), channel_id=1, source_target_pairs={{0,16},{4,20},{8,24},{12,28},{16,0},{20,4},{24,8},{28,12},{1,17},{... | collective-permute-start | bytes 153608 | tf_op jit(solution)/shard_map/ppermute | solution.py:25
  84.6 4.5 %collective-permute-start.21 = (f32[80,256]{1,0:T(8,128)S(1)}, f32[80,256]{1,0:T(8,128)S(1)}, u32[]{:S(2)}, u32[]{:S(2)}) collective-permute-start(f32[80,256]{1,0:T(8,128)S(1)} %maximum_select_fusion.16), channel_id=1, source_target_pairs={{0,2},{1,3},{2,0},{3,1},{4,6},{5,7},{6,4},{7,5},{8,10},{9,11},{10,... | collective-permute-start | bytes 245768 | tf_op jit(solution)/shard_map/ppermute | solution.py:25
  88.2 4.7 %collective-permute-start.11 = (f32[40,640]{1,0:T(8,128)S(1)}, f32[40,640]{1,0:T(8,128)S(1)}, u32[]{:S(2)}, u32[]{:S(2)}) collective-permute-start(f32[40,640]{1,0:T(8,128)S(1)} %maximum_select_fusion.13), channel_id=1, source_target_pairs={{0,8},{4,12},{8,0},{12,4},{16,24},{20,28},{24,16},{28,20},{1,9},{5... | collective-permute-start | bytes 307208 | tf_op jit(solution)/shard_map/ppermute | solution.py:25
  89.1 5.6 %collective-permute-start.22 = (f32[160,256]{1,0:T(8,128)S(1)}, f32[160,256]{1,0:T(8,128)S(1)}, u32[]{:S(2)}, u32[]{:S(2)}) collective-permute-start(f32[160,256]{1,0:T(8,128)S(1)} %maximum_select_fusion.12), channel_id=1, source_target_pairs={{0,8},{4,12},{8,0},{12,4},{16,24},{20,28},{24,16},{28,20},{1,9},{5... | collective-permute-start | bytes 491528 | tf_op jit(solution)/shard_map/ppermute | solution.py:25
  93.0 5.8 %collective-permute-start.12 = (f32[40,1280]{1,0:T(8,128)S(1)}, f32[40,1280]{1,0:T(8,128)S(1)}, u32[]{:S(2)}, u32[]{:S(2)}) collective-permute-start(f32[40,1280]{1,0:T(8,128)S(1)} %maximum_select_fusion.9), channel_id=1, source_target_pairs={{0,4},{4,0},{8,12},{12,8},{16,20},{20,16},{24,28},{28,24},{1,5},{5... | collective-permute-start | bytes 614408 | tf_op jit(solution)/shard_map/ppermute | solution.py:25
  94.7 7.6 %collective-permute-start.23 = (f32[320,256]{1,0:T(8,128)S(1)}, f32[320,256]{1,0:T(8,128)S(1)}, u32[]{:S(2)}, u32[]{:S(2)}) collective-permute-start(f32[320,256]{1,0:T(8,128)S(1)} %maximum_select_fusion.8), channel_id=1, source_target_pairs={{0,4},{4,0},{8,12},{12,8},{16,20},{20,16},{24,28},{28,24},{1,5},{5... | collective-permute-start | bytes 983048 | tf_op jit(solution)/shard_map/ppermute | solution.py:25
  98.8 8.0 %collective-permute-start.13 = (f32[80,1280]{1,0:T(8,128)S(1)}, f32[80,1280]{1,0:T(8,128)S(1)}, u32[]{:S(2)}, u32[]{:S(2)}) collective-permute-start(f32[80,1280]{1,0:T(8,128)S(1)} %maximum_select_fusion.4), channel_id=1, source_target_pairs={{0,2},{1,3},{2,0},{3,1},{4,6},{5,7},{6,4},{7,5},{8,10},{9,11},{10,... | collective-permute-start | bytes 1228808 | tf_op jit(solution)/shard_map/ppermute | solution.py:25
  102.4 6.0 %collective-permute-start.24 = (f32[640,256]{1,0:T(8,128)S(1)}, f32[640,256]{1,0:T(8,128)}, u32[]{:S(2)}, u32[]{:S(2)}) collective-permute-start(f32[640,256]{1,0:T(8,128)S(1)} %maximum_select_fusion.3), channel_id=1, source_target_pairs={{0,1},{1,0},{2,3},{3,2},{4,5},{5,4},{6,7},{7,6},{8,9},{9,8},{10,11... | collective-permute-start | bytes 1966088 | tf_op jit(solution)/shard_map/ppermute | solution.py:25
  106.9 4.0 %collective-permute-start.14 = (f32[160,1280]{1,0:T(8,128)S(1)}, f32[160,1280]{1,0:T(8,128)S(1)}, u32[]{:S(2)}, u32[]{:S(2)}) collective-permute-start(f32[160,1280]{1,0:T(8,128)S(1)} %maximum_select_fusion.2), channel_id=1, source_target_pairs={{0,1},{1,0},{2,3},{3,2},{4,5},{5,4},{6,7},{7,6},{8,9},{9,8},{10,11... | collective-permute-start | bytes 2457608 | tf_op jit(solution)/shard_map/ppermute | solution.py:25

commit v7 on v6

--- a/solution.py
+++ b/solution.py
@@ -148,6 +148,9 @@
         images = feature_map.shape[0] // POS
         channels = head_weight.shape[1]
         pooled = pooled_of(feature_map, head_weight, head_shift)
+        pre = jnp.dot(feature_map, head_weight, preferred_element_type=jnp.float32) + head_shift
+        sig = jax.nn.sigmoid(pre)
+        factor = lax.optimization_barrier(sig * (1.0 + pre * (1.0 - sig)))
         proj = jnp.dot(pooled, proj_weight, preferred_element_type=jnp.float32)
         rnorm = jnp.sqrt(jnp.sum(proj * proj, axis=1, keepdims=True) + 1e-06)
         unit = proj / rnorm
@@ -177,9 +180,7 @@
         grad_act = jnp.broadcast_to(
             (grad_pooled / POS)[:, None, :], (images, POS, channels)
         ).reshape(images * POS, channels)
-        pre = jnp.dot(feature_map, head_weight, preferred_element_type=jnp.float32) + head_shift
-        sig = jax.nn.sigmoid(pre)
-        grad_pre = (grad_act * sig * (1.0 + pre * (1.0 - sig))).astype(jnp.bfloat16)
+        grad_pre = (grad_act * factor).astype(jnp.bfloat16)
         c_in = feature_map.shape[1]
         if steps:
             grad_proj = lax.dot_general(

time: 114 us -> 114 us (level)
  waiting for transfers between devices: 52 us -> 48.7 us
  other arithmetic: 7.92 us -> 10.3 us
  matrix products: 7.92 us -> 9.28 us
    ppermute x25, waiting for transfers between devices: 52 us -> 48.7 us  [swap(): return lax.ppermute(x, ax, [(i, i ^ mask) for i in range(mesh.shape[ax])])]
    reduce_sum x0 -> x1, other arithmetic: none -> 2.35 us  [body(): grad_shift = jnp.sum(grad_pre.astype(jnp.float32), axis=0)]
    dot_general x1, matrix products: 1.96 us -> 3.31 us  [body(): jnp.dot(feature_map, head_weight, preferred_element_type=jnp.float32)]
  transfers between devices with their start and end apart: 25 -> 25, of which waited for: 19 -> 19; matrix products, arithmetic and copies ran while one was open for 6% -> 9% of each run, Pallas kernels for 0% -> 0%
where the time goes in v7:
time: 114 us; the launch traced here: 113 us
  waiting for transfers between devices  48.7 us (43%)
  starting transfers between devices  34.5 us (30%)
  other arithmetic  10.3 us (9%)
  matrix products  9.28 us (8%)
  Pallas kernels  5.06 us (4%)
  between operations  3.59 us (3%)
  local copies, waits for them, and re-layouts  1.99 us (2%)
    ppermute x25, waiting for transfers between devices, swap(): return lax.ppermute(x, ax, [(i, i ^ mask) for i in range(mesh.shape[ax])])  48.7 us
    ppermute x25, starting transfers between devices, swap(): return lax.ppermute(x, ax, [(i, i ^ mask) for i in range(mesh.shape[ax])])  34.5 us
    pallas_call x1, Pallas kernels, pooled_of(): pl.pallas_call(pooled_kernel, out_shape=jax.ShapeDtypeStruct((rows // POS...  5.06 us
    select_n x10, other arithmetic, all_reduce(): jnp.where(my_bit(ax, mask), jnp.concatenate([g, c], axis=d), jnp.concaten...  4.13 us
    dot_general x1, matrix products, body(): jnp.dot(feature_map, head_weight, preferred_element_type=jnp.float32)  3.31 us
    dot_general x1, matrix products, pair_terms(): lax.dot_general(rows_z, piece, (((1,), (1,)), ((), ())), preferred_elemen...  2.5 us
    reduce_sum x1, other arithmetic, body(): grad_shift = jnp.sum(grad_pre.astype(jnp.float32), axis=0)  2.35 us
  transfers between devices with their start and end apart: 25, of which 19 were waited for; matrix products, arithmetic and copies ran while one was open for 9% of the time, Pallas kernels for 0%

profile of v7, /device:TPU:0, one launch (start us, length us, event | category | flops | bytes accessed | tf_op | source)
XLA Modules:
  0.0 113.4 jit_solution(5013648003158476942)
XLA Ops:
  0.7 5.1 %shard_map.75 = bf16[40,1280]{1,0:T(8,128)(2,1)} custom-call(bf16[320,640]{1,0:T(8,128)(2,1)} %bitcast.82, bf16[320,1280]{1,0:T(8,128)(2,1)} %w_ref.1, f32[1280]{0:T(1024)} %shift_ref.1), custom_call_target="tpu_custom_call" | custom-call | flops 524288000 | bytes 1336320 | tf_op jit(solution)/shard_map/pallas_call | solution.py:126
  7.1 4.1 %collective-permute-start = (bf16[1,40,256]{2,1,0:T(8,128)(2,1)S(1)}, bf16[1,40,256]{2,1,0:T(8,128)(2,1)S(1)}, u32[]{:S(2)}, u32[]{:S(2)}) collective-permute-start(bf16[1,40,256]{2,1,0:T(8,128)(2,1)S(1)} %fusion.48), channel_id=1, source_target_pairs={{0,16},{4,20},{8,24},{12,28},{16,0},{20,4},{24,8},{28,12},{1,17},{... | collective-permute-start | bytes 61448 | tf_op jit(solution)/shard_map/ppermute | solution.py:25
  11.4 1.6 %collective-permute-done = bf16[1,40,256]{2,1,0:T(8,128)(2,1)S(1)} collective-permute-done((bf16[1,40,256]{2,1,0:T(8,128)(2,1)S(1)}, bf16[1,40,256]{2,1,0:T(8,128)(2,1)S(1)}, u32[]{:S(2)}, u32[]{:S(2)}) %collective-permute-start) | collective-permute-done | bytes 20512 | tf_op jit(solution)/shard_map/ppermute | solution.py:25
  13.0 2.0 %collective-permute-start.1 = (bf16[2,1,40,256]{3,2,0,1:T(8,128)(2,1)S(1)}, bf16[2,1,40,256]{3,2,0,1:T(8,128)(2,1)S(1)}, u32[]{:S(2)}, u32[]{:S(2)}) collective-permute-start(bf16[2,1,40,256]{3,2,0,1:T(8,128)(2,1)S(1)} %maximum_select_fusion.17), channel_id=1, source_target_pairs={{0,8},{4,12},{8,0},{12,4},{16,24},{20,28},{24,16},{28,20},{1,9},{5... | collective-permute-start | bytes 122888 | tf_op jit(solution)/shard_map/ppermute | solution.py:25
  15.0 2.1 %collective-permute-done.1 = bf16[2,1,40,256]{3,2,0,1:T(8,128)(2,1)S(1)} collective-permute-done((bf16[2,1,40,256]{3,2,0,1:T(8,128)(2,1)S(1)}, bf16[2,1,40,256]{3,2,0,1:T(8,128)(2,1)S(1)}, u32[]{:S(2)}, u32[]{:S(2)}) %collective-permute-start.1) | collective-permute-done | bytes 40992 | tf_op jit(solution)/shard_map/ppermute | solution.py:25
  17.1 2.0 %collective-permute-start.2 = (bf16[2,2,1,40,256]{4,3,1,0,2:T(8,128)(2,1)S(1)}, bf16[2,2,1,40,256]{4,3,1,0,2:T(8,128)(2,1)S(1)}, u32[]{:S(2)}, u32[]{:S(2)}) collective-permute-start(bf16[2,2,1,40,256]{4,3,1,0,2:T(8,128)(2,1)S(1)} %maximum_select_fusion.14), channel_id=1, source_target_pairs={{0,4},{4,0},{8,12},{12,8},{16,20},{20,16},{24,28},{28,24},{1,5},{5... | collective-permute-start | bytes 245768 | tf_op jit(solution)/shard_map/ppermute | solution.py:25
  19.1 2.5 %collective-permute-done.2 = bf16[2,2,1,40,256]{4,3,1,0,2:T(8,128)(2,1)S(1)} collective-permute-done((bf16[2,2,1,40,256]{4,3,1,0,2:T(8,128)(2,1)S(1)}, bf16[2,2,1,40,256]{4,3,1,0,2:T(8,128)(2,1)S(1)}, u32[]{:S(2)}, u32[]{:S(2)}) %collective-permute-start.2) | collective-permute-done | bytes 81952 | tf_op jit(solution)/shard_map/ppermute | solution.py:25
  21.6 2.0 %collective-permute-start.3 = (bf16[2,2,2,1,40,256]{5,4,2,1,0,3:T(8,128)(2,1)S(1)}, bf16[2,2,2,1,40,256]{5,4,2,1,0,3:T(8,128)(2,1)S(1)}, u32[]{:S(2)}, u32[]{:S(2)}) collective-permute-start(bf16[2,2,2,1,40,256]{5,4,2,1,0,3:T(8,128)(2,1)S(1)} %maximum_select_fusion.10), channel_id=1, source_target_pairs={{0,2},{1,3},{2,0},{3,1},{4,6},{5,7},{6,4},{7,5},{8,10},{9,11},{10,... | collective-permute-start | bytes 491528 | tf_op jit(solution)/shard_map/ppermute | solution.py:25
  23.6 3.3 %add_multiply_fusion = f32[640,1280]{1,0:T(8,128)} fusion(bf16[640,320]{0,1:T(8,128)(2,1)S(1)} %copy-done.5, bf16[320,1280]{1,0:T(8,128)(2,1)S(1)} %copy-done.4, f32[1280]{0:T(1024)S(1)} %copy-done.6), kind=kOutput, calls=%fused_computation.9 | convolution fusion | flops 530841600 | bytes 4510720 | tf_op jit(solution)/shard_map/dot_general | solution.py:151
  28.9 2.5 %fusion.8 = f32[]{:T(128)} fusion(bf16[1280,256]{1,0:T(8,128)(2,1)S(1)} %bitcast.73), kind=kOutput, calls=%fused_computation.17 | convolution fusion | flops 847052800 | bytes 655364 | tf_op jit(solution)/shard_map/dot_general | solution.py:105
  33.6 2.4 %convert_reduce_fusion = (f32[1280]{0:T(1024)S(1)}, bf16[640,1280]{1,0:T(8,128)(2,1)S(1)}) fusion(f32[640,1280]{1,0:T(8,128)} %add_multiply_fusion, f32[40,1280]{1,0:T(8,128)S(1)} %convolution_multiply_fusion), kind=kLoop, calls=%fused_computation.8 | loop fusion | flops 3275520 | bytes 5125120 | tf_op jit(solution)/shard_map/reduce_sum | solution.py:189
  38.4 1.6 %collective-permute-done.15 = f32[640,256]{1,0:T(8,128)S(1)} collective-permute-done((f32[640,256]{1,0:T(8,128)}, f32[640,256]{1,0:T(8,128)S(1)}, u32[]{:S(2)}, u32[]{:S(2)}) %collective-permute-start.15) | collective-permute-done | bytes 655392 | tf_op jit(solution)/shard_map/ppermute | solution.py:25
  40.1 2.0 %collective-permute-start.16 = (f32[320,256]{1,0:T(8,128)S(1)}, f32[320,256]{1,0:T(8,128)S(1)}, u32[]{:S(2)}, u32[]{:S(2)}) collective-permute-start(f32[320,256]{1,0:T(8,128)S(1)} %constant_dynamic-slice_fusion.3), channel_id=1, source_target_pairs={{0,4},{4,0},{8,12},{12,8},{16,20},{20,16},{24,28},{28,24},{1,5},{5... | collective-permute-start | bytes 983048 | tf_op jit(solution)/shard_map/ppermute | solution.py:25
  44.2 5.9 %collective-permute-done.16 = f32[320,256]{1,0:T(8,128)S(1)} collective-permute-done((f32[320,256]{1,0:T(8,128)S(1)}, f32[320,256]{1,0:T(8,128)S(1)}, u32[]{:S(2)}, u32[]{:S(2)}) %collective-permute-start.16) | collective-permute-done | bytes 327712 | tf_op jit(solution)/shard_map/ppermute | solution.py:25
  50.2 1.8 %collective-permute-start.17 = (f32[160,256]{1,0:T(8,128)S(1)}, f32[160,256]{1,0:T(8,128)S(1)}, u32[]{:S(2)}, u32[]{:S(2)}) collective-permute-start(f32[160,256]{1,0:T(8,128)S(1)} %constant_dynamic-slice_fusion.2), channel_id=1, source_target_pairs={{0,8},{4,12},{8,0},{12,4},{16,24},{20,28},{24,16},{28,20},{1,9},{5... | collective-permute-start | bytes 491528 | tf_op jit(solution)/shard_map/ppermute | solution.py:25
  52.0 1.6 %collective-permute-start.6 = (f32[81,1280]{1,0:T(8,128)S(1)}, f32[81,1280]{1,0:T(8,128)S(1)}, u32[]{:S(2)}, u32[]{:S(2)}) collective-permute-start(f32[81,1280]{1,0:T(8,128)S(1)} %pad_maximum_fusion.5), channel_id=1, source_target_pairs={{0,2},{1,3},{2,0},{3,1},{4,6},{5,7},{6,4},{7,5},{8,10},{9,11},{10,... | collective-permute-start | bytes 1244168 | tf_op jit(solution)/shard_map/ppermute | solution.py:25
  53.8 2.1 %collective-permute-done.17 = f32[160,256]{1,0:T(8,128)S(1)} collective-permute-done((f32[160,256]{1,0:T(8,128)S(1)}, f32[160,256]{1,0:T(8,128)S(1)}, u32[]{:S(2)}, u32[]{:S(2)}) %collective-permute-start.17) | collective-permute-done | bytes 163872 | tf_op jit(solution)/shard_map/ppermute | solution.py:25
  55.9 1.6 %collective-permute-start.18 = (f32[80,256]{1,0:T(8,128)S(1)}, f32[80,256]{1,0:T(8,128)S(1)}, u32[]{:S(2)}, u32[]{:S(2)}) collective-permute-start(f32[80,256]{1,0:T(8,128)S(1)} %constant_dynamic-slice_fusion.1), channel_id=1, source_target_pairs={{0,2},{1,3},{2,0},{3,1},{4,6},{5,7},{6,4},{7,5},{8,10},{9,11},{10,... | collective-permute-start | bytes 245768 | tf_op jit(solution)/shard_map/ppermute | solution.py:25
  57.5 6.7 %collective-permute-done.6 = f32[81,1280]{1,0:T(8,128)S(1)} collective-permute-done((f32[81,1280]{1,0:T(8,128)S(1)}, f32[81,1280]{1,0:T(8,128)S(1)}, u32[]{:S(2)}, u32[]{:S(2)}) %collective-permute-start.6) | collective-permute-done | bytes 414752 | tf_op jit(solution)/shard_map/ppermute | solution.py:25
  64.4 1.6 %collective-permute-start.7 = (f32[41,1280]{1,0:T(8,128)S(1)}, f32[41,1280]{1,0:T(8,128)S(1)}, u32[]{:S(2)}, u32[]{:S(2)}) collective-permute-start(f32[41,1280]{1,0:T(8,128)S(1)} %pad_maximum_fusion.6), channel_id=1, source_target_pairs={{0,4},{4,0},{8,12},{12,8},{16,20},{20,16},{24,28},{28,24},{1,5},{5... | collective-permute-start | bytes 629768 | tf_op jit(solution)/shard_map/ppermute | solution.py:25
  66.0 4.6 %collective-permute-done.7 = f32[41,1280]{1,0:T(8,128)S(1)} collective-permute-done((f32[41,1280]{1,0:T(8,128)S(1)}, f32[41,1280]{1,0:T(8,128)S(1)}, u32[]{:S(2)}, u32[]{:S(2)}) %collective-permute-start.7) | collective-permute-done | bytes 209952 | tf_op jit(solution)/shard_map/ppermute | solution.py:25
  71.4 2.5 %collective-permute-start.19 = (f32[40,256]{1,0:T(8,128)S(1)}, f32[40,256]{1,0:T(8,128)S(1)}, u32[]{:S(2)}, u32[]{:S(2)}) collective-permute-start(f32[40,256]{1,0:T(8,128)S(1)} %constant_dynamic-slice_fusion), channel_id=1, source_target_pairs={{0,16},{4,20},{8,24},{12,28},{16,0},{20,4},{24,8},{28,12},{1,17},{... | collective-permute-start | bytes 122888 | tf_op jit(solution)/shard_map/ppermute | solution.py:25
  74.0 2.9 %collective-permute-done.8 = f32[42,640]{1,0:T(8,128)S(1)} collective-permute-done((f32[42,640]{1,0:T(8,128)S(1)}, f32[42,640]{1,0:T(8,128)S(1)}, u32[]{:S(2)}, u32[]{:S(2)}) %collective-permute-start.8) | collective-permute-done | bytes 107552 | tf_op jit(solution)/shard_map/ppermute | solution.py:25
  77.2 2.0 %collective-permute-start.9 = (f32[44,320]{1,0:T(8,128)S(1)}, f32[44,320]{1,0:T(8,128)S(1)}, u32[]{:S(2)}, u32[]{:S(2)}) collective-permute-start(f32[44,320]{1,0:T(8,128)S(1)} %pad_maximum_fusion.8), channel_id=1, source_target_pairs={{0,16},{4,20},{8,24},{12,28},{16,0},{20,4},{24,8},{28,12},{1,17},{... | collective-permute-start | bytes 168968 | tf_op jit(solution)/shard_map/ppermute | solution.py:25
  80.2 2.3 %collective-permute-done.9 = f32[44,320]{1,0:T(8,128)S(1)} collective-permute-done((f32[44,320]{1,0:T(8,128)S(1)}, f32[44,320]{1,0:T(8,128)S(1)}, u32[]{:S(2)}, u32[]{:S(2)}) %collective-permute-start.9) | collective-permute-done | bytes 56352 | tf_op jit(solution)/shard_map/ppermute | solution.py:25
  82.7 2.0 %collective-permute-start.10 = (f32[40,320]{1,0:T(8,128)S(1)}, f32[40,320]{1,0:T(8,128)S(1)}, u32[]{:S(2)}, u32[]{:S(2)}) collective-permute-start(f32[40,320]{1,0:T(8,128)S(1)} %slice_add_fusion.4), channel_id=1, source_target_pairs={{0,16},{4,20},{8,24},{12,28},{16,0},{20,4},{24,8},{28,12},{1,17},{... | collective-permute-start | bytes 153608 | tf_op jit(solution)/shard_map/ppermute | solution.py:25
  86.2 2.0 %collective-permute-done.10 = f32[40,320]{1,0:T(8,128)S(1)} collective-permute-done((f32[40,320]{1,0:T(8,128)S(1)}, f32[40,320]{1,0:T(8,128)S(1)}, u32[]{:S(2)}, u32[]{:S(2)}) %collective-permute-start.10) | collective-permute-done | bytes 51232 | tf_op jit(solution)/shard_map/ppermute | solution.py:25
  90.5 2.5 %collective-permute-done.11 = f32[40,640]{1,0:T(8,128)S(1)} collective-permute-done((f32[40,640]{1,0:T(8,128)S(1)}, f32[40,640]{1,0:T(8,128)S(1)}, u32[]{:S(2)}, u32[]{:S(2)}) %collective-permute-start.11) | collective-permute-done | bytes 102432 | tf_op jit(solution)/shard_map/ppermute | solution.py:25
  96.2 2.6 %collective-permute-done.12 = f32[40,1280]{1,0:T(8,128)S(1)} collective-permute-done((f32[40,1280]{1,0:T(8,128)S(1)}, f32[40,1280]{1,0:T(8,128)S(1)}, u32[]{:S(2)}, u32[]{:S(2)}) %collective-permute-start.12) | collective-permute-done | bytes 204832 | tf_op jit(solution)/shard_map/ppermute | solution.py:25
  100.3 2.1 %collective-permute-done.23 = f32[320,256]{1,0:T(8,128)S(1)} collective-permute-done((f32[320,256]{1,0:T(8,128)S(1)}, f32[320,256]{1,0:T(8,128)S(1)}, u32[]{:S(2)}, u32[]{:S(2)}) %collective-permute-start.23) | collective-permute-done | bytes 327712 | tf_op jit(solution)/shard_map/ppermute | solution.py:25
  102.5 4.4 %collective-permute-done.13 = f32[80,1280]{1,0:T(8,128)S(1)} collective-permute-done((f32[80,1280]{1,0:T(8,128)S(1)}, f32[80,1280]{1,0:T(8,128)S(1)}, u32[]{:S(2)}, u32[]{:S(2)}) %collective-permute-start.13) | collective-permute-done | bytes 409632 | tf_op jit(solution)/shard_map/ppermute | solution.py:25
  108.5 2.5 %maximum_select_fusion.1 = f32[1280,256]{1,0:T(8,128)} fusion(f32[640,256]{1,0:T(8,128)S(1)} %maximum_select_fusion.3, f32[640,256]{1,0:T(8,128)} %collective-permute-done.24, pred[]{:T(512)S(6)} %ne.10), kind=kLoop, calls=%fused_computation.18 | loop fusion | flops 983040 | bytes 2621441 | tf_op jit(solution)/shard_map/jit(_where)/select_n | solution.py:93
  (111 shorter events, 23.0 us)
Async XLA Ops:
  0.6 5.1 %copy-start = (bf16[1280,256]{1,0:T(8,128)(2,1)S(1)}, bf16[1280,256]{1,0:T(8,128)(2,1)}, u32[]{:S(2)}) copy-start(bf16[1280,256]{1,0:T(8,128)(2,1)} %param.7) | copy-start | bytes 1966084
  0.6 23.0 %copy-start.4 = (bf16[320,1280]{1,0:T(8,128)(2,1)S(1)}, bf16[320,1280]{1,0:T(8,128)(2,1)}, u32[]{:S(2)}) copy-start(bf16[320,1280]{1,0:T(8,128)(2,1)} %w_ref.1) | copy-start | bytes 2457604
  0.7 22.9 %copy-start.5 = (bf16[640,320]{0,1:T(8,128)(2,1)S(1)}, bf16[640,320]{0,1:T(8,128)(2,1)}, u32[]{:S(2)}) copy-start(bf16[640,320]{0,1:T(8,128)(2,1)} %param.4) | copy-start | bytes 1228804
  0.7 22.9 %copy-start.6 = (f32[1280]{0:T(1024)S(1)}, f32[1280]{0:T(1024)}, u32[]{:S(2)}) copy-start(f32[1280]{0:T(1024)} %shift_ref.1) | copy-start | bytes 15364
  7.1 5.9 %collective-permute-start = (bf16[1,40,256]{2,1,0:T(8,128)(2,1)S(1)}, bf16[1,40,256]{2,1,0:T(8,128)(2,1)S(1)}, u32[]{:S(2)}, u32[]{:S(2)}) collective-permute-start(bf16[1,40,256]{2,1,0:T(8,128)(2,1)S(1)} %fusion.48), channel_id=1, source_target_pairs={{0,16},{4,20},{8,24},{12,28},{16,0},{20,4},{24,8},{28,12},{1,17},{... | collective-permute-start | bytes 61448 | tf_op jit(solution)/shard_map/ppermute | solution.py:25
  13.0 4.1 %collective-permute-start.1 = (bf16[2,1,40,256]{3,2,0,1:T(8,128)(2,1)S(1)}, bf16[2,1,40,256]{3,2,0,1:T(8,128)(2,1)S(1)}, u32[]{:S(2)}, u32[]{:S(2)}) collective-permute-start(bf16[2,1,40,256]{3,2,0,1:T(8,128)(2,1)S(1)} %maximum_select_fusion.17), channel_id=1, source_target_pairs={{0,8},{4,12},{8,0},{12,4},{16,24},{20,28},{24,16},{28,20},{1,9},{5... | collective-permute-start | bytes 122888 | tf_op jit(solution)/shard_map/ppermute | solution.py:25
  17.1 4.5 %collective-permute-start.2 = (bf16[2,2,1,40,256]{4,3,1,0,2:T(8,128)(2,1)S(1)}, bf16[2,2,1,40,256]{4,3,1,0,2:T(8,128)(2,1)S(1)}, u32[]{:S(2)}, u32[]{:S(2)}) collective-permute-start(bf16[2,2,1,40,256]{4,3,1,0,2:T(8,128)(2,1)S(1)} %maximum_select_fusion.14), channel_id=1, source_target_pairs={{0,4},{4,0},{8,12},{12,8},{16,20},{20,16},{24,28},{28,24},{1,5},{5... | collective-permute-start | bytes 245768 | tf_op jit(solution)/shard_map/ppermute | solution.py:25
  21.6 5.4 %collective-permute-start.3 = (bf16[2,2,2,1,40,256]{5,4,2,1,0,3:T(8,128)(2,1)S(1)}, bf16[2,2,2,1,40,256]{5,4,2,1,0,3:T(8,128)(2,1)S(1)}, u32[]{:S(2)}, u32[]{:S(2)}) collective-permute-start(bf16[2,2,2,1,40,256]{5,4,2,1,0,3:T(8,128)(2,1)S(1)} %maximum_select_fusion.10), channel_id=1, source_target_pairs={{0,2},{1,3},{2,0},{3,1},{4,6},{5,7},{6,4},{7,5},{8,10},{9,11},{10,... | collective-permute-start | bytes 491528 | tf_op jit(solution)/shard_map/ppermute | solution.py:25
  27.0 1.7 %collective-permute-start.4 = (bf16[2,2,2,2,1,40,256]{6,5,3,2,1,4,0:T(8,128)(2,1)S(1)}, bf16[2,2,2,2,1,40,256]{6,5,3,2,1,4,0:T(8,128)(2,1)S(1)}, u32[]{:S(2)}, u32[]{:S(2)}) collective-permute-start(bf16[2,2,2,2,1,40,256]{6,5,3,2,1,4,0:T(8,128)(2,1)S(1)} %maximum_select_fusion.5), channel_id=1, source_target_pairs={{0,1},{1,0},{2,3},{3,2},{4,5},{5,4},{6,7},{7,6},{8,9},{9,8},{10,11... | collective-permute-start | bytes 983048 | tf_op jit(solution)/shard_map/ppermute | solution.py:25
  31.4 1.8 %copy-start.3 = (bf16[40,1280]{1,0:T(8,128)(2,1)S(1)}, bf16[40,1280]{1,0:T(8,128)(2,1)}, u32[]{:S(2)}) copy-start(bf16[40,1280]{1,0:T(8,128)(2,1)} %shard_map.75) | copy-start | bytes 307204
  36.7 1.4 %copy-start.1 = (f32[1280,320]{0,1:T(8,128)}, f32[1280,320]{0,1:T(8,128)S(1)}, u32[]{:S(2)}) copy-start(f32[1280,320]{0,1:T(8,128)S(1)} %fusion.32) | copy-start | bytes 4915204
  37.7 2.3 %collective-permute-start.15 = (f32[640,256]{1,0:T(8,128)}, f32[640,256]{1,0:T(8,128)S(1)}, u32[]{:S(2)}, u32[]{:S(2)}) collective-permute-start(f32[640,256]{1,0:T(8,128)} %constant_dynamic-slice_fusion.4), channel_id=1, source_target_pairs={{0,1},{1,0},{2,3},{3,2},{4,5},{5,4},{6,7},{7,6},{8,9},{9,8},{10,11... | collective-permute-start | bytes 1966088 | tf_op jit(solution)/shard_map/ppermute | solution.py:25
  38.1 4.0 %collective-permute-start.5 = (f32[161,1280]{1,0:T(8,128)S(1)}, f32[161,1280]{1,0:T(8,128)}, u32[]{:S(2)}, u32[]{:S(2)}) collective-permute-start(f32[161,1280]{1,0:T(8,128)S(1)} %pad_maximum_fusion), channel_id=1, source_target_pairs={{0,1},{1,0},{2,3},{3,2},{4,5},{5,4},{6,7},{7,6},{8,9},{9,8},{10,11... | collective-permute-start | bytes 2472968 | tf_op jit(solution)/shard_map/ppermute | solution.py:25
  38.4 3.7 %copy-start.2 = (f32[1280,320]{0,1:T(8,128)S(1)}, f32[1280,320]{0,1:T(8,128)}, u32[]{:S(2)}) copy-start(f32[1280,320]{0,1:T(8,128)} %copy-done.1) | copy-start | bytes 4915204
  40.1 10.0 %collective-permute-start.16 = (f32[320,256]{1,0:T(8,128)S(1)}, f32[320,256]{1,0:T(8,128)S(1)}, u32[]{:S(2)}, u32[]{:S(2)}) collective-permute-start(f32[320,256]{1,0:T(8,128)S(1)} %constant_dynamic-slice_fusion.3), channel_id=1, source_target_pairs={{0,4},{4,0},{8,12},{12,8},{16,20},{20,16},{24,28},{28,24},{1,5},{5... | collective-permute-start | bytes 983048 | tf_op jit(solution)/shard_map/ppermute | solution.py:25
  50.2 5.6 %collective-permute-start.17 = (f32[160,256]{1,0:T(8,128)S(1)}, f32[160,256]{1,0:T(8,128)S(1)}, u32[]{:S(2)}, u32[]{:S(2)}) collective-permute-start(f32[160,256]{1,0:T(8,128)S(1)} %constant_dynamic-slice_fusion.2), channel_id=1, source_target_pairs={{0,8},{4,12},{8,0},{12,4},{16,24},{20,28},{24,16},{28,20},{1,9},{5... | collective-permute-start | bytes 491528 | tf_op jit(solution)/shard_map/ppermute | solution.py:25
  52.0 12.2 %collective-permute-start.6 = (f32[81,1280]{1,0:T(8,128)S(1)}, f32[81,1280]{1,0:T(8,128)S(1)}, u32[]{:S(2)}, u32[]{:S(2)}) collective-permute-start(f32[81,1280]{1,0:T(8,128)S(1)} %pad_maximum_fusion.5), channel_id=1, source_target_pairs={{0,2},{1,3},{2,0},{3,1},{4,6},{5,7},{6,4},{7,5},{8,10},{9,11},{10,... | collective-permute-start | bytes 1244168 | tf_op jit(solution)/shard_map/ppermute | solution.py:25
  55.9 10.0 %collective-permute-start.18 = (f32[80,256]{1,0:T(8,128)S(1)}, f32[80,256]{1,0:T(8,128)S(1)}, u32[]{:S(2)}, u32[]{:S(2)}) collective-permute-start(f32[80,256]{1,0:T(8,128)S(1)} %constant_dynamic-slice_fusion.1), channel_id=1, source_target_pairs={{0,2},{1,3},{2,0},{3,1},{4,6},{5,7},{6,4},{7,5},{8,10},{9,11},{10,... | collective-permute-start | bytes 245768 | tf_op jit(solution)/shard_map/ppermute | solution.py:25
  64.4 6.3 %collective-permute-start.7 = (f32[41,1280]{1,0:T(8,128)S(1)}, f32[41,1280]{1,0:T(8,128)S(1)}, u32[]{:S(2)}, u32[]{:S(2)}) collective-permute-start(f32[41,1280]{1,0:T(8,128)S(1)} %pad_maximum_fusion.6), channel_id=1, source_target_pairs={{0,4},{4,0},{8,12},{12,8},{16,20},{20,16},{24,28},{28,24},{1,5},{5... | collective-permute-start | bytes 629768 | tf_op jit(solution)/shard_map/ppermute | solution.py:25
  70.8 6.2 %collective-permute-start.8 = (f32[42,640]{1,0:T(8,128)S(1)}, f32[42,640]{1,0:T(8,128)S(1)}, u32[]{:S(2)}, u32[]{:S(2)}) collective-permute-start(f32[42,640]{1,0:T(8,128)S(1)} %pad_maximum_fusion.7), channel_id=1, source_target_pairs={{0,8},{4,12},{8,0},{12,4},{16,24},{20,28},{24,16},{28,20},{1,9},{5... | collective-permute-start | bytes 322568 | tf_op jit(solution)/shard_map/ppermute | solution.py:25
  71.4 7.8 %collective-permute-start.19 = (f32[40,256]{1,0:T(8,128)S(1)}, f32[40,256]{1,0:T(8,128)S(1)}, u32[]{:S(2)}, u32[]{:S(2)}) collective-permute-start(f32[40,256]{1,0:T(8,128)S(1)} %constant_dynamic-slice_fusion), channel_id=1, source_target_pairs={{0,16},{4,20},{8,24},{12,28},{16,0},{20,4},{24,8},{28,12},{1,17},{... | collective-permute-start | bytes 122888 | tf_op jit(solution)/shard_map/ppermute | solution.py:25
  77.2 5.4 %collective-permute-start.9 = (f32[44,320]{1,0:T(8,128)S(1)}, f32[44,320]{1,0:T(8,128)S(1)}, u32[]{:S(2)}, u32[]{:S(2)}) collective-permute-start(f32[44,320]{1,0:T(8,128)S(1)} %pad_maximum_fusion.8), channel_id=1, source_target_pairs={{0,16},{4,20},{8,24},{12,28},{16,0},{20,4},{24,8},{28,12},{1,17},{... | collective-permute-start | bytes 168968 | tf_op jit(solution)/shard_map/ppermute | solution.py:25
  79.2 5.5 %collective-permute-start.20 = (f32[40,256]{1,0:T(8,128)S(1)}, f32[40,256]{1,0:T(8,128)S(1)}, u32[]{:S(2)}, u32[]{:S(2)}) collective-permute-start(f32[40,256]{1,0:T(8,128)S(1)} %dynamic-slice_add_fusion.4), channel_id=1, source_target_pairs={{0,16},{4,20},{8,24},{12,28},{16,0},{20,4},{24,8},{28,12},{1,17},{... | collective-permute-start | bytes 122888 | tf_op jit(solution)/shard_map/ppermute | solution.py:25
  82.7 5.5 %collective-permute-start.10 = (f32[40,320]{1,0:T(8,128)S(1)}, f32[40,320]{1,0:T(8,128)S(1)}, u32[]{:S(2)}, u32[]{:S(2)}) collective-permute-start(f32[40,320]{1,0:T(8,128)S(1)} %slice_add_fusion.4), channel_id=1, source_target_pairs={{0,16},{4,20},{8,24},{12,28},{16,0},{20,4},{24,8},{28,12},{1,17},{... | collective-permute-start | bytes 153608 | tf_op jit(solution)/shard_map/ppermute | solution.py:25
  84.7 4.5 %collective-permute-start.21 = (f32[80,256]{1,0:T(8,128)S(1)}, f32[80,256]{1,0:T(8,128)S(1)}, u32[]{:S(2)}, u32[]{:S(2)}) collective-permute-start(f32[80,256]{1,0:T(8,128)S(1)} %maximum_select_fusion.16), channel_id=1, source_target_pairs={{0,2},{1,3},{2,0},{3,1},{4,6},{5,7},{6,4},{7,5},{8,10},{9,11},{10,... | collective-permute-start | bytes 245768 | tf_op jit(solution)/shard_map/ppermute | solution.py:25
  88.3 4.7 %collective-permute-start.11 = (f32[40,640]{1,0:T(8,128)S(1)}, f32[40,640]{1,0:T(8,128)S(1)}, u32[]{:S(2)}, u32[]{:S(2)}) collective-permute-start(f32[40,640]{1,0:T(8,128)S(1)} %maximum_select_fusion.13), channel_id=1, source_target_pairs={{0,8},{4,12},{8,0},{12,4},{16,24},{20,28},{24,16},{28,20},{1,9},{5... | collective-permute-start | bytes 307208 | tf_op jit(solution)/shard_map/ppermute | solution.py:25
  89.2 5.6 %collective-permute-start.22 = (f32[160,256]{1,0:T(8,128)S(1)}, f32[160,256]{1,0:T(8,128)S(1)}, u32[]{:S(2)}, u32[]{:S(2)}) collective-permute-start(f32[160,256]{1,0:T(8,128)S(1)} %maximum_select_fusion.12), channel_id=1, source_target_pairs={{0,8},{4,12},{8,0},{12,4},{16,24},{20,28},{24,16},{28,20},{1,9},{5... | collective-permute-start | bytes 491528 | tf_op jit(solution)/shard_map/ppermute | solution.py:25
  93.1 5.8 %collective-permute-start.12 = (f32[40,1280]{1,0:T(8,128)S(1)}, f32[40,1280]{1,0:T(8,128)S(1)}, u32[]{:S(2)}, u32[]{:S(2)}) collective-permute-start(f32[40,1280]{1,0:T(8,128)S(1)} %maximum_select_fusion.9), channel_id=1, source_target_pairs={{0,4},{4,0},{8,12},{12,8},{16,20},{20,16},{24,28},{28,24},{1,5},{5... | collective-permute-start | bytes 614408 | tf_op jit(solution)/shard_map/ppermute | solution.py:25
  94.8 7.6 %collective-permute-start.23 = (f32[320,256]{1,0:T(8,128)S(1)}, f32[320,256]{1,0:T(8,128)S(1)}, u32[]{:S(2)}, u32[]{:S(2)}) collective-permute-start(f32[320,256]{1,0:T(8,128)S(1)} %maximum_select_fusion.8), channel_id=1, source_target_pairs={{0,4},{4,0},{8,12},{12,8},{16,20},{20,16},{24,28},{28,24},{1,5},{5... | collective-permute-start | bytes 983048 | tf_op jit(solution)/shard_map/ppermute | solution.py:25
  98.9 8.0 %collective-permute-start.13 = (f32[80,1280]{1,0:T(8,128)S(1)}, f32[80,1280]{1,0:T(8,128)S(1)}, u32[]{:S(2)}, u32[]{:S(2)}) collective-permute-start(f32[80,1280]{1,0:T(8,128)S(1)} %maximum_select_fusion.4), channel_id=1, source_target_pairs={{0,2},{1,3},{2,0},{3,1},{4,6},{5,7},{6,4},{7,5},{8,10},{9,11},{10,... | collective-permute-start | bytes 1228808 | tf_op jit(solution)/shard_map/ppermute | solution.py:25
  102.4 6.0 %collective-permute-start.24 = (f32[640,256]{1,0:T(8,128)S(1)}, f32[640,256]{1,0:T(8,128)}, u32[]{:S(2)}, u32[]{:S(2)}) collective-permute-start(f32[640,256]{1,0:T(8,128)S(1)} %maximum_select_fusion.3), channel_id=1, source_target_pairs={{0,1},{1,0},{2,3},{3,2},{4,5},{5,4},{6,7},{7,6},{8,9},{9,8},{10,11... | collective-permute-start | bytes 1966088 | tf_op jit(solution)/shard_map/ppermute | solution.py:25
  107.0 4.0 %collective-permute-start.14 = (f32[160,1280]{1,0:T(8,128)S(1)}, f32[160,1280]{1,0:T(8,128)S(1)}, u32[]{:S(2)}, u32[]{:S(2)}) collective-permute-start(f32[160,1280]{1,0:T(8,128)S(1)} %maximum_select_fusion.2), channel_id=1, source_target_pairs={{0,1},{1,0},{2,3},{3,2},{4,5},{5,4},{6,7},{7,6},{8,9},{9,8},{10,11... | collective-permute-start | bytes 2457608 | tf_op jit(solution)/shard_map/ppermute | solution.py:25

commit v8 on v7

--- a/solution.py
+++ b/solution.py
@@ -119,7 +119,7 @@
     out_ref[...] = jnp.mean(act.reshape(images, POS, channels), axis=1).astype(out_ref.dtype)
 
 
-def pooled_of(feature_map, head_weight, head_shift, block_rows=128):
+def pooled_of(feature_map, head_weight, head_shift, block_rows=640):
     rows, c_in = feature_map.shape
     channels = head_weight.shape[1]
     block_rows = block_rows if rows % block_rows == 0 else rows

time: 114 us -> 112 us (0.982)
  Pallas kernels: 5.06 us -> 3.47 us
    pallas_call x1, Pallas kernels: 5.06 us -> 3.47 us  [pooled_of(): pl.pallas_call(pooled_kernel, out_shape=jax.ShapeDtypeStruct((rows // POS...]
where the time goes in v8:
time: 112 us
  waiting for transfers between devices  48.8 us (44%)
  starting transfers between devices  34.5 us (31%)
  other arithmetic  10.3 us (9%)
  matrix products  9.28 us (8%)
  between operations  3.59 us (3%)
  Pallas kernels  3.47 us (3%)
  local copies, waits for them, and re-layouts  2 us (2%)
    ppermute x25, waiting for transfers between devices, swap(): return lax.ppermute(x, ax, [(i, i ^ mask) for i in range(mesh.shape[ax])])  48.8 us
    ppermute x25, starting transfers between devices, swap(): return lax.ppermute(x, ax, [(i, i ^ mask) for i in range(mesh.shape[ax])])  34.5 us
    select_n x10, other arithmetic, all_reduce(): jnp.where(my_bit(ax, mask), jnp.concatenate([g, c], axis=d), jnp.concaten...  4.13 us
    pallas_call x1, Pallas kernels, pooled_of(): pl.pallas_call(pooled_kernel, out_shape=jax.ShapeDtypeStruct((rows // POS...  3.47 us
    dot_general x1, matrix products, body(): jnp.dot(feature_map, head_weight, preferred_element_type=jnp.float32)  3.31 us
    dot_general x1, matrix products, pair_terms(): lax.dot_general(rows_z, piece, (((1,), (1,)), ((), ())), preferred_elemen...  2.5 us
    reduce_sum x1, other arithmetic, body(): grad_shift = jnp.sum(grad_pre.astype(jnp.float32), axis=0)  2.35 us
  transfers between devices with their start and end apart: 25, of which 19 were waited for; matrix products, arithmetic and copies ran while one was open for 9% of the time, Pallas kernels for 0%

profile of v8, /device:TPU:0, one launch (start us, length us, event | category | flops | bytes accessed | tf_op | source)
XLA Modules:
  0.0 111.9 jit_solution(2942171398116088334)
XLA Ops:
  0.7 3.5 %shard_map.75 = bf16[40,1280]{1,0:T(8,128)(2,1)} custom-call(bf16[320,640]{1,0:T(8,128)(2,1)} %bitcast.82, bf16[320,1280]{1,0:T(8,128)(2,1)} %w_ref.1, f32[1280]{0:T(1024)} %shift_ref.1), custom_call_target="tpu_custom_call" | custom-call | flops 524288000 | bytes 1336320 | tf_op jit(solution)/shard_map/pallas_call | solution.py:126
  5.5 4.1 %collective-permute-start = (bf16[1,40,256]{2,1,0:T(8,128)(2,1)S(1)}, bf16[1,40,256]{2,1,0:T(8,128)(2,1)S(1)}, u32[]{:S(2)}, u32[]{:S(2)}) collective-permute-start(bf16[1,40,256]{2,1,0:T(8,128)(2,1)S(1)} %fusion.48), channel_id=1, source_target_pairs={{0,16},{4,20},{8,24},{12,28},{16,0},{20,4},{24,8},{28,12},{1,17},{... | collective-permute-start | bytes 61448 | tf_op jit(solution)/shard_map/ppermute | solution.py:25
  9.8 1.6 %collective-permute-done = bf16[1,40,256]{2,1,0:T(8,128)(2,1)S(1)} collective-permute-done((bf16[1,40,256]{2,1,0:T(8,128)(2,1)S(1)}, bf16[1,40,256]{2,1,0:T(8,128)(2,1)S(1)}, u32[]{:S(2)}, u32[]{:S(2)}) %collective-permute-start) | collective-permute-done | bytes 20512 | tf_op jit(solution)/shard_map/ppermute | solution.py:25
  11.4 2.0 %collective-permute-start.1 = (bf16[2,1,40,256]{3,2,0,1:T(8,128)(2,1)S(1)}, bf16[2,1,40,256]{3,2,0,1:T(8,128)(2,1)S(1)}, u32[]{:S(2)}, u32[]{:S(2)}) collective-permute-start(bf16[2,1,40,256]{3,2,0,1:T(8,128)(2,1)S(1)} %maximum_select_fusion.17), channel_id=1, source_target_pairs={{0,8},{4,12},{8,0},{12,4},{16,24},{20,28},{24,16},{28,20},{1,9},{5... | collective-permute-start | bytes 122888 | tf_op jit(solution)/shard_map/ppermute | solution.py:25
  13.4 2.1 %collective-permute-done.1 = bf16[2,1,40,256]{3,2,0,1:T(8,128)(2,1)S(1)} collective-permute-done((bf16[2,1,40,256]{3,2,0,1:T(8,128)(2,1)S(1)}, bf16[2,1,40,256]{3,2,0,1:T(8,128)(2,1)S(1)}, u32[]{:S(2)}, u32[]{:S(2)}) %collective-permute-start.1) | collective-permute-done | bytes 40992 | tf_op jit(solution)/shard_map/ppermute | solution.py:25
  15.5 2.0 %collective-permute-start.2 = (bf16[2,2,1,40,256]{4,3,1,0,2:T(8,128)(2,1)S(1)}, bf16[2,2,1,40,256]{4,3,1,0,2:T(8,128)(2,1)S(1)}, u32[]{:S(2)}, u32[]{:S(2)}) collective-permute-start(bf16[2,2,1,40,256]{4,3,1,0,2:T(8,128)(2,1)S(1)} %maximum_select_fusion.14), channel_id=1, source_target_pairs={{0,4},{4,0},{8,12},{12,8},{16,20},{20,16},{24,28},{28,24},{1,5},{5... | collective-permute-start | bytes 245768 | tf_op jit(solution)/shard_map/ppermute | solution.py:25
  17.5 2.5 %collective-permute-done.2 = bf16[2,2,1,40,256]{4,3,1,0,2:T(8,128)(2,1)S(1)} collective-permute-done((bf16[2,2,1,40,256]{4,3,1,0,2:T(8,128)(2,1)S(1)}, bf16[2,2,1,40,256]{4,3,1,0,2:T(8,128)(2,1)S(1)}, u32[]{:S(2)}, u32[]{:S(2)}) %collective-permute-start.2) | collective-permute-done | bytes 81952 | tf_op jit(solution)/shard_map/ppermute | solution.py:25
  20.0 2.0 %collective-permute-start.3 = (bf16[2,2,2,1,40,256]{5,4,2,1,0,3:T(8,128)(2,1)S(1)}, bf16[2,2,2,1,40,256]{5,4,2,1,0,3:T(8,128)(2,1)S(1)}, u32[]{:S(2)}, u32[]{:S(2)}) collective-permute-start(bf16[2,2,2,1,40,256]{5,4,2,1,0,3:T(8,128)(2,1)S(1)} %maximum_select_fusion.10), channel_id=1, source_target_pairs={{0,2},{1,3},{2,0},{3,1},{4,6},{5,7},{6,4},{7,5},{8,10},{9,11},{10,... | collective-permute-start | bytes 491528 | tf_op jit(solution)/shard_map/ppermute | solution.py:25
  22.0 3.3 %add_multiply_fusion = f32[640,1280]{1,0:T(8,128)} fusion(bf16[640,320]{0,1:T(8,128)(2,1)S(1)} %copy-done.5, bf16[320,1280]{1,0:T(8,128)(2,1)S(1)} %copy-done.4, f32[1280]{0:T(1024)S(1)} %copy-done.6), kind=kOutput, calls=%fused_computation.9 | convolution fusion | flops 530841600 | bytes 4510720 | tf_op jit(solution)/shard_map/dot_general | solution.py:151
  27.3 2.5 %fusion.8 = f32[]{:T(128)} fusion(bf16[1280,256]{1,0:T(8,128)(2,1)S(1)} %bitcast.73), kind=kOutput, calls=%fused_computation.17 | convolution fusion | flops 847052800 | bytes 655364 | tf_op jit(solution)/shard_map/dot_general | solution.py:105
  32.0 2.4 %convert_reduce_fusion = (f32[1280]{0:T(1024)S(1)}, bf16[640,1280]{1,0:T(8,128)(2,1)S(1)}) fusion(f32[640,1280]{1,0:T(8,128)} %add_multiply_fusion, f32[40,1280]{1,0:T(8,128)S(1)} %convolution_multiply_fusion), kind=kLoop, calls=%fused_computation.8 | loop fusion | flops 3275520 | bytes 5125120 | tf_op jit(solution)/shard_map/reduce_sum | solution.py:189
  36.8 1.6 %collective-permute-done.15 = f32[640,256]{1,0:T(8,128)S(1)} collective-permute-done((f32[640,256]{1,0:T(8,128)}, f32[640,256]{1,0:T(8,128)S(1)}, u32[]{:S(2)}, u32[]{:S(2)}) %collective-permute-start.15) | collective-permute-done | bytes 655392 | tf_op jit(solution)/shard_map/ppermute | solution.py:25
  38.5 2.0 %collective-permute-start.16 = (f32[320,256]{1,0:T(8,128)S(1)}, f32[320,256]{1,0:T(8,128)S(1)}, u32[]{:S(2)}, u32[]{:S(2)}) collective-permute-start(f32[320,256]{1,0:T(8,128)S(1)} %constant_dynamic-slice_fusion.3), channel_id=1, source_target_pairs={{0,4},{4,0},{8,12},{12,8},{16,20},{20,16},{24,28},{28,24},{1,5},{5... | collective-permute-start | bytes 983048 | tf_op jit(solution)/shard_map/ppermute | solution.py:25
  42.6 5.9 %collective-permute-done.16 = f32[320,256]{1,0:T(8,128)S(1)} collective-permute-done((f32[320,256]{1,0:T(8,128)S(1)}, f32[320,256]{1,0:T(8,128)S(1)}, u32[]{:S(2)}, u32[]{:S(2)}) %collective-permute-start.16) | collective-permute-done | bytes 327712 | tf_op jit(solution)/shard_map/ppermute | solution.py:25
  48.6 1.8 %collective-permute-start.17 = (f32[160,256]{1,0:T(8,128)S(1)}, f32[160,256]{1,0:T(8,128)S(1)}, u32[]{:S(2)}, u32[]{:S(2)}) collective-permute-start(f32[160,256]{1,0:T(8,128)S(1)} %constant_dynamic-slice_fusion.2), channel_id=1, source_target_pairs={{0,8},{4,12},{8,0},{12,4},{16,24},{20,28},{24,16},{28,20},{1,9},{5... | collective-permute-start | bytes 491528 | tf_op jit(solution)/shard_map/ppermute | solution.py:25
  50.4 1.6 %collective-permute-start.6 = (f32[81,1280]{1,0:T(8,128)S(1)}, f32[81,1280]{1,0:T(8,128)S(1)}, u32[]{:S(2)}, u32[]{:S(2)}) collective-permute-start(f32[81,1280]{1,0:T(8,128)S(1)} %pad_maximum_fusion.5), channel_id=1, source_target_pairs={{0,2},{1,3},{2,0},{3,1},{4,6},{5,7},{6,4},{7,5},{8,10},{9,11},{10,... | collective-permute-start | bytes 1244168 | tf_op jit(solution)/shard_map/ppermute | solution.py:25
  52.2 2.1 %collective-permute-done.17 = f32[160,256]{1,0:T(8,128)S(1)} collective-permute-done((f32[160,256]{1,0:T(8,128)S(1)}, f32[160,256]{1,0:T(8,128)S(1)}, u32[]{:S(2)}, u32[]{:S(2)}) %collective-permute-start.17) | collective-permute-done | bytes 163872 | tf_op jit(solution)/shard_map/ppermute | solution.py:25
  54.3 1.6 %collective-permute-start.18 = (f32[80,256]{1,0:T(8,128)S(1)}, f32[80,256]{1,0:T(8,128)S(1)}, u32[]{:S(2)}, u32[]{:S(2)}) collective-permute-start(f32[80,256]{1,0:T(8,128)S(1)} %constant_dynamic-slice_fusion.1), channel_id=1, source_target_pairs={{0,2},{1,3},{2,0},{3,1},{4,6},{5,7},{6,4},{7,5},{8,10},{9,11},{10,... | collective-permute-start | bytes 245768 | tf_op jit(solution)/shard_map/ppermute | solution.py:25
  55.9 6.7 %collective-permute-done.6 = f32[81,1280]{1,0:T(8,128)S(1)} collective-permute-done((f32[81,1280]{1,0:T(8,128)S(1)}, f32[81,1280]{1,0:T(8,128)S(1)}, u32[]{:S(2)}, u32[]{:S(2)}) %collective-permute-start.6) | collective-permute-done | bytes 414752 | tf_op jit(solution)/shard_map/ppermute | solution.py:25
  62.8 1.6 %collective-permute-start.7 = (f32[41,1280]{1,0:T(8,128)S(1)}, f32[41,1280]{1,0:T(8,128)S(1)}, u32[]{:S(2)}, u32[]{:S(2)}) collective-permute-start(f32[41,1280]{1,0:T(8,128)S(1)} %pad_maximum_fusion.6), channel_id=1, source_target_pairs={{0,4},{4,0},{8,12},{12,8},{16,20},{20,16},{24,28},{28,24},{1,5},{5... | collective-permute-start | bytes 629768 | tf_op jit(solution)/shard_map/ppermute | solution.py:25
  64.4 4.6 %collective-permute-done.7 = f32[41,1280]{1,0:T(8,128)S(1)} collective-permute-done((f32[41,1280]{1,0:T(8,128)S(1)}, f32[41,1280]{1,0:T(8,128)S(1)}, u32[]{:S(2)}, u32[]{:S(2)}) %collective-permute-start.7) | collective-permute-done | bytes 209952 | tf_op jit(solution)/shard_map/ppermute | solution.py:25
  69.8 2.5 %collective-permute-start.19 = (f32[40,256]{1,0:T(8,128)S(1)}, f32[40,256]{1,0:T(8,128)S(1)}, u32[]{:S(2)}, u32[]{:S(2)}) collective-permute-start(f32[40,256]{1,0:T(8,128)S(1)} %constant_dynamic-slice_fusion), channel_id=1, source_target_pairs={{0,16},{4,20},{8,24},{12,28},{16,0},{20,4},{24,8},{28,12},{1,17},{... | collective-permute-start | bytes 122888 | tf_op jit(solution)/shard_map/ppermute | solution.py:25
  72.4 2.9 %collective-permute-done.8 = f32[42,640]{1,0:T(8,128)S(1)} collective-permute-done((f32[42,640]{1,0:T(8,128)S(1)}, f32[42,640]{1,0:T(8,128)S(1)}, u32[]{:S(2)}, u32[]{:S(2)}) %collective-permute-start.8) | collective-permute-done | bytes 107552 | tf_op jit(solution)/shard_map/ppermute | solution.py:25
  75.6 2.0 %collective-permute-start.9 = (f32[44,320]{1,0:T(8,128)S(1)}, f32[44,320]{1,0:T(8,128)S(1)}, u32[]{:S(2)}, u32[]{:S(2)}) collective-permute-start(f32[44,320]{1,0:T(8,128)S(1)} %pad_maximum_fusion.8), channel_id=1, source_target_pairs={{0,16},{4,20},{8,24},{12,28},{16,0},{20,4},{24,8},{28,12},{1,17},{... | collective-permute-start | bytes 168968 | tf_op jit(solution)/shard_map/ppermute | solution.py:25
  78.7 2.3 %collective-permute-done.9 = f32[44,320]{1,0:T(8,128)S(1)} collective-permute-done((f32[44,320]{1,0:T(8,128)S(1)}, f32[44,320]{1,0:T(8,128)S(1)}, u32[]{:S(2)}, u32[]{:S(2)}) %collective-permute-start.9) | collective-permute-done | bytes 56352 | tf_op jit(solution)/shard_map/ppermute | solution.py:25
  81.1 2.0 %collective-permute-start.10 = (f32[40,320]{1,0:T(8,128)S(1)}, f32[40,320]{1,0:T(8,128)S(1)}, u32[]{:S(2)}, u32[]{:S(2)}) collective-permute-start(f32[40,320]{1,0:T(8,128)S(1)} %slice_add_fusion.4), channel_id=1, source_target_pairs={{0,16},{4,20},{8,24},{12,28},{16,0},{20,4},{24,8},{28,12},{1,17},{... | collective-permute-start | bytes 153608 | tf_op jit(solution)/shard_map/ppermute | solution.py:25
  84.6 2.0 %collective-permute-done.10 = f32[40,320]{1,0:T(8,128)S(1)} collective-permute-done((f32[40,320]{1,0:T(8,128)S(1)}, f32[40,320]{1,0:T(8,128)S(1)}, u32[]{:S(2)}, u32[]{:S(2)}) %collective-permute-start.10) | collective-permute-done | bytes 51232 | tf_op jit(solution)/shard_map/ppermute | solution.py:25
  88.9 2.5 %collective-permute-done.11 = f32[40,640]{1,0:T(8,128)S(1)} collective-permute-done((f32[40,640]{1,0:T(8,128)S(1)}, f32[40,640]{1,0:T(8,128)S(1)}, u32[]{:S(2)}, u32[]{:S(2)}) %collective-permute-start.11) | collective-permute-done | bytes 102432 | tf_op jit(solution)/shard_map/ppermute | solution.py:25
  94.6 2.7 %collective-permute-done.12 = f32[40,1280]{1,0:T(8,128)S(1)} collective-permute-done((f32[40,1280]{1,0:T(8,128)S(1)}, f32[40,1280]{1,0:T(8,128)S(1)}, u32[]{:S(2)}, u32[]{:S(2)}) %collective-permute-start.12) | collective-permute-done | bytes 204832 | tf_op jit(solution)/shard_map/ppermute | solution.py:25
  98.7 2.1 %collective-permute-done.23 = f32[320,256]{1,0:T(8,128)S(1)} collective-permute-done((f32[320,256]{1,0:T(8,128)S(1)}, f32[320,256]{1,0:T(8,128)S(1)}, u32[]{:S(2)}, u32[]{:S(2)}) %collective-permute-start.23) | collective-permute-done | bytes 327712 | tf_op jit(solution)/shard_map/ppermute | solution.py:25
  100.9 4.4 %collective-permute-done.13 = f32[80,1280]{1,0:T(8,128)S(1)} collective-permute-done((f32[80,1280]{1,0:T(8,128)S(1)}, f32[80,1280]{1,0:T(8,128)S(1)}, u32[]{:S(2)}, u32[]{:S(2)}) %collective-permute-start.13) | collective-permute-done | bytes 409632 | tf_op jit(solution)/shard_map/ppermute | solution.py:25
  106.9 2.5 %maximum_select_fusion.1 = f32[1280,256]{1,0:T(8,128)} fusion(f32[640,256]{1,0:T(8,128)S(1)} %maximum_select_fusion.3, f32[640,256]{1,0:T(8,128)} %collective-permute-done.24, pred[]{:T(512)S(6)} %ne.10), kind=kLoop, calls=%fused_computation.18 | loop fusion | flops 983040 | bytes 2621441 | tf_op jit(solution)/shard_map/jit(_where)/select_n | solution.py:93
  (111 shorter events, 23.0 us)
Async XLA Ops:
  0.6 3.5 %copy-start = (bf16[1280,256]{1,0:T(8,128)(2,1)S(1)}, bf16[1280,256]{1,0:T(8,128)(2,1)}, u32[]{:S(2)}) copy-start(bf16[1280,256]{1,0:T(8,128)(2,1)} %param.7) | copy-start | bytes 1966084
  0.6 21.4 %copy-start.4 = (bf16[320,1280]{1,0:T(8,128)(2,1)S(1)}, bf16[320,1280]{1,0:T(8,128)(2,1)}, u32[]{:S(2)}) copy-start(bf16[320,1280]{1,0:T(8,128)(2,1)} %w_ref.1) | copy-start | bytes 2457604
  0.7 21.4 %copy-start.5 = (bf16[640,320]{0,1:T(8,128)(2,1)S(1)}, bf16[640,320]{0,1:T(8,128)(2,1)}, u32[]{:S(2)}) copy-start(bf16[640,320]{0,1:T(8,128)(2,1)} %param.4) | copy-start | bytes 1228804
  0.7 21.3 %copy-start.6 = (f32[1280]{0:T(1024)S(1)}, f32[1280]{0:T(1024)}, u32[]{:S(2)}) copy-start(f32[1280]{0:T(1024)} %shift_ref.1) | copy-start | bytes 15364
  5.5 5.9 %collective-permute-start = (bf16[1,40,256]{2,1,0:T(8,128)(2,1)S(1)}, bf16[1,40,256]{2,1,0:T(8,128)(2,1)S(1)}, u32[]{:S(2)}, u32[]{:S(2)}) collective-permute-start(bf16[1,40,256]{2,1,0:T(8,128)(2,1)S(1)} %fusion.48), channel_id=1, source_target_pairs={{0,16},{4,20},{8,24},{12,28},{16,0},{20,4},{24,8},{28,12},{1,17},{... | collective-permute-start | bytes 61448 | tf_op jit(solution)/shard_map/ppermute | solution.py:25
  11.4 4.1 %collective-permute-start.1 = (bf16[2,1,40,256]{3,2,0,1:T(8,128)(2,1)S(1)}, bf16[2,1,40,256]{3,2,0,1:T(8,128)(2,1)S(1)}, u32[]{:S(2)}, u32[]{:S(2)}) collective-permute-start(bf16[2,1,40,256]{3,2,0,1:T(8,128)(2,1)S(1)} %maximum_select_fusion.17), channel_id=1, source_target_pairs={{0,8},{4,12},{8,0},{12,4},{16,24},{20,28},{24,16},{28,20},{1,9},{5... | collective-permute-start | bytes 122888 | tf_op jit(solution)/shard_map/ppermute | solution.py:25
  15.5 4.5 %collective-permute-start.2 = (bf16[2,2,1,40,256]{4,3,1,0,2:T(8,128)(2,1)S(1)}, bf16[2,2,1,40,256]{4,3,1,0,2:T(8,128)(2,1)S(1)}, u32[]{:S(2)}, u32[]{:S(2)}) collective-permute-start(bf16[2,2,1,40,256]{4,3,1,0,2:T(8,128)(2,1)S(1)} %maximum_select_fusion.14), channel_id=1, source_target_pairs={{0,4},{4,0},{8,12},{12,8},{16,20},{20,16},{24,28},{28,24},{1,5},{5... | collective-permute-start | bytes 245768 | tf_op jit(solution)/shard_map/ppermute | solution.py:25
  20.0 5.4 %collective-permute-start.3 = (bf16[2,2,2,1,40,256]{5,4,2,1,0,3:T(8,128)(2,1)S(1)}, bf16[2,2,2,1,40,256]{5,4,2,1,0,3:T(8,128)(2,1)S(1)}, u32[]{:S(2)}, u32[]{:S(2)}) collective-permute-start(bf16[2,2,2,1,40,256]{5,4,2,1,0,3:T(8,128)(2,1)S(1)} %maximum_select_fusion.10), channel_id=1, source_target_pairs={{0,2},{1,3},{2,0},{3,1},{4,6},{5,7},{6,4},{7,5},{8,10},{9,11},{10,... | collective-permute-start | bytes 491528 | tf_op jit(solution)/shard_map/ppermute | solution.py:25
  25.5 1.7 %collective-permute-start.4 = (bf16[2,2,2,2,1,40,256]{6,5,3,2,1,4,0:T(8,128)(2,1)S(1)}, bf16[2,2,2,2,1,40,256]{6,5,3,2,1,4,0:T(8,128)(2,1)S(1)}, u32[]{:S(2)}, u32[]{:S(2)}) collective-permute-start(bf16[2,2,2,2,1,40,256]{6,5,3,2,1,4,0:T(8,128)(2,1)S(1)} %maximum_select_fusion.5), channel_id=1, source_target_pairs={{0,1},{1,0},{2,3},{3,2},{4,5},{5,4},{6,7},{7,6},{8,9},{9,8},{10,11... | collective-permute-start | bytes 983048 | tf_op jit(solution)/shard_map/ppermute | solution.py:25
  29.8 1.8 %copy-start.3 = (bf16[40,1280]{1,0:T(8,128)(2,1)S(1)}, bf16[40,1280]{1,0:T(8,128)(2,1)}, u32[]{:S(2)}) copy-start(bf16[40,1280]{1,0:T(8,128)(2,1)} %shard_map.75) | copy-start | bytes 307204
  35.1 1.4 %copy-start.1 = (f32[1280,320]{0,1:T(8,128)}, f32[1280,320]{0,1:T(8,128)S(1)}, u32[]{:S(2)}) copy-start(f32[1280,320]{0,1:T(8,128)S(1)} %fusion.32) | copy-start | bytes 4915204
  36.1 2.3 %collective-permute-start.15 = (f32[640,256]{1,0:T(8,128)}, f32[640,256]{1,0:T(8,128)S(1)}, u32[]{:S(2)}, u32[]{:S(2)}) collective-permute-start(f32[640,256]{1,0:T(8,128)} %constant_dynamic-slice_fusion.4), channel_id=1, source_target_pairs={{0,1},{1,0},{2,3},{3,2},{4,5},{5,4},{6,7},{7,6},{8,9},{9,8},{10,11... | collective-permute-start | bytes 1966088 | tf_op jit(solution)/shard_map/ppermute | solution.py:25
  36.5 4.0 %collective-permute-start.5 = (f32[161,1280]{1,0:T(8,128)S(1)}, f32[161,1280]{1,0:T(8,128)}, u32[]{:S(2)}, u32[]{:S(2)}) collective-permute-start(f32[161,1280]{1,0:T(8,128)S(1)} %pad_maximum_fusion), channel_id=1, source_target_pairs={{0,1},{1,0},{2,3},{3,2},{4,5},{5,4},{6,7},{7,6},{8,9},{9,8},{10,11... | collective-permute-start | bytes 2472968 | tf_op jit(solution)/shard_map/ppermute | solution.py:25
  36.8 3.7 %copy-start.2 = (f32[1280,320]{0,1:T(8,128)S(1)}, f32[1280,320]{0,1:T(8,128)}, u32[]{:S(2)}) copy-start(f32[1280,320]{0,1:T(8,128)} %copy-done.1) | copy-start | bytes 4915204
  38.5 10.0 %collective-permute-start.16 = (f32[320,256]{1,0:T(8,128)S(1)}, f32[320,256]{1,0:T(8,128)S(1)}, u32[]{:S(2)}, u32[]{:S(2)}) collective-permute-start(f32[320,256]{1,0:T(8,128)S(1)} %constant_dynamic-slice_fusion.3), channel_id=1, source_target_pairs={{0,4},{4,0},{8,12},{12,8},{16,20},{20,16},{24,28},{28,24},{1,5},{5... | collective-permute-start | bytes 983048 | tf_op jit(solution)/shard_map/ppermute | solution.py:25
  48.6 5.6 %collective-permute-start.17 = (f32[160,256]{1,0:T(8,128)S(1)}, f32[160,256]{1,0:T(8,128)S(1)}, u32[]{:S(2)}, u32[]{:S(2)}) collective-permute-start(f32[160,256]{1,0:T(8,128)S(1)} %constant_dynamic-slice_fusion.2), channel_id=1, source_target_pairs={{0,8},{4,12},{8,0},{12,4},{16,24},{20,28},{24,16},{28,20},{1,9},{5... | collective-permute-start | bytes 491528 | tf_op jit(solution)/shard_map/ppermute | solution.py:25
  50.4 12.2 %collective-permute-start.6 = (f32[81,1280]{1,0:T(8,128)S(1)}, f32[81,1280]{1,0:T(8,128)S(1)}, u32[]{:S(2)}, u32[]{:S(2)}) collective-permute-start(f32[81,1280]{1,0:T(8,128)S(1)} %pad_maximum_fusion.5), channel_id=1, source_target_pairs={{0,2},{1,3},{2,0},{3,1},{4,6},{5,7},{6,4},{7,5},{8,10},{9,11},{10,... | collective-permute-start | bytes 1244168 | tf_op jit(solution)/shard_map/ppermute | solution.py:25
  54.3 10.0 %collective-permute-start.18 = (f32[80,256]{1,0:T(8,128)S(1)}, f32[80,256]{1,0:T(8,128)S(1)}, u32[]{:S(2)}, u32[]{:S(2)}) collective-permute-start(f32[80,256]{1,0:T(8,128)S(1)} %constant_dynamic-slice_fusion.1), channel_id=1, source_target_pairs={{0,2},{1,3},{2,0},{3,1},{4,6},{5,7},{6,4},{7,5},{8,10},{9,11},{10,... | collective-permute-start | bytes 245768 | tf_op jit(solution)/shard_map/ppermute | solution.py:25
  62.8 6.3 %collective-permute-start.7 = (f32[41,1280]{1,0:T(8,128)S(1)}, f32[41,1280]{1,0:T(8,128)S(1)}, u32[]{:S(2)}, u32[]{:S(2)}) collective-permute-start(f32[41,1280]{1,0:T(8,128)S(1)} %pad_maximum_fusion.6), channel_id=1, source_target_pairs={{0,4},{4,0},{8,12},{12,8},{16,20},{20,16},{24,28},{28,24},{1,5},{5... | collective-permute-start | bytes 629768 | tf_op jit(solution)/shard_map/ppermute | solution.py:25
  69.2 6.2 %collective-permute-start.8 = (f32[42,640]{1,0:T(8,128)S(1)}, f32[42,640]{1,0:T(8,128)S(1)}, u32[]{:S(2)}, u32[]{:S(2)}) collective-permute-start(f32[42,640]{1,0:T(8,128)S(1)} %pad_maximum_fusion.7), channel_id=1, source_target_pairs={{0,8},{4,12},{8,0},{12,4},{16,24},{20,28},{24,16},{28,20},{1,9},{5... | collective-permute-start | bytes 322568 | tf_op jit(solution)/shard_map/ppermute | solution.py:25
  69.8 7.8 %collective-permute-start.19 = (f32[40,256]{1,0:T(8,128)S(1)}, f32[40,256]{1,0:T(8,128)S(1)}, u32[]{:S(2)}, u32[]{:S(2)}) collective-permute-start(f32[40,256]{1,0:T(8,128)S(1)} %constant_dynamic-slice_fusion), channel_id=1, source_target_pairs={{0,16},{4,20},{8,24},{12,28},{16,0},{20,4},{24,8},{28,12},{1,17},{... | collective-permute-start | bytes 122888 | tf_op jit(solution)/shard_map/ppermute | solution.py:25
  75.6 5.4 %collective-permute-start.9 = (f32[44,320]{1,0:T(8,128)S(1)}, f32[44,320]{1,0:T(8,128)S(1)}, u32[]{:S(2)}, u32[]{:S(2)}) collective-permute-start(f32[44,320]{1,0:T(8,128)S(1)} %pad_maximum_fusion.8), channel_id=1, source_target_pairs={{0,16},{4,20},{8,24},{12,28},{16,0},{20,4},{24,8},{28,12},{1,17},{... | collective-permute-start | bytes 168968 | tf_op jit(solution)/shard_map/ppermute | solution.py:25
  77.6 5.5 %collective-permute-start.20 = (f32[40,256]{1,0:T(8,128)S(1)}, f32[40,256]{1,0:T(8,128)S(1)}, u32[]{:S(2)}, u32[]{:S(2)}) collective-permute-start(f32[40,256]{1,0:T(8,128)S(1)} %dynamic-slice_add_fusion.4), channel_id=1, source_target_pairs={{0,16},{4,20},{8,24},{12,28},{16,0},{20,4},{24,8},{28,12},{1,17},{... | collective-permute-start | bytes 122888 | tf_op jit(solution)/shard_map/ppermute | solution.py:25
  81.1 5.5 %collective-permute-start.10 = (f32[40,320]{1,0:T(8,128)S(1)}, f32[40,320]{1,0:T(8,128)S(1)}, u32[]{:S(2)}, u32[]{:S(2)}) collective-permute-start(f32[40,320]{1,0:T(8,128)S(1)} %slice_add_fusion.4), channel_id=1, source_target_pairs={{0,16},{4,20},{8,24},{12,28},{16,0},{20,4},{24,8},{28,12},{1,17},{... | collective-permute-start | bytes 153608 | tf_op jit(solution)/shard_map/ppermute | solution.py:25
  83.1 4.5 %collective-permute-start.21 = (f32[80,256]{1,0:T(8,128)S(1)}, f32[80,256]{1,0:T(8,128)S(1)}, u32[]{:S(2)}, u32[]{:S(2)}) collective-permute-start(f32[80,256]{1,0:T(8,128)S(1)} %maximum_select_fusion.16), channel_id=1, source_target_pairs={{0,2},{1,3},{2,0},{3,1},{4,6},{5,7},{6,4},{7,5},{8,10},{9,11},{10,... | collective-permute-start | bytes 245768 | tf_op jit(solution)/shard_map/ppermute | solution.py:25
  86.7 4.7 %collective-permute-start.11 = (f32[40,640]{1,0:T(8,128)S(1)}, f32[40,640]{1,0:T(8,128)S(1)}, u32[]{:S(2)}, u32[]{:S(2)}) collective-permute-start(f32[40,640]{1,0:T(8,128)S(1)} %maximum_select_fusion.13), channel_id=1, source_target_pairs={{0,8},{4,12},{8,0},{12,4},{16,24},{20,28},{24,16},{28,20},{1,9},{5... | collective-permute-start | bytes 307208 | tf_op jit(solution)/shard_map/ppermute | solution.py:25
  87.6 5.6 %collective-permute-start.22 = (f32[160,256]{1,0:T(8,128)S(1)}, f32[160,256]{1,0:T(8,128)S(1)}, u32[]{:S(2)}, u32[]{:S(2)}) collective-permute-start(f32[160,256]{1,0:T(8,128)S(1)} %maximum_select_fusion.12), channel_id=1, source_target_pairs={{0,8},{4,12},{8,0},{12,4},{16,24},{20,28},{24,16},{28,20},{1,9},{5... | collective-permute-start | bytes 491528 | tf_op jit(solution)/shard_map/ppermute | solution.py:25
  91.5 5.8 %collective-permute-start.12 = (f32[40,1280]{1,0:T(8,128)S(1)}, f32[40,1280]{1,0:T(8,128)S(1)}, u32[]{:S(2)}, u32[]{:S(2)}) collective-permute-start(f32[40,1280]{1,0:T(8,128)S(1)} %maximum_select_fusion.9), channel_id=1, source_target_pairs={{0,4},{4,0},{8,12},{12,8},{16,20},{20,16},{24,28},{28,24},{1,5},{5... | collective-permute-start | bytes 614408 | tf_op jit(solution)/shard_map/ppermute | solution.py:25
  93.2 7.6 %collective-permute-start.23 = (f32[320,256]{1,0:T(8,128)S(1)}, f32[320,256]{1,0:T(8,128)S(1)}, u32[]{:S(2)}, u32[]{:S(2)}) collective-permute-start(f32[320,256]{1,0:T(8,128)S(1)} %maximum_select_fusion.8), channel_id=1, source_target_pairs={{0,4},{4,0},{8,12},{12,8},{16,20},{20,16},{24,28},{28,24},{1,5},{5... | collective-permute-start | bytes 983048 | tf_op jit(solution)/shard_map/ppermute | solution.py:25
  97.3 8.0 %collective-permute-start.13 = (f32[80,1280]{1,0:T(8,128)S(1)}, f32[80,1280]{1,0:T(8,128)S(1)}, u32[]{:S(2)}, u32[]{:S(2)}) collective-permute-start(f32[80,1280]{1,0:T(8,128)S(1)} %maximum_select_fusion.4), channel_id=1, source_target_pairs={{0,2},{1,3},{2,0},{3,1},{4,6},{5,7},{6,4},{7,5},{8,10},{9,11},{10,... | collective-permute-start | bytes 1228808 | tf_op jit(solution)/shard_map/ppermute | solution.py:25
  100.9 6.0 %collective-permute-start.24 = (f32[640,256]{1,0:T(8,128)S(1)}, f32[640,256]{1,0:T(8,128)}, u32[]{:S(2)}, u32[]{:S(2)}) collective-permute-start(f32[640,256]{1,0:T(8,128)S(1)} %maximum_select_fusion.3), channel_id=1, source_target_pairs={{0,1},{1,0},{2,3},{3,2},{4,5},{5,4},{6,7},{7,6},{8,9},{9,8},{10,11... | collective-permute-start | bytes 1966088 | tf_op jit(solution)/shard_map/ppermute | solution.py:25
  105.4 4.0 %collective-permute-start.14 = (f32[160,1280]{1,0:T(8,128)S(1)}, f32[160,1280]{1,0:T(8,128)S(1)}, u32[]{:S(2)}, u32[]{:S(2)}) collective-permute-start(f32[160,1280]{1,0:T(8,128)S(1)} %maximum_select_fusion.2), channel_id=1, source_target_pairs={{0,1},{1,0},{2,3},{3,2},{4,5},{5,4},{6,7},{7,6},{8,9},{9,8},{10,11... | collective-permute-start | bytes 2457608 | tf_op jit(solution)/shard_map/ppermute | solution.py:25
